TPU v7x, 256 devices: a whole 4x4x8 slice. The times are simulated.
256 devices in a mesh: wide: 32 (over x_lo, z, core), tm: 8 (over x_hi, y).
Axes of the slice: x: 4 (x_hi: 2, x_lo: 2; x = x_hi * 2 + x_lo), y: 4, z: 8, core: 2. Of those that a mesh axis runs over, the one named last changes fastest.
Arguments:
- voltages: int32 [256, 524288], P('wide', 'tm'), may hold values from -128 to 127
- taps: int32 [16, 1024], replicated, may hold values from -32 to 32
Outputs:
- visibility: float32 [256, 2, 512, 256], P('tm', None, 'wide')
All inputs are finite; a program needn't handle non-finite values.
Results may differ from a plain program's by a relative error of at most 0.0024.
Values may be sent and summed in bfloat16 or wider, within the bound.
No kernel may reach another device: no remote copies, remote signals or barrier semaphores. Data moves between devices by JAX's collectives and lax.ppermute only.
A program may use at most 64 MiB of HBM per device.

v0:
```python
import jax
import jax.numpy as jnp
from jax import lax
from jax.sharding import PartitionSpec as P

FIR_SCALE = 2.0 ** (-12)


def shifted(array, axis, by):
    devices = lax.axis_size(axis)
    pairs = [(i, i + by) for i in range(devices) if 0 <= i + by < devices]
    return lax.ppermute(array, axis, pairs)


def gram_rows(own_rows, own_rotated, full_rows):
    real_part = jnp.einsum("akt,bkt->akb", own_rows, full_rows, preferred_element_type=jnp.float32)
    imag_part = jnp.einsum(
        "akt,bkt->akb", own_rotated, full_rows, preferred_element_type=jnp.float32
    )
    return jnp.stack([real_part, imag_part], axis=1)


def shards(voltages, taps):
    local_inputs = voltages.shape[0]
    length = taps.shape[1]
    lags = taps.shape[0]
    spectra_dev = voltages.shape[1] // length
    channels = length // 2
    frames = voltages.astype(jnp.bfloat16).reshape(local_inputs, spectra_dev, length)
    previous = shifted(frames[:, spectra_dev - (lags - 1) :, :], "tm", 1)
    extended = jnp.concatenate([previous, frames], axis=1).astype(jnp.float32)
    taps_float = taps.astype(jnp.float32)
    filtered = jnp.zeros((local_inputs, spectra_dev, length), jnp.float32)
    for lag in range(lags):
        filtered = (
            filtered
            + taps_float[lag] * extended[:, lags - 1 - lag : lags - 1 - lag + spectra_dev, :]
        )
    filtered = filtered * FIR_SCALE
    sample_idx = jnp.arange(length, dtype=jnp.int32)
    channel_idx = jnp.arange(channels, dtype=jnp.int32)
    phase_steps = sample_idx[:, None] * channel_idx[None, :] % length
    angles = 2.0 * jnp.pi / length * phase_steps.astype(jnp.float32)
    dft_table = jnp.stack([jnp.cos(angles), -jnp.sin(angles)], axis=1) * length ** (-0.5)
    spectra = jnp.einsum(
        "asl,lrc->acrs",
        filtered,
        dft_table,
        precision=lax.Precision.HIGHEST,
        preferred_element_type=jnp.float32,
    ).astype(jnp.bfloat16)
    widen = lax.axis_size("wide")
    ranks = lax.axis_size("tm")
    norm_factor = 1.0 / (spectra_dev * ranks)
    packed = spectra.reshape(local_inputs, widen, channels // widen, 2 * spectra_dev)
    full_rows = lax.all_to_all(packed, "wide", split_axis=1, concat_axis=0, tiled=True)[:, 0]
    rotated = jnp.concatenate(
        [full_rows[..., spectra_dev:], -full_rows[..., :spectra_dev]], axis=-1
    )
    grams = gram_rows(full_rows, rotated, full_rows)
    summed = lax.psum_scatter(grams, "tm", scatter_dimension=0, tiled=True)
    return summed * norm_factor


def solution(mesh):
    placed = (P("wide", "tm"), P())
    return jax.shard_map(
        shards, mesh=mesh, in_specs=placed, out_specs=P("tm", None, "wide", None), check_vma=False
    )
```

profile of v0, /device:TPU:1, one launch (start us, length us, event | category | flops | bytes accessed | tf_op | source)
XLA Modules:
  0.0 218.4 jit_solution(1083958352350195433)
XLA Ops:
  6.5 0.0 reduce-scatter.2.cloned.1.call-start
  6.5 1.7 convert_element_type.33
  8.2 0.0 copy-start
  8.2 0.6 copy.11
  8.8 0.1 slice.141
  8.9 4.0 %collective-permute-start = (bf16[8,15,1024]{2,1,0:T(8,128)(2,1)S(1)}, bf16[8,15,1024]{2,1,0:T(8,128)(2,1)S(1)}, u32[]{:S(2)}, u32[]{:S(2)}) collective-permute-start(bf16[8,15,1024]{2,1,0:T(8,128)(2,1)S(1)} %slice.141), channel_id=1, source_target_pairs={{0,1},{1,2},{2,3},{3,4},{4,5},{5,6},{6,7},{8,9},{9,10},{10,11},{11... | collective-permute-start | bytes 737288 | tf_op jit(solution)/shard_map/ppermute | solution.py:12
  13.0 0.0 copy-done
  13.0 9.1 %sine_negate_fusion = (f32[1024,1,512]{2,0,1:T(8,128)S(1)}, f32[1024,1,512]{2,0,1:T(8,128)}) fusion(), kind=kLoop, calls=%fused_computation.48 | loop fusion | flops 7864320 | bytes 4194304 | tf_op jit(solution)/shard_map/neg | solution.py:44
  22.1 0.0 collective-permute-done
  22.1 0.4 maximum_convert_fusion
  22.5 12.3 %fusion.49 = bf16[8,512,2,64]{1,3,0,2:T(8,128)(2,1)S(1)} fusion(f32[8,79,1024]{2,1,0:T(8,128)S(1)} %maximum_convert_fusion, f32[1024,1,512]{2,0,1:T(8,128)S(1)} %get-tuple-element.23, f32[1024,1,512]{2,0,1:T(8,128)} %get-tuple-element.24, f32[1024]{0:T(1024)S(1)} %bitcast.57, f32[1024]{0:T(1024)S(1)} %bitcast.58, f32[1024]{0:T(1024)S(1)} %bitcast.59, ...), kind=kOutput, calls=%fused_computation.53 | convolution fusion | flops 6461849600 | bytes 38862848 | tf_op jit(solution)/shard_map/asl,lrc->acrs/dot_general | solution.py:45
  34.8 1.5 copy.13
  36.3 1.2 reshape.93
  37.5 0.3 copy.14
  37.8 36.8 %all_to_all.15 = bf16[8,32,16,128]{3,2,0,1:T(8,128)(2,1)S(1)} all-to-all(bf16[8,32,16,128]{3,2,0,1:T(8,128)(2,1)S(1)} %copy.14), channel_id=1, replica_groups=mesh['wide'=32,'tm'=8] {'wide'}, dimensions={1} | all-to-all | bytes 2097152 | tf_op jit(solution)/shard_map/all_to_all | solution.py:56
  74.5 0.3 copy.21
  74.8 0.7 convolution_bitcast_fusion.1
  75.5 0.4 fusion.79
  76.0 0.9 convolution_bitcast_fusion
  76.9 3.8 %pad_maximum_fusion = f32[256,2,16,256]{0,3,2,1:T(8,128)} fusion(f32[256,1,16,256]{0,3,2,1:T(8,128)S(1)} %convolution_bitcast_fusion, f32[256,1,16,256]{0,3,2,1:T(8,128)S(1)} %convolution_bitcast_fusion.1), kind=kLoop, calls=%fused_computation | loop fusion | flops 2097152 | bytes 16777216 | tf_op jit(solution)/shard_map/stack | solution.py:20
  80.7 10.3 %copy.16 = f32[256,2,16,256]{3,2,1,0:T(8,128)} copy(f32[256,2,16,256]{0,3,2,1:T(8,128)} %pad_maximum_fusion) | data formatting | bytes 16777216 | tf_op jit(solution)/shard_map/stack | solution.py:20
  91.0 0.0 reduce-scatter.2.cloned.1.call-update
  91.0 118.2 %reduce-scatter.2.cloned.1.call-done = f32[32,2,16,256]{3,2,1,0:T(8,128)} async-done(((f32[256,2,16,256]{3,2,1,0:T(8,128)}), f32[32,2,16,256]{3,2,1,0:T(8,128)}) %reduce-scatter.2.cloned.1.call-update) | async-done | bytes 1048592 | tf_op jit(solution)/shard_map/reduce_scatter | solution.py:61
  209.2 2.3 %broadcast_multiply_fusion = f32[32,2,16,256]{3,2,1,0:T(8,128)} fusion(f32[32,2,16,256]{3,2,1,0:T(8,128)} %reduce-scatter.2.cloned.1.call-done), kind=kLoop, calls=%fused_computation.78 | loop fusion | flops 262144 | bytes 2097152 | tf_op jit(solution)/shard_map/mul | solution.py:62
  (2 shorter events, 0.1 us)
Async XLA Ops:
  6.5 202.7 %reduce-scatter.2.cloned.1.call-start = ((), (), s32[]{:S(2)}) async-start(), calls=%async_computation.2 | async-start | bytes 9437184 | tf_op jit(solution)/shard_map/reduce_scatter | solution.py:61
  8.2 4.7 %copy-start = (s32[16,1024]{1,0:T(8,128)S(1)}, s32[16,1024]{1,0:T(8,128)}, u32[]{:S(2)}) copy-start(s32[16,1024]{1,0:T(8,128)} %param.3) | copy-start | bytes 196612
  8.9 13.2 %collective-permute-start = (bf16[8,15,1024]{2,1,0:T(8,128)(2,1)S(1)}, bf16[8,15,1024]{2,1,0:T(8,128)(2,1)S(1)}, u32[]{:S(2)}, u32[]{:S(2)}) collective-permute-start(bf16[8,15,1024]{2,1,0:T(8,128)(2,1)S(1)} %slice.141), channel_id=1, source_target_pairs={{0,1},{1,2},{2,3},{3,4},{4,5},{5,6},{6,7},{8,9},{9,10},{10,11},{11... | collective-permute-start | bytes 737288 | tf_op jit(solution)/shard_map/ppermute | solution.py:12
Sparse Core Ops, SparseCore 0:
  91.1 118.0 reduce-scatter.1
where the time goes:
time: 219 us; the launch traced here: 218 us
  waiting for transfers between devices  118 us (54%)
  blocking collectives  36.8 us (17%)
  other arithmetic  17.7 us (8%)
  local copies, waits for them, and re-layouts  14.2 us (6%)
  matrix products  13.9 us (6%)
  between operations  13.5 us (6%)
  starting transfers between devices  4.05 us (2%)
    reduce_scatter x1, waiting for transfers between devices, shards(): summed = lax.psum_scatter(grams, 'tm', scatter_dimension=0, tiled=True)  118 us
    all_to_all x1, blocking collectives, shards(): lax.all_to_all(packed, 'wide', split_axis=1, concat_axis=0, tiled=True)  36.8 us
    dot_general x1, matrix products, shards(): jnp.einsum('asl,lrc->acrs', filtered, dft_table, precision=lax.Precision....  12.3 us
    another operation x1, local copies, waits for them, and re-layouts, gram_rows(): return jnp.stack([real_part, imag_part], axis=1)  10.3 us
    neg x1, other arithmetic, shards(): -jnp.sin(angles)  9.1 us
  transfers between devices with their start and end apart: 2, of which 1 were waited for; matrix products, arithmetic and copies ran while one was open for 4% of the time, Pallas kernels for 0%

commit v1 on v0

v1 whole, which is shorter than its diff:
```python
import numpy as np
import jax
import jax.numpy as jnp
from jax import lax
from jax.sharding import PartitionSpec as P

FIR_SCALE = 2.0 ** (-12)


def shifted(array, axis, by):
    devices = lax.axis_size(axis)
    pairs = [(i, i + by) for i in range(devices) if 0 <= i + by < devices]
    return lax.ppermute(array, axis, pairs)


def dft_factors(length, channels, split):
    hi = np.arange(length // split)[:, None] * split * np.arange(channels)[None, :] % length
    lo = np.arange(split)[:, None] * np.arange(channels)[None, :] % length
    ang_hi = 2.0 * np.pi / length * hi
    ang_lo = 2.0 * np.pi / length * lo
    return (
        np.cos(ang_hi).astype(np.float32),
        (-np.sin(ang_hi)).astype(np.float32),
        np.cos(ang_lo).astype(np.float32),
        (-np.sin(ang_lo)).astype(np.float32),
    )


def dft_table(length, channels):
    split = 32
    ch, sh, cl, sl = (jnp.asarray(t) for t in dft_factors(length, channels, split))
    re = ch[:, None, :] * cl[None, :, :] - sh[:, None, :] * sl[None, :, :]
    im = ch[:, None, :] * sl[None, :, :] + sh[:, None, :] * cl[None, :, :]
    table = jnp.stack([re, im], axis=2).reshape(length, 2, channels)
    return table * length ** (-0.5)


def shards(voltages, taps):
    local_inputs = voltages.shape[0]
    length = taps.shape[1]
    lags = taps.shape[0]
    spectra_dev = voltages.shape[1] // length
    channels = length // 2
    widen = lax.axis_size("wide")
    ranks = lax.axis_size("tm")
    groups = widen * ranks
    per_group = channels // groups

    frames = voltages.reshape(local_inputs, spectra_dev, length).transpose(1, 0, 2)
    frames = frames.astype(jnp.bfloat16)
    previous = shifted(frames[spectra_dev - (lags - 1) :], "tm", 1)
    extended = jnp.concatenate([previous, frames], axis=0).astype(jnp.float32)
    taps_float = taps.astype(jnp.float32)
    filtered = taps_float[0] * extended[lags - 1 : lags - 1 + spectra_dev]
    for lag in range(1, lags):
        filtered = filtered + taps_float[lag] * extended[lags - 1 - lag : lags - 1 - lag + spectra_dev]
    filtered = filtered * FIR_SCALE

    table = dft_table(length, channels)
    spectra = jnp.einsum(
        "sin,nrk->kirs",
        filtered,
        table,
        precision=lax.Precision.HIGHEST,
        preferred_element_type=jnp.float32,
    ).astype(jnp.bfloat16)
    packed = spectra.reshape(groups, per_group, local_inputs, 2, spectra_dev)
    got = lax.all_to_all(packed, ("wide", "tm"), 0, 0, tiled=True)
    got = got.reshape(widen, ranks, per_group, local_inputs, 2, spectra_dev)
    got = got.transpose(2, 0, 3, 1, 4, 5)
    rotated = jnp.stack([got[..., 1, :], -got[..., 0, :]], axis=-2)
    inputs = widen * local_inputs
    depth = ranks * 2 * spectra_dev
    full = got.reshape(per_group, inputs, depth)
    rotated = rotated.reshape(per_group, inputs, depth)
    real_part = jnp.einsum("cak,cbk->acb", full, full, preferred_element_type=jnp.float32)
    imag_part = jnp.einsum("cak,cbk->acb", rotated, full, preferred_element_type=jnp.float32)
    norm_factor = 1.0 / (spectra_dev * ranks)
    grams = jnp.stack([real_part, imag_part], axis=1) * norm_factor
    return lax.all_to_all(grams, "tm", 0, 2, tiled=True)


def solution(mesh):
    placed = (P("wide", "tm"), P())
    return jax.shard_map(
        shards, mesh=mesh, in_specs=placed, out_specs=P("tm", None, "wide", None), check_vma=False
    )
```

time: 219 us -> 122 us (0.56)
  waiting for transfers between devices: 118 us -> 3.04 us
  blocking collectives: 36.8 us -> 68.9 us
  between operations: 13.5 us -> 0.22 us
  other arithmetic: 17.7 us -> 13.4 us
  local copies, waits for them, and re-layouts: 14.2 us -> 16.6 us
    reduce_scatter x1 -> x0, waiting for transfers between devices: 118 us -> none  [shards(): summed = lax.psum_scatter(grams, 'tm', scatter_dimension=0, tiled=True)]
    all_to_all x1 -> x2, blocking collectives: 36.8 us -> 68.9 us  [the longest x1 48.2 us: shards(): got = lax.all_to_all(packed, ('wide', 'tm'), 0, 0, tiled=True)]
    another operation x1 -> x0, local copies, waits for them, and re-layouts: 10.3 us -> none  [gram_rows(): return jnp.stack([real_part, imag_part], axis=1)]
    neg x1 -> x0, other arithmetic: 9.1 us -> none  [shards(): -jnp.sin(angles)]
    reshape x3, local copies, waits for them, and re-layouts: 2.05 us -> 7.66 us  [the longest x1 3.9 us: shards(): got = got.reshape(widen, ranks, per_group, local_inputs, 2, spectra_dev)]
    unnamed x2 -> x14, local copies, waits for them, and re-layouts: 0.01 us -> 3.51 us
    slice x1, other arithmetic: 0.42 us -> 3.86 us  [shards(): rotated = jnp.stack([got[..., 1, :], -got[..., 0, :]], axis=-2)]
    ppermute x1, waiting for transfers between devices: 0.01 us -> 3.04 us  [shifted(): return lax.ppermute(array, axis, pairs)]
  transfers between devices with their start and end apart: 2 -> 1, of which waited for: 1 -> 1; matrix products, arithmetic and copies ran while one was open for 4% -> 2% of each run, Pallas kernels for 0% -> 0%
where the time goes in v1:
time: 122 us
  blocking collectives  68.9 us (56%)
  local copies, waits for them, and re-layouts  16.6 us (14%)
  matrix products  15.3 us (13%)
  other arithmetic  13.4 us (11%)
  starting transfers between devices  4.18 us (3%)
  waiting for transfers between devices  3.04 us (2%)
    all_to_all x1, blocking collectives, shards(): got = lax.all_to_all(packed, ('wide', 'tm'), 0, 0, tiled=True)  48.2 us
    all_to_all x1, blocking collectives, shards(): return lax.all_to_all(grams, 'tm', 0, 2, tiled=True)  20.7 us
    dot_general x1, matrix products, shards(): jnp.einsum('sin,nrk->kirs', filtered, table, precision=lax.Precision.HIGH...  12.2 us
    another operation x1, other arithmetic, shards(): rotated = jnp.stack([got[..., 1, :], -got[..., 0, :]], axis=-2)  5.57 us
    ppermute x1, starting transfers between devices, shifted(): return lax.ppermute(array, axis, pairs)  4.18 us
    reshape x1, local copies, waits for them, and re-layouts, shards(): got = got.reshape(widen, ranks, per_group, local_inputs, 2, spectra_dev)  3.9 us
    slice x1, other arithmetic, shards(): rotated = jnp.stack([got[..., 1, :], -got[..., 0, :]], axis=-2)  3.86 us
    unnamed x14, local copies, waits for them, and re-layouts  3.51 us
  transfers between devices with their start and end apart: 1, of which 1 were waited for; matrix products, arithmetic and copies ran while one was open for 2% of the time, Pallas kernels for 0%

profile of v1, /device:TPU:1, one launch (start us, length us, event | category | flops | bytes accessed | tf_op | source)
XLA Modules:
  0.0 121.5 jit_solution(9818463238301153220)
XLA Ops:
  0.0 1.7 %convert_element_type.22 = bf16[8,65536]{1,0:T(8,128)(2,1)S(1)} convert(s32[8,65536]{1,0:T(8,128)} %param.6) | non-fusion elementwise | flops 524288 | bytes 3145728 | tf_op jit(solution)/shard_map/convert_element_type | solution.py:50
  1.7 0.0 copy-start.1
  1.7 0.0 copy-start.2
  1.7 0.0 copy-start.3
  1.7 0.0 copy-start.4
  1.7 0.6 copy.31
  2.3 0.1 slice.141
  2.4 0.0 copy-start.5
  2.4 4.2 %collective-permute-start = (bf16[15,8,1024]{2,0,1:T(8,128)(2,1)S(1)}, bf16[15,8,1024]{2,0,1:T(8,128)(2,1)S(1)}, u32[]{:S(2)}, u32[]{:S(2)}) collective-permute-start(bf16[15,8,1024]{2,0,1:T(8,128)(2,1)S(1)} %slice.141), channel_id=1, source_target_pairs={{0,1},{1,2},{2,3},{3,4},{4,5},{5,6},{6,7},{8,9},{9,10},{10,11},{11... | collective-permute-start | bytes 737288 | tf_op jit(solution)/shard_map/ppermute | solution.py:13
  6.6 0.0 copy-done.1
  6.6 0.0 copy-done.2
  6.6 0.0 copy-done.3
  6.6 0.0 copy-done.4
  6.6 1.8 %multiply_subtract_fusion = (f32[32,32,512]{2,1,0:T(8,128)S(1)}, f32[32,32,512]{2,1,0:T(8,128)}) fusion(f32[32,512]{1,0:T(8,128)S(1)} %copy-done.1, f32[32,512]{1,0:T(8,128)S(1)} %copy-done.3, f32[32,512]{1,0:T(8,128)S(1)} %copy-done.2, f32[32,512]{1,0:T(8,128)S(1)} %copy-done.4), kind=kLoop, calls=%fused_computation.43 | loop fusion | flops 3145728 | bytes 4456448 | tf_op jit(solution)/shard_map/sub | solution.py:32
  8.4 0.0 copy-done.5
  8.5 3.0 %collective-permute-done = bf16[15,8,1024]{2,0,1:T(8,128)(2,1)S(1)} collective-permute-done((bf16[15,8,1024]{2,0,1:T(8,128)(2,1)S(1)}, bf16[15,8,1024]{2,0,1:T(8,128)(2,1)S(1)}, u32[]{:S(2)}, u32[]{:S(2)}) %collective-permute-start) | collective-permute-done | bytes 245792 | tf_op jit(solution)/shard_map/ppermute | solution.py:13
  11.5 0.4 maximum_convert_fusion
  11.9 12.2 %fusion.43 = bf16[512,8,2,64]{0,3,1,2:T(8,128)(2,1)S(1)} fusion(f32[79,8,1024]{2,0,1:T(8,128)S(1)} %maximum_convert_fusion, f32[1024,1,512]{2,0,1:T(8,128)} %bitcast.73, f32[1024,1,512]{2,0,1:T(8,128)S(1)} %bitcast.72, f32[1024]{0:T(1024)S(1)} %bitcast.75, f32[1024]{0:T(1024)S(1)} %bitcast.76, f32[1024]{0:T(1024)S(1)} %bitcast.77, f32[1024]{0:T(1024)S(1)} %bitcast.78, ...), kind=kOutput, calls=%fused_computation.45 | convolution fusion | flops 6461849600 | bytes 38862848 | tf_op jit(solution)/shard_map/sin,nrk->kirs/dot_general | solution.py:60
  24.2 2.2 %copy.21 = bf16[512,8,2,64]{3,1,2,0:T(8,128)(2,1)S(1)} copy(bf16[512,8,2,64]{0,3,1,2:T(8,128)(2,1)S(1)} %fusion.43) | data formatting | bytes 2097152 | tf_op jit(solution)/shard_map/convert_element_type | solution.py:66
  26.4 1.2 reshape.139
  27.6 48.2 %all_to_all.23 = bf16[256,2,1024]{2,1,0:T(2,128)(2,1)S(1)} all-to-all(bf16[256,2,1024]{2,1,0:T(2,128)(2,1)S(1)} %reshape.139), channel_id=1, replica_groups=mesh['wide'=32,'tm'=8] {'wide','tm'}, dimensions={0} | all-to-all | bytes 2097152 | tf_op jit(solution)/shard_map/all_to_all | solution.py:68
  75.8 2.3 %reshape.140 = bf16[256,2,2,8,64]{4,3,2,1,0:T(8,128)(2,1)} reshape(bf16[256,2,1024]{2,1,0:T(2,128)(2,1)S(1)} %all_to_all.23) | data formatting | bytes 2097152
  78.0 3.9 %copy.30 = bf16[32,8,2,8,2,64]{5,4,1,3,0,2:T(2,128)(2,1)S(1)} copy(bf16[32,8,2,8,2,64]{5,3,4,2,1,0:T(8,128)(2,1)} %bitcast.66) | data formatting | bytes 2097152 | tf_op jit(solution)/shard_map/reshape | solution.py:69
  81.9 1.5 %reshape.135 = bf16[2,256,1024]{2,1,0:T(8,128)(2,1)S(1)} reshape(bf16[2,32,8,8,2,64]{5,4,3,2,1,0:T(2,128)(2,1)S(1)} %bitcast.63) | data formatting | bytes 2097152 | tf_op jit(solution)/shard_map/reshape | solution.py:74
  83.4 3.9 %fusion.68 = (bf16[2,32,8,8,1,64]{5,4,3,2,1,0:T(2,128)(2,1)S(1)}, bf16[2,32,8,8,1,64]{5,4,3,2,1,0:T(2,128)(2,1)S(1)}) fusion(bf16[2,32,8,8,2,64]{5,4,3,2,1,0:T(2,128)(2,1)S(1)} %bitcast.64), kind=kLoop, calls=%fused_computation.71 | loop fusion | flops 262144 | bytes 2097152 | tf_op jit(solution)/shard_map/slice | solution.py:71
  87.3 1.3 %convolution_bitcast_fusion.1 = f32[256,1,2,256]{0,3,2,1:T(8,128)} fusion(bf16[2,256,1024]{2,1,0:T(8,128)(2,1)S(1)} %reshape.135), kind=kOutput, calls=%fused_computation.48 | convolution fusion | flops 268435456 | bytes 1572864 | tf_op jit(solution)/shard_map/cak,cbk->acb/dot_general | solution.py:76
  88.6 5.6 %pad_maximum_fusion = bf16[2,32,8,8,2,64]{5,4,3,2,1,0:T(2,128)(2,1)S(1)} fusion(bf16[2,32,8,8,1,64]{5,4,3,2,1,0:T(2,128)(2,1)S(1)} %get-tuple-element.6, bf16[2,32,8,8,1,64]{5,4,3,2,1,0:T(2,128)(2,1)S(1)} %get-tuple-element.5), kind=kLoop, calls=%fused_computation.39 | loop fusion | flops 2097152 | bytes 2097152 | tf_op jit(solution)/shard_map/stack | solution.py:71
  94.1 2.3 %reshape.136 = bf16[2,256,1024]{2,1,0:T(8,128)(2,1)} reshape(bf16[2,32,8,8,2,64]{5,4,3,2,1,0:T(2,128)(2,1)S(1)} %pad_maximum_fusion) | data formatting | bytes 2097152 | tf_op jit(solution)/shard_map/reshape | solution.py:75
  96.4 0.0 copy-start
  96.4 1.7 %convolution_bitcast_fusion = f32[256,1,2,256]{0,3,2,1:T(8,128)S(1)} fusion(bf16[2,256,1024]{2,1,0:T(8,128)(2,1)S(1)} %reshape.135, bf16[2,256,1024]{2,1,0:T(8,128)(2,1)} %reshape.136), kind=kOutput, calls=%fused_computation.47 | convolution fusion | flops 268435456 | bytes 2621440 | tf_op jit(solution)/shard_map/cak,cbk->acb/dot_general | solution.py:77
  98.2 0.0 copy-done
  98.2 0.1 maximum_multiply_fusion.1
  98.3 0.6 copy.23
  98.9 20.7 %all_to_all.24 = f32[256,2,2,256]{3,2,1,0:T(2,128)S(1)} all-to-all(f32[256,2,2,256]{3,2,1,0:T(2,128)S(1)} %copy.23), channel_id=1, replica_groups=mesh['wide'=32,'tm'=8] {'tm'}, dimensions={0} | all-to-all | bytes 2097152 | tf_op jit(solution)/shard_map/all_to_all | solution.py:80
  119.6 0.2 copy.24
  119.8 0.1 copy.25
  119.9 1.6 %copy.26 = f32[32,2,16,256]{3,2,1,0:T(8,128)} copy(f32[32,2,16,256]{3,0,2,1:T(8,128)S(1)} %bitcast.71) | data formatting | bytes 2097152 | tf_op jit(solution)/shard_map/all_to_all | solution.py:80
  (2 shorter events, 0.1 us)
Async XLA Ops:
  1.7 4.9 %copy-start.1 = (f32[32,512]{1,0:T(8,128)S(1)}, f32[32,512]{1,0:T(8,128)}, u32[]{:S(2)}) copy-start(f32[32,512]{1,0:T(8,128)} %constant.17.clone) | copy-start | bytes 196612
  1.7 4.9 %copy-start.2 = (f32[32,512]{1,0:T(8,128)S(1)}, f32[32,512]{1,0:T(8,128)}, u32[]{:S(2)}) copy-start(f32[32,512]{1,0:T(8,128)} %constant.16.clone) | copy-start | bytes 196612
  1.7 4.9 %copy-start.3 = (f32[32,512]{1,0:T(8,128)S(1)}, f32[32,512]{1,0:T(8,128)}, u32[]{:S(2)}) copy-start(f32[32,512]{1,0:T(8,128)} %constant.15.clone) | copy-start | bytes 196612
  1.7 4.9 %copy-start.4 = (f32[32,512]{1,0:T(8,128)S(1)}, f32[32,512]{1,0:T(8,128)}, u32[]{:S(2)}) copy-start(f32[32,512]{1,0:T(8,128)} %constant.14.clone) | copy-start | bytes 196612
  2.4 6.0 %copy-start.5 = (s32[16,1024]{1,0:T(8,128)S(1)}, s32[16,1024]{1,0:T(8,128)}, u32[]{:S(2)}) copy-start(s32[16,1024]{1,0:T(8,128)} %param.7) | copy-start | bytes 196612
  2.4 9.1 %collective-permute-start = (bf16[15,8,1024]{2,0,1:T(8,128)(2,1)S(1)}, bf16[15,8,1024]{2,0,1:T(8,128)(2,1)S(1)}, u32[]{:S(2)}, u32[]{:S(2)}) collective-permute-start(bf16[15,8,1024]{2,0,1:T(8,128)(2,1)S(1)} %slice.141), channel_id=1, source_target_pairs={{0,1},{1,2},{2,3},{3,4},{4,5},{5,6},{6,7},{8,9},{9,10},{10,11},{11... | collective-permute-start | bytes 737288 | tf_op jit(solution)/shard_map/ppermute | solution.py:13
  96.4 1.8 %copy-start = (f32[256,1,2,256]{0,3,2,1:T(8,128)S(1)}, f32[256,1,2,256]{0,3,2,1:T(8,128)}, u32[]{:S(2)}) copy-start(f32[256,1,2,256]{0,3,2,1:T(8,128)} %convolution_bitcast_fusion.1) | copy-start | bytes 1572868

commit v2 on v1

--- a/solution.py
+++ b/solution.py
@@ -2,6 +2,8 @@
 import jax
 import jax.numpy as jnp
 from jax import lax
+from jax.experimental import pallas as pl
+from jax.experimental.pallas import tpu as pltpu
 from jax.sharding import PartitionSpec as P
 
 FIR_SCALE = 2.0 ** (-12)
@@ -61,23 +63,55 @@
         "sin,nrk->kirs",
         filtered,
         table,
-        precision=lax.Precision.HIGHEST,
+        precision=lax.Precision.HIGH,
         preferred_element_type=jnp.float32,
     ).astype(jnp.bfloat16)
     packed = spectra.reshape(groups, per_group, local_inputs, 2, spectra_dev)
     got = lax.all_to_all(packed, ("wide", "tm"), 0, 0, tiled=True)
-    got = got.reshape(widen, ranks, per_group, local_inputs, 2, spectra_dev)
-    got = got.transpose(2, 0, 3, 1, 4, 5)
-    rotated = jnp.stack([got[..., 1, :], -got[..., 0, :]], axis=-2)
+    got = got.reshape(widen, ranks, per_group, local_inputs, 2 * spectra_dev).astype(jnp.float32)
+    norm_factor = 1.0 / (spectra_dev * ranks)
+    grams = channel_grams(got, norm_factor)
+    back = lax.all_to_all(grams, "tm", 0, 0, tiled=True)
+    rows = back.shape[3]
+    return back.transpose(3, 1, 0, 2, 4).reshape(rows, 2, ranks * per_group, back.shape[4])
+
+
+def gram_kernel(scale, x_ref, o_ref):
+    widen, ranks, groups, local_inputs, depth = x_ref.shape
     inputs = widen * local_inputs
-    depth = ranks * 2 * spectra_dev
-    full = got.reshape(per_group, inputs, depth)
-    rotated = rotated.reshape(per_group, inputs, depth)
-    real_part = jnp.einsum("cak,cbk->acb", full, full, preferred_element_type=jnp.float32)
-    imag_part = jnp.einsum("cak,cbk->acb", rotated, full, preferred_element_type=jnp.float32)
-    norm_factor = 1.0 / (spectra_dev * ranks)
-    grams = jnp.stack([real_part, imag_part], axis=1) * norm_factor
-    return lax.all_to_all(grams, "tm", 0, 2, tiled=True)
+    half = depth // 2
+    lane = lax.broadcasted_iota(jnp.int32, (inputs, depth), 1)
+    sign = jnp.where(lane < half, -1.0, 1.0).astype(jnp.float32)
+    rows = inputs // ranks
+    for c in range(groups):
+        acc = jnp.zeros((inputs, 2 * inputs), jnp.float32)
+        for t in range(ranks):
+            x = x_ref[:, t, c, :, :].reshape(inputs, depth)
+            rot = pltpu.roll(x, half, 1) * sign
+            y = jnp.concatenate([x, rot], axis=0).astype(jnp.bfloat16)
+            acc = acc + lax.dot_general(
+                x.astype(jnp.bfloat16), y, (((1,), (1,)), ((), ())),
+                preferred_element_type=jnp.float32,
+            )
+        acc = acc * scale
+        o_ref[:, 0, c, :, :] = acc[:, :inputs].reshape(ranks, rows, inputs)
+        o_ref[:, 1, c, :, :] = acc[:, inputs:].reshape(ranks, rows, inputs)
+
+
+def channel_grams(got, scale):
+    widen, ranks, groups, local_inputs, depth = got.shape
+    inputs = widen * local_inputs
+    rows = inputs // ranks
+    flops = 2 * groups * ranks * inputs * 2 * inputs * depth
+    return pl.pallas_call(
+        lambda x_ref, o_ref: gram_kernel(scale, x_ref, o_ref),
+        out_shape=jax.ShapeDtypeStruct((ranks, 2, groups, rows, inputs), jnp.float32),
+        in_specs=[pl.BlockSpec(memory_space=pltpu.VMEM)],
+        out_specs=pl.BlockSpec(memory_space=pltpu.VMEM),
+        cost_estimate=pl.CostEstimate(
+            flops=flops, transcendentals=0, bytes_accessed=got.size * 4 + 2 * groups * inputs * inputs * 4
+        ),
+    )(got)
 
 
 def solution(mesh):

time: 122 us -> 119 us (0.975)
  local copies, waits for them, and re-layouts: 16.6 us -> 26.2 us
  other arithmetic: 13.4 us -> 3.88 us
  matrix products: 15.3 us -> 8.62 us
  Pallas kernels: 0 us -> 3.87 us
    convert_element_type x0 -> x2, local copies, waits for them, and re-layouts: none -> 9.69 us  [shards(): got.reshape(widen, ranks, per_group, local_inputs, 2 * spectra_dev)]
    another operation x1 -> x0, other arithmetic: 5.57 us -> none  [shards(): rotated = jnp.stack([got[..., 1, :], -got[..., 0, :]], axis=-2)]
    pallas_call x0 -> x1, Pallas kernels: none -> 3.87 us  [channel_grams(): pl.pallas_call(lambda x_ref, o_ref: gram_kernel(scale, x_ref, o_ref), out...]
    slice x1 -> x0, other arithmetic: 3.86 us -> none  [shards(): rotated = jnp.stack([got[..., 1, :], -got[..., 0, :]], axis=-2)]
    dot_general x1, matrix products: 12.2 us -> 8.62 us  [shards(): jnp.einsum('sin,nrk->kirs', filtered, table, precision=lax.Precision.HIGH...]
    dot_general x2 -> x0, matrix products: 3.02 us -> none  [the longest x1 1.75 us: shards(): jnp.einsum('cak,cbk->acb', rotated, full, preferred_element_type=jnp.floa...]
    unnamed x14 -> x12, local copies, waits for them, and re-layouts: 3.51 us -> 6.42 us
    reshape x3 -> x2, local copies, waits for them, and re-layouts: 7.66 us -> 5.09 us  [the longest x1 3.51 us: shards(): packed = spectra.reshape(groups, per_group, local_inputs, 2, spectra_dev)]
where the time goes in v2:
time: 119 us
  blocking collectives  69.2 us (58%)
  local copies, waits for them, and re-layouts  26.2 us (22%)
  matrix products  8.62 us (7%)
  starting transfers between devices  4.18 us (4%)
  other arithmetic  3.88 us (3%)
  Pallas kernels  3.87 us (3%)
  waiting for transfers between devices  3.03 us (3%)
    all_to_all x1, blocking collectives, shards(): got = lax.all_to_all(packed, ('wide', 'tm'), 0, 0, tiled=True)  48.1 us
    all_to_all x1, blocking collectives, shards(): back = lax.all_to_all(grams, 'tm', 0, 0, tiled=True)  21.1 us
    convert_element_type x2, local copies, waits for them, and re-layouts, shards(): got.reshape(widen, ranks, per_group, local_inputs, 2 * spectra_dev)  9.69 us
    dot_general x1, matrix products, shards(): jnp.einsum('sin,nrk->kirs', filtered, table, precision=lax.Precision.HIGH...  8.62 us
    unnamed x12, local copies, waits for them, and re-layouts  6.42 us
    ppermute x1, starting transfers between devices, shifted(): return lax.ppermute(array, axis, pairs)  4.18 us
    pallas_call x1, Pallas kernels, channel_grams(): pl.pallas_call(lambda x_ref, o_ref: gram_kernel(scale, x_ref, o_ref), out...  3.87 us
    reshape x1, local copies, waits for them, and re-layouts, shards(): packed = spectra.reshape(groups, per_group, local_inputs, 2, spectra_dev)  3.51 us
  transfers between devices with their start and end apart: 1, of which 1 were waited for; matrix products, arithmetic and copies ran while one was open for 2% of the time, Pallas kernels for 0%

profile of v2, /device:TPU:1, one launch (start us, length us, event | category | flops | bytes accessed | tf_op | source)
XLA Modules:
  0.0 119.1 jit_solution(5268110539987989014)
XLA Ops:
  0.0 1.7 %convert_element_type.27 = bf16[8,65536]{1,0:T(8,128)(2,1)S(1)} convert(s32[8,65536]{1,0:T(8,128)} %param.6) | non-fusion elementwise | flops 524288 | bytes 3145728 | tf_op jit(solution)/shard_map/convert_element_type | solution.py:52
  1.7 0.0 copy-start
  1.7 0.0 copy-start.1
  1.7 0.0 copy-start.2
  1.7 0.0 copy-start.3
  1.7 0.6 copy.29
  2.3 0.1 slice.133
  2.4 0.0 copy-start.4
  2.4 4.2 %collective-permute-start = (bf16[15,8,1024]{2,0,1:T(8,128)(2,1)S(1)}, bf16[15,8,1024]{2,0,1:T(8,128)(2,1)S(1)}, u32[]{:S(2)}, u32[]{:S(2)}) collective-permute-start(bf16[15,8,1024]{2,0,1:T(8,128)(2,1)S(1)} %slice.133), channel_id=1, source_target_pairs={{0,1},{1,2},{2,3},{3,4},{4,5},{5,6},{6,7},{8,9},{9,10},{10,11},{11... | collective-permute-start | bytes 737288 | tf_op jit(solution)/shard_map/ppermute | solution.py:15
  6.6 0.0 copy-done
  6.6 0.0 copy-done.1
  6.6 0.0 copy-done.2
  6.6 0.0 copy-done.3
  6.6 1.8 %multiply_subtract_fusion = (f32[32,32,512]{2,1,0:T(8,128)S(1)}, f32[32,32,512]{2,1,0:T(8,128)}) fusion(f32[32,512]{1,0:T(8,128)S(1)} %copy-done, f32[32,512]{1,0:T(8,128)S(1)} %copy-done.2, f32[32,512]{1,0:T(8,128)S(1)} %copy-done.1, f32[32,512]{1,0:T(8,128)S(1)} %copy-done.3), kind=kLoop, calls=%fused_computation.40 | loop fusion | flops 3145728 | bytes 4456448 | tf_op jit(solution)/shard_map/sub | solution.py:34
  8.4 0.0 copy-done.4
  8.5 3.0 %collective-permute-done = bf16[15,8,1024]{2,0,1:T(8,128)(2,1)S(1)} collective-permute-done((bf16[15,8,1024]{2,0,1:T(8,128)(2,1)S(1)}, bf16[15,8,1024]{2,0,1:T(8,128)(2,1)S(1)}, u32[]{:S(2)}, u32[]{:S(2)}) %collective-permute-start) | collective-permute-done | bytes 245792 | tf_op jit(solution)/shard_map/ppermute | solution.py:15
  11.5 0.4 maximum_convert_fusion
  11.9 8.6 %fusion.43 = bf16[512,8,2,64]{0,3,1,2:T(8,128)(2,1)S(1)} fusion(f32[79,8,1024]{2,0,1:T(8,128)S(1)} %maximum_convert_fusion, f32[1024,1,512]{2,0,1:T(8,128)} %bitcast.50, f32[1024,1,512]{2,0,1:T(8,128)S(1)} %bitcast.49, f32[1024]{0:T(1024)S(1)} %bitcast.52, f32[1024]{0:T(1024)S(1)} %bitcast.53, f32[1024]{0:T(1024)S(1)} %bitcast.54, f32[1024]{0:T(1024)S(1)} %bitcast.55, ...), kind=kOutput, calls=%fused_computation.42 | convolution fusion | flops 3240624128 | bytes 38862848 | tf_op jit(solution)/shard_map/sin,nrk->kirs/dot_general | solution.py:62
  20.6 2.2 %copy.21 = bf16[512,8,2,64]{3,1,2,0:T(8,128)(2,1)S(1)} copy(bf16[512,8,2,64]{0,3,1,2:T(8,128)(2,1)S(1)} %fusion.43) | data formatting | bytes 2097152 | tf_op jit(solution)/shard_map/convert_element_type | solution.py:68
  22.8 3.5 %copy.22 = bf16[256,2,8,2,64]{4,3,2,1,0:T(2,128)(2,1)} copy(bf16[256,2,8,2,64]{4,2,3,1,0:T(8,128)(2,1)S(1)} %bitcast.43) | data formatting | bytes 2097152 | tf_op jit(solution)/shard_map/reshape | solution.py:69
  26.3 5.2 %reshape.135 = bf16[256,2,1024]{2,1,0:T(2,128)(2,1)S(1)} reshape(bf16[256,2,8,2,64]{4,3,2,1,0:T(2,128)(2,1)} %copy.22) | data formatting | bytes 2097152
  31.4 48.1 %all_to_all.10 = bf16[256,2,1024]{2,1,0:T(2,128)(2,1)S(1)} all-to-all(bf16[256,2,1024]{2,1,0:T(2,128)(2,1)S(1)} %reshape.135), channel_id=1, replica_groups=mesh['wide'=32,'tm'=8] {'wide','tm'}, dimensions={0} | all-to-all | bytes 2097152 | tf_op jit(solution)/shard_map/all_to_all | solution.py:70
  79.6 1.2 %reshape.136 = bf16[256,2,8,2,64]{4,3,2,1,0:T(2,128)(2,1)S(1)} reshape(bf16[256,2,1024]{2,1,0:T(2,128)(2,1)S(1)} %all_to_all.10) | data formatting | bytes 2097152
  80.8 2.0 %copy.23 = bf16[256,2,8,2,64]{0,4,3,2,1:T(8,128)(2,1)S(1)} copy(bf16[256,2,8,2,64]{4,3,2,1,0:T(2,128)(2,1)S(1)} %reshape.136) | data formatting | bytes 2097152 | tf_op jit(solution)/shard_map/all_to_all | solution.py:70
  82.8 4.3 %copy.24 = f32[256,2,8,2,64]{4,3,2,1,0:T(2,128)} copy(bf16[256,2,8,2,64]{0,4,3,2,1:T(8,128)(2,1)S(1)} %copy.23) | data formatting | bytes 3145728 | tf_op jit(solution)/shard_map/convert_element_type | solution.py:71
  87.1 5.4 %reshape.132.x_ref = f32[32,8,2,8,128]{4,3,2,1,0:T(8,128)} reshape(f32[256,2,8,2,64]{4,3,2,1,0:T(2,128)} %copy.24) | data formatting | bytes 4194304 | tf_op jit(solution)/shard_map/convert_element_type | solution.py:71
  92.5 3.9 %shard_map.64 = f32[8,2,2,32,256]{4,3,2,1,0:T(8,128)} custom-call(f32[32,8,2,8,128]{4,3,2,1,0:T(8,128)} %reshape.132.x_ref), custom_call_target="tpu_custom_call" | custom-call | flops 536870912 | bytes 3145728 | tf_op jit(solution)/shard_map/pallas_call | solution.py:106
  96.3 21.1 %all_to_all.11 = f32[8,2,2,32,256]{4,3,2,1,0:T(8,128)S(1)} all-to-all(f32[8,2,2,32,256]{4,3,2,1,0:T(8,128)} %shard_map.64), channel_id=1, replica_groups=mesh['wide'=32,'tm'=8] {'tm'}, dimensions={0} | all-to-all | bytes 2097152 | tf_op jit(solution)/shard_map/all_to_all | solution.py:74
  117.4 0.1 copy.25
  117.5 1.6 %copy.26 = f32[32,2,16,256]{3,2,1,0:T(8,128)} copy(f32[32,2,16,256]{3,0,2,1:T(8,128)S(1)} %bitcast.48) | data formatting | bytes 2097152 | tf_op jit(solution)/shard_map/reshape | solution.py:76
  (2 shorter events, 0.1 us)
Async XLA Ops:
  1.7 4.9 %copy-start = (f32[32,512]{1,0:T(8,128)S(1)}, f32[32,512]{1,0:T(8,128)}, u32[]{:S(2)}) copy-start(f32[32,512]{1,0:T(8,128)} %constant.15.clone) | copy-start | bytes 196612
  1.7 4.9 %copy-start.1 = (f32[32,512]{1,0:T(8,128)S(1)}, f32[32,512]{1,0:T(8,128)}, u32[]{:S(2)}) copy-start(f32[32,512]{1,0:T(8,128)} %constant.14.clone) | copy-start | bytes 196612
  1.7 4.9 %copy-start.2 = (f32[32,512]{1,0:T(8,128)S(1)}, f32[32,512]{1,0:T(8,128)}, u32[]{:S(2)}) copy-start(f32[32,512]{1,0:T(8,128)} %constant.13.clone) | copy-start | bytes 196612
  1.7 4.9 %copy-start.3 = (f32[32,512]{1,0:T(8,128)S(1)}, f32[32,512]{1,0:T(8,128)}, u32[]{:S(2)}) copy-start(f32[32,512]{1,0:T(8,128)} %constant.12.clone) | copy-start | bytes 196612
  2.4 6.0 %copy-start.4 = (s32[16,1024]{1,0:T(8,128)S(1)}, s32[16,1024]{1,0:T(8,128)}, u32[]{:S(2)}) copy-start(s32[16,1024]{1,0:T(8,128)} %param.7) | copy-start | bytes 196612
  2.4 9.1 %collective-permute-start = (bf16[15,8,1024]{2,0,1:T(8,128)(2,1)S(1)}, bf16[15,8,1024]{2,0,1:T(8,128)(2,1)S(1)}, u32[]{:S(2)}, u32[]{:S(2)}) collective-permute-start(bf16[15,8,1024]{2,0,1:T(8,128)(2,1)S(1)} %slice.133), channel_id=1, source_target_pairs={{0,1},{1,2},{2,3},{3,4},{4,5},{5,6},{6,7},{8,9},{9,10},{10,11},{11... | collective-permute-start | bytes 737288 | tf_op jit(solution)/shard_map/ppermute | solution.py:15

commit v3 on v2

--- a/solution.py
+++ b/solution.py
@@ -66,41 +66,45 @@
         precision=lax.Precision.HIGH,
         preferred_element_type=jnp.float32,
     ).astype(jnp.bfloat16)
-    packed = spectra.reshape(groups, per_group, local_inputs, 2, spectra_dev)
+    packed = spectra.reshape(groups, per_group * local_inputs, 2 * spectra_dev)
     got = lax.all_to_all(packed, ("wide", "tm"), 0, 0, tiled=True)
-    got = got.reshape(widen, ranks, per_group, local_inputs, 2 * spectra_dev).astype(jnp.float32)
+    got = got.reshape(widen, ranks, per_group * local_inputs, 2 * spectra_dev)
     norm_factor = 1.0 / (spectra_dev * ranks)
-    grams = channel_grams(got, norm_factor)
+    grams = channel_grams(got, norm_factor, per_group)
     back = lax.all_to_all(grams, "tm", 0, 0, tiled=True)
     rows = back.shape[3]
     return back.transpose(3, 1, 0, 2, 4).reshape(rows, 2, ranks * per_group, back.shape[4])
 
 
 def gram_kernel(scale, x_ref, o_ref):
-    widen, ranks, groups, local_inputs, depth = x_ref.shape
+    widen, ranks, stacked, depth = x_ref.shape
+    groups = o_ref.shape[2]
+    local_inputs = stacked // groups
     inputs = widen * local_inputs
     half = depth // 2
     lane = lax.broadcasted_iota(jnp.int32, (inputs, depth), 1)
     sign = jnp.where(lane < half, -1.0, 1.0).astype(jnp.float32)
     rows = inputs // ranks
-    for c in range(groups):
-        acc = jnp.zeros((inputs, 2 * inputs), jnp.float32)
-        for t in range(ranks):
-            x = x_ref[:, t, c, :, :].reshape(inputs, depth)
+    accs = [jnp.zeros((inputs, 2 * inputs), jnp.float32) for _ in range(groups)]
+    for t in range(ranks):
+        block = x_ref[:, t, :, :].astype(jnp.float32)
+        for c in range(groups):
+            x = block[:, c * local_inputs : (c + 1) * local_inputs, :].reshape(inputs, depth)
             rot = pltpu.roll(x, half, 1) * sign
             y = jnp.concatenate([x, rot], axis=0).astype(jnp.bfloat16)
-            acc = acc + lax.dot_general(
+            accs[c] = accs[c] + lax.dot_general(
                 x.astype(jnp.bfloat16), y, (((1,), (1,)), ((), ())),
                 preferred_element_type=jnp.float32,
             )
-        acc = acc * scale
+    for c in range(groups):
+        acc = accs[c] * scale
         o_ref[:, 0, c, :, :] = acc[:, :inputs].reshape(ranks, rows, inputs)
         o_ref[:, 1, c, :, :] = acc[:, inputs:].reshape(ranks, rows, inputs)
 
 
-def channel_grams(got, scale):
-    widen, ranks, groups, local_inputs, depth = got.shape
-    inputs = widen * local_inputs
+def channel_grams(got, scale, groups):
+    widen, ranks, stacked, depth = got.shape
+    inputs = widen * stacked // groups
     rows = inputs // ranks
     flops = 2 * groups * ranks * inputs * 2 * inputs * depth
     return pl.pallas_call(
@@ -109,7 +113,7 @@
         in_specs=[pl.BlockSpec(memory_space=pltpu.VMEM)],
         out_specs=pl.BlockSpec(memory_space=pltpu.VMEM),
         cost_estimate=pl.CostEstimate(
-            flops=flops, transcendentals=0, bytes_accessed=got.size * 4 + 2 * groups * inputs * inputs * 4
+            flops=flops, transcendentals=0, bytes_accessed=got.size * 2 + 2 * groups * inputs * inputs * 4
         ),
     )(got)
 

time: 119 us -> 98.4 us (0.83)
  local copies, waits for them, and re-layouts: 26.2 us -> 5.4 us
    convert_element_type x2 -> x0, local copies, waits for them, and re-layouts: 9.69 us -> none  [shards(): got.reshape(widen, ranks, per_group, local_inputs, 2 * spectra_dev)]
    unnamed x12 -> x10, local copies, waits for them, and re-layouts: 6.42 us -> 0.03 us
    reshape x1, local copies, waits for them, and re-layouts: 3.51 us -> 1 us  [shards(): packed = spectra.reshape(groups, per_group * local_inputs, 2 * spectra_dev)]
    all_to_all x1 -> x0, local copies, waits for them, and re-layouts: 1.96 us -> none  [shards(): got = lax.all_to_all(packed, ('wide', 'tm'), 0, 0, tiled=True)]
where the time goes in v3:
time: 98.4 us; the launch traced here: 98.1 us
  blocking collectives  69.3 us (70%)
  matrix products  8.63 us (9%)
  local copies, waits for them, and re-layouts  5.4 us (5%)
  starting transfers between devices  4.18 us (4%)
  other arithmetic  3.88 us (4%)
  Pallas kernels  3.5 us (4%)
  waiting for transfers between devices  3.03 us (3%)
    all_to_all x1, blocking collectives, shards(): got = lax.all_to_all(packed, ('wide', 'tm'), 0, 0, tiled=True)  48.2 us
    all_to_all x1, blocking collectives, shards(): back = lax.all_to_all(grams, 'tm', 0, 0, tiled=True)  21.1 us
    dot_general x1, matrix products, shards(): jnp.einsum('sin,nrk->kirs', filtered, table, precision=lax.Precision.HIGH...  8.63 us
    ppermute x1, starting transfers between devices, shifted(): return lax.ppermute(array, axis, pairs)  4.18 us
    pallas_call x1, Pallas kernels, channel_grams(): pl.pallas_call(lambda x_ref, o_ref: gram_kernel(scale, x_ref, o_ref), out...  3.5 us
    ppermute x1, waiting for transfers between devices, shifted(): return lax.ppermute(array, axis, pairs)  3.03 us
    convert_element_type x1, local copies, waits for them, and re-layouts, shards(): spectra = jnp.einsum('sin,nrk->kirs', filtered, table, precision=lax.Prec...  1.98 us
  transfers between devices with their start and end apart: 1, of which 1 were waited for; matrix products, arithmetic and copies ran while one was open for 2% of the time, Pallas kernels for 0%

profile of v3, /device:TPU:1, one launch (start us, length us, event | category | flops | bytes accessed | tf_op | source)
XLA Modules:
  0.0 98.1 jit_solution(4028431150562163561)
XLA Ops:
  0.0 1.7 %convert_element_type.22 = bf16[8,65536]{1,0:T(8,128)(2,1)S(1)} convert(s32[8,65536]{1,0:T(8,128)} %param.6) | non-fusion elementwise | flops 524288 | bytes 3145728 | tf_op jit(solution)/shard_map/convert_element_type | solution.py:52
  1.7 0.0 copy-start
  1.7 0.0 copy-start.1
  1.7 0.0 copy-start.2
  1.7 0.0 copy-start.3
  1.7 0.6 copy.14
  2.3 0.1 slice.133
  2.4 0.0 copy-start.4
  2.4 4.2 %collective-permute-start = (bf16[15,8,1024]{2,0,1:T(8,128)(2,1)S(1)}, bf16[15,8,1024]{2,0,1:T(8,128)(2,1)S(1)}, u32[]{:S(2)}, u32[]{:S(2)}) collective-permute-start(bf16[15,8,1024]{2,0,1:T(8,128)(2,1)S(1)} %slice.133), channel_id=1, source_target_pairs={{0,1},{1,2},{2,3},{3,4},{4,5},{5,6},{6,7},{8,9},{9,10},{10,11},{11... | collective-permute-start | bytes 737288 | tf_op jit(solution)/shard_map/ppermute | solution.py:15
  6.6 0.0 copy-done
  6.6 0.0 copy-done.1
  6.6 0.0 copy-done.2
  6.6 0.0 copy-done.3
  6.6 1.8 %multiply_subtract_fusion = (f32[32,32,512]{2,1,0:T(8,128)S(1)}, f32[32,32,512]{2,1,0:T(8,128)}) fusion(f32[32,512]{1,0:T(8,128)S(1)} %copy-done, f32[32,512]{1,0:T(8,128)S(1)} %copy-done.2, f32[32,512]{1,0:T(8,128)S(1)} %copy-done.1, f32[32,512]{1,0:T(8,128)S(1)} %copy-done.3), kind=kLoop, calls=%fused_computation.40 | loop fusion | flops 3145728 | bytes 4456448 | tf_op jit(solution)/shard_map/sub | solution.py:34
  8.4 0.0 copy-done.4
  8.5 3.0 %collective-permute-done = bf16[15,8,1024]{2,0,1:T(8,128)(2,1)S(1)} collective-permute-done((bf16[15,8,1024]{2,0,1:T(8,128)(2,1)S(1)}, bf16[15,8,1024]{2,0,1:T(8,128)(2,1)S(1)}, u32[]{:S(2)}, u32[]{:S(2)}) %collective-permute-start) | collective-permute-done | bytes 245792 | tf_op jit(solution)/shard_map/ppermute | solution.py:15
  11.5 0.4 maximum_convert_fusion
  11.9 8.6 %fusion.43 = bf16[512,8,2,64]{0,3,1,2:T(8,128)(2,1)S(1)} fusion(f32[79,8,1024]{2,0,1:T(8,128)S(1)} %maximum_convert_fusion, f32[1024,1,512]{2,0,1:T(8,128)} %bitcast.50, f32[1024,1,512]{2,0,1:T(8,128)S(1)} %bitcast.49, f32[1024]{0:T(1024)S(1)} %bitcast.52, f32[1024]{0:T(1024)S(1)} %bitcast.53, f32[1024]{0:T(1024)S(1)} %bitcast.54, f32[1024]{0:T(1024)S(1)} %bitcast.55, ...), kind=kOutput, calls=%fused_computation.42 | convolution fusion | flops 3240624128 | bytes 38862848 | tf_op jit(solution)/shard_map/sin,nrk->kirs/dot_general | solution.py:62
  20.6 2.0 %copy.9 = bf16[512,8,2,64]{3,2,1,0:T(2,128)(2,1)S(1)} copy(bf16[512,8,2,64]{0,3,1,2:T(8,128)(2,1)S(1)} %fusion.43) | data formatting | bytes 2097152 | tf_op jit(solution)/shard_map/convert_element_type | solution.py:68
  22.6 1.0 %reshape.130 = bf16[256,16,128]{2,1,0:T(8,128)(2,1)S(1)} reshape(bf16[512,8,2,64]{3,2,1,0:T(2,128)(2,1)S(1)} %copy.9) | data formatting | bytes 2097152 | tf_op jit(solution)/shard_map/reshape | solution.py:69
  23.6 48.2 %all_to_all.10 = bf16[256,16,128]{2,1,0:T(8,128)(2,1)} all-to-all(bf16[256,16,128]{2,1,0:T(8,128)(2,1)S(1)} %reshape.130), channel_id=1, replica_groups=mesh['wide'=32,'tm'=8] {'wide','tm'}, dimensions={0} | all-to-all | bytes 2097152 | tf_op jit(solution)/shard_map/all_to_all | solution.py:70
  71.8 3.5 %shard_map.64 = f32[8,2,2,32,256]{4,3,2,1,0:T(8,128)} custom-call(bf16[32,8,16,128]{3,2,1,0:T(8,128)(2,1)} %bitcast.46), custom_call_target="tpu_custom_call" | custom-call | flops 536870912 | bytes 2097152 | tf_op jit(solution)/shard_map/pallas_call | solution.py:110
  75.3 21.1 %all_to_all.11 = f32[8,2,2,32,256]{4,3,2,1,0:T(8,128)S(1)} all-to-all(f32[8,2,2,32,256]{4,3,2,1,0:T(8,128)} %shard_map.64), channel_id=1, replica_groups=mesh['wide'=32,'tm'=8] {'tm'}, dimensions={0} | all-to-all | bytes 2097152 | tf_op jit(solution)/shard_map/all_to_all | solution.py:74
  96.4 0.1 copy.10
  96.5 1.6 %copy.11 = f32[32,2,16,256]{3,2,1,0:T(8,128)} copy(f32[32,2,16,256]{3,0,2,1:T(8,128)S(1)} %bitcast.48) | data formatting | bytes 2097152 | tf_op jit(solution)/shard_map/reshape | solution.py:76
  (2 shorter events, 0.1 us)
Async XLA Ops:
  1.7 4.9 %copy-start = (f32[32,512]{1,0:T(8,128)S(1)}, f32[32,512]{1,0:T(8,128)}, u32[]{:S(2)}) copy-start(f32[32,512]{1,0:T(8,128)} %constant.15.clone) | copy-start | bytes 196612
  1.7 4.9 %copy-start.1 = (f32[32,512]{1,0:T(8,128)S(1)}, f32[32,512]{1,0:T(8,128)}, u32[]{:S(2)}) copy-start(f32[32,512]{1,0:T(8,128)} %constant.14.clone) | copy-start | bytes 196612
  1.7 4.9 %copy-start.2 = (f32[32,512]{1,0:T(8,128)S(1)}, f32[32,512]{1,0:T(8,128)}, u32[]{:S(2)}) copy-start(f32[32,512]{1,0:T(8,128)} %constant.13.clone) | copy-start | bytes 196612
  1.7 4.9 %copy-start.3 = (f32[32,512]{1,0:T(8,128)S(1)}, f32[32,512]{1,0:T(8,128)}, u32[]{:S(2)}) copy-start(f32[32,512]{1,0:T(8,128)} %constant.12.clone) | copy-start | bytes 196612
  2.4 6.0 %copy-start.4 = (s32[16,1024]{1,0:T(8,128)S(1)}, s32[16,1024]{1,0:T(8,128)}, u32[]{:S(2)}) copy-start(s32[16,1024]{1,0:T(8,128)} %param.7) | copy-start | bytes 196612
  2.4 9.1 %collective-permute-start = (bf16[15,8,1024]{2,0,1:T(8,128)(2,1)S(1)}, bf16[15,8,1024]{2,0,1:T(8,128)(2,1)S(1)}, u32[]{:S(2)}, u32[]{:S(2)}) collective-permute-start(bf16[15,8,1024]{2,0,1:T(8,128)(2,1)S(1)} %slice.133), channel_id=1, source_target_pairs={{0,1},{1,2},{2,3},{3,4},{4,5},{5,6},{6,7},{8,9},{9,10},{10,11},{11... | collective-permute-start | bytes 737288 | tf_op jit(solution)/shard_map/ppermute | solution.py:15

commit v4 on v3

--- a/solution.py
+++ b/solution.py
@@ -51,21 +51,29 @@
     frames = voltages.reshape(local_inputs, spectra_dev, length).transpose(1, 0, 2)
     frames = frames.astype(jnp.bfloat16)
     previous = shifted(frames[spectra_dev - (lags - 1) :], "tm", 1)
-    extended = jnp.concatenate([previous, frames], axis=0).astype(jnp.float32)
     taps_float = taps.astype(jnp.float32)
-    filtered = taps_float[0] * extended[lags - 1 : lags - 1 + spectra_dev]
-    for lag in range(1, lags):
-        filtered = filtered + taps_float[lag] * extended[lags - 1 - lag : lags - 1 - lag + spectra_dev]
-    filtered = filtered * FIR_SCALE
+    table = dft_table(length, channels)
 
-    table = dft_table(length, channels)
-    spectra = jnp.einsum(
-        "sin,nrk->kirs",
-        filtered,
-        table,
-        precision=lax.Precision.HIGH,
-        preferred_element_type=jnp.float32,
-    ).astype(jnp.bfloat16)
+    def channelize(extended, count):
+        extended = extended.astype(jnp.float32)
+        filtered = taps_float[0] * extended[lags - 1 : lags - 1 + count]
+        for lag in range(1, lags):
+            filtered = filtered + taps_float[lag] * extended[lags - 1 - lag : lags - 1 - lag + count]
+        filtered = filtered * FIR_SCALE
+        return [
+            jnp.einsum(
+                "sin,nk->kis",
+                filtered,
+                table[:, part, :],
+                precision=lax.Precision.HIGH,
+                preferred_element_type=jnp.float32,
+            ).astype(jnp.bfloat16)
+            for part in range(2)
+        ]
+
+    later = channelize(frames, spectra_dev - (lags - 1))
+    head = channelize(jnp.concatenate([previous, frames[: 2 * (lags - 1)]], axis=0), lags - 1)
+    spectra = jnp.concatenate([head[0], later[0], head[1], later[1]], axis=-1)
     packed = spectra.reshape(groups, per_group * local_inputs, 2 * spectra_dev)
     got = lax.all_to_all(packed, ("wide", "tm"), 0, 0, tiled=True)
     got = got.reshape(widen, ranks, per_group * local_inputs, 2 * spectra_dev)

time: 98.4 us -> 90.8 us (0.923)
  other arithmetic: 3.88 us -> 8.67 us
  matrix products: 8.63 us -> 4.93 us
  waiting for transfers between devices: 3.03 us -> 0.01 us
  blocking collectives: 69.3 us -> 66.5 us
  local copies, waits for them, and re-layouts: 5.4 us -> 2.62 us
    mul x0 -> x3, other arithmetic: none -> 5.2 us  [the longest x2 4.69 us: channelize(): filtered = filtered * FIR_SCALE]
    dot_general x1 -> x4, matrix products: 8.63 us -> 4.93 us  [channelize(): jnp.einsum('sin,nk->kis', filtered, table[:, part, :], precision=lax.Prec...]
    ppermute x1, waiting for transfers between devices: 3.03 us -> 0.01 us  [shifted(): return lax.ppermute(array, axis, pairs)]
    all_to_all x1, blocking collectives: 48.2 us -> 45.5 us  [shards(): got = lax.all_to_all(packed, ('wide', 'tm'), 0, 0, tiled=True)]
    convert_element_type x2 -> x0, local copies, waits for them, and re-layouts: 2.56 us -> none  [the longest x1 1.98 us: shards(): spectra = jnp.einsum('sin,nrk->kirs', filtered, table, precision=lax.Prec...]
    sub x1, other arithmetic: 1.8 us -> 0.61 us  [dft_table(): re = ch[:, None, :] * cl[None, :, :] - sh[:, None, :] * sl[None, :, :]]
    reshape x1 -> x0, local copies, waits for them, and re-layouts: 1 us -> none  [shards(): packed = spectra.reshape(groups, per_group * local_inputs, 2 * spectra_dev)]
    convert_element_type x1 -> x2, other arithmetic: 1.69 us -> 2.37 us  [shards(): frames = frames.astype(jnp.bfloat16)]
  transfers between devices with their start and end apart: 1 -> 1, of which waited for: 1 -> 0; matrix products, arithmetic and copies ran while one was open for 2% -> 9% of each run, Pallas kernels for 0% -> 0%
where the time goes in v4:
time: 90.8 us; the launch traced here: 90.5 us
  blocking collectives  66.5 us (73%)
  other arithmetic  8.67 us (10%)
  matrix products  4.93 us (5%)
  starting transfers between devices  4.05 us (4%)
  Pallas kernels  3.5 us (4%)
  local copies, waits for them, and re-layouts  2.62 us (3%)
    all_to_all x1, blocking collectives, shards(): got = lax.all_to_all(packed, ('wide', 'tm'), 0, 0, tiled=True)  45.5 us
    all_to_all x1, blocking collectives, shards(): back = lax.all_to_all(grams, 'tm', 0, 0, tiled=True)  21.1 us
    dot_general x4, matrix products, channelize(): jnp.einsum('sin,nk->kis', filtered, table[:, part, :], precision=lax.Prec...  4.93 us
    mul x2, other arithmetic, channelize(): filtered = filtered * FIR_SCALE  4.69 us
    ppermute x1, starting transfers between devices, shifted(): return lax.ppermute(array, axis, pairs)  4.05 us
    pallas_call x1, Pallas kernels, channel_grams(): pl.pallas_call(lambda x_ref, o_ref: gram_kernel(scale, x_ref, o_ref), out...  3.5 us
    convert_element_type x2, other arithmetic, shards(): frames = frames.astype(jnp.bfloat16)  2.37 us
  transfers between devices with their start and end apart: 1, of which 0 were waited for; matrix products, arithmetic and copies ran while one was open for 9% of the time, Pallas kernels for 0%

profile of v4, /device:TPU:1, one launch (start us, length us, event | category | flops | bytes accessed | tf_op | source)
XLA Modules:
  0.0 90.5 jit_solution(16005093081457495822)
XLA Ops:
  0.0 1.7 %convert_element_type.43 = bf16[8,65536]{1,0:T(8,128)(2,1)S(1)} convert(s32[8,65536]{1,0:T(8,128)} %param.6) | non-fusion elementwise | flops 524288 | bytes 3145728 | tf_op jit(solution)/shard_map/convert_element_type | solution.py:52
  1.7 0.0 copy-start.4
  1.7 0.7 copy_bitcast_fusion
  2.4 0.0 copy-start
  2.4 0.0 copy-start.1
  2.4 0.0 copy-start.2
  2.4 0.0 copy-start.3
  2.4 0.1 slice.228
  2.5 4.0 %collective-permute-start = (bf16[15,8,1024]{2,0,1:T(8,128)(2,1)S(1)}, bf16[15,8,1024]{2,0,1:T(8,128)(2,1)S(1)}, u32[]{:S(2)}, u32[]{:S(2)}) collective-permute-start(bf16[15,8,1024]{2,0,1:T(8,128)(2,1)S(1)} %slice.228), channel_id=1, source_target_pairs={{0,1},{1,2},{2,3},{3,4},{4,5},{5,6},{6,7},{8,9},{9,10},{10,11},{11... | collective-permute-start | bytes 737288 | tf_op jit(solution)/shard_map/ppermute | solution.py:15
  6.6 0.0 copy-done.4
  6.7 0.0 copy-done
  6.7 0.0 copy-done.1
  6.7 0.0 copy-done.2
  6.7 0.0 copy-done.3
  6.7 0.6 multiply_subtract_fusion
  7.4 0.5 maximum_multiply_fusion
  7.9 3.7 %fusion.5 = f32[49,8,1024]{2,0,1:T(8,128)S(1)} fusion(f32[64,8,1024]{2,0,1:T(8,128)S(1)} %get-tuple-element.6, f32[1024]{0:T(1024)S(1)} %bitcast.74, f32[1024]{0:T(1024)S(1)} %bitcast.76, f32[1024]{0:T(1024)S(1)} %bitcast.78, f32[1024]{0:T(1024)S(1)} %bitcast.80, f32[1024]{0:T(1024)S(1)} %bitcast.82, f32[1024]{0:T(1024)S(1)} %bitcast.84, ...), kind=kLoop, calls=%fused_computation.11 | loop fusion | flops 12845056 | bytes 27361280 | tf_op jit(solution)/shard_map/mul | solution.py:62
  11.5 1.7 %fusion.23 = bf16[512,8,49]{0,2,1:T(8,128)(2,1)S(1)} fusion(f32[49,8,1024]{2,0,1:T(8,128)S(1)} %fusion.5, f32[1024,2,512]{2,0,1:T(8,128)S(1)} %maximum_multiply_fusion), kind=kOutput, calls=%fused_computation.44 | convolution fusion | flops 1233326080 | bytes 4333568 | tf_op jit(solution)/shard_map/sin,nk->kis/dot_general | solution.py:64
  13.2 1.7 %fusion.22 = bf16[512,8,49]{0,2,1:T(8,128)(2,1)S(1)} fusion(f32[49,8,1024]{2,0,1:T(8,128)S(1)} %fusion.5, f32[1024,2,512]{2,0,1:T(8,128)S(1)} %maximum_multiply_fusion), kind=kOutput, calls=%fused_computation.43 | convolution fusion | flops 1233326080 | bytes 4333568 | tf_op jit(solution)/shard_map/sin,nk->kis/dot_general | solution.py:64
  14.9 0.0 collective-permute-done
  14.9 0.2 maximum_convert_fusion
  15.2 1.0 %fusion.29 = f32[15,8,1024]{2,0,1:T(8,128)S(1)} fusion(f32[45,8,1024]{2,0,1:T(8,128)S(1)} %maximum_convert_fusion, f32[1024]{0:T(1024)S(1)} %bitcast.75, f32[1024]{0:T(1024)S(1)} %bitcast.77, f32[1024]{0:T(1024)S(1)} %bitcast.79, f32[1024]{0:T(1024)S(1)} %bitcast.81, f32[1024]{0:T(1024)S(1)} %bitcast.83, f32[1024]{0:T(1024)S(1)} %bitcast.85, ...), kind=kLoop, calls=%fused_computation.54 | loop fusion | flops 3932160 | bytes 8421376 | tf_op jit(solution)/shard_map/mul | solution.py:62
  16.2 0.8 fusion.27
  17.0 0.8 fusion.26
  17.7 0.3 pad_maximum_fusion
  18.0 0.8 copy.9
  18.8 45.5 %all_to_all.10 = bf16[256,16,128]{2,1,0:T(8,128)(2,1)} all-to-all(bf16[256,16,128]{2,1,0:T(8,128)(2,1)S(1)} %bitcast.68), channel_id=1, replica_groups=mesh['wide'=32,'tm'=8] {'wide','tm'}, dimensions={0} | all-to-all | bytes 2097152 | tf_op jit(solution)/shard_map/all_to_all | solution.py:78
  64.3 3.5 %shard_map.64 = f32[8,2,2,32,256]{4,3,2,1,0:T(8,128)} custom-call(bf16[32,8,16,128]{3,2,1,0:T(8,128)(2,1)} %bitcast.69), custom_call_target="tpu_custom_call" | custom-call | flops 536870912 | bytes 2097152 | tf_op jit(solution)/shard_map/pallas_call | solution.py:118
  67.8 21.1 %all_to_all.11 = f32[8,2,2,32,256]{4,3,2,1,0:T(8,128)S(1)} all-to-all(f32[8,2,2,32,256]{4,3,2,1,0:T(8,128)} %shard_map.64), channel_id=1, replica_groups=mesh['wide'=32,'tm'=8] {'tm'}, dimensions={0} | all-to-all | bytes 2097152 | tf_op jit(solution)/shard_map/all_to_all | solution.py:82
  88.8 0.1 copy.10
  88.9 1.6 %copy.11 = f32[32,2,16,256]{3,2,1,0:T(8,128)} copy(f32[32,2,16,256]{3,0,2,1:T(8,128)S(1)} %bitcast.71) | data formatting | bytes 2097152 | tf_op jit(solution)/shard_map/reshape | solution.py:84
  (3 shorter events, 0.1 us)
Async XLA Ops:
  1.7 4.9 %copy-start.4 = (s32[16,1024]{1,0:T(8,128)S(1)}, s32[16,1024]{1,0:T(8,128)}, u32[]{:S(2)}) copy-start(s32[16,1024]{1,0:T(8,128)} %param.7) | copy-start | bytes 196612
  2.4 4.3 %copy-start = (f32[32,512]{1,0:T(8,128)S(1)}, f32[32,512]{1,0:T(8,128)}, u32[]{:S(2)}) copy-start(f32[32,512]{1,0:T(8,128)} %constant.16.clone) | copy-start | bytes 196612
  2.4 4.3 %copy-start.1 = (f32[32,512]{1,0:T(8,128)S(1)}, f32[32,512]{1,0:T(8,128)}, u32[]{:S(2)}) copy-start(f32[32,512]{1,0:T(8,128)} %constant.15.clone) | copy-start | bytes 196612
  2.4 4.3 %copy-start.2 = (f32[32,512]{1,0:T(8,128)S(1)}, f32[32,512]{1,0:T(8,128)}, u32[]{:S(2)}) copy-start(f32[32,512]{1,0:T(8,128)} %constant.14.clone) | copy-start | bytes 196612
  2.4 4.3 %copy-start.3 = (f32[32,512]{1,0:T(8,128)S(1)}, f32[32,512]{1,0:T(8,128)}, u32[]{:S(2)}) copy-start(f32[32,512]{1,0:T(8,128)} %constant.5.clone) | copy-start | bytes 196612
  2.5 12.4 %collective-permute-start = (bf16[15,8,1024]{2,0,1:T(8,128)(2,1)S(1)}, bf16[15,8,1024]{2,0,1:T(8,128)(2,1)S(1)}, u32[]{:S(2)}, u32[]{:S(2)}) collective-permute-start(bf16[15,8,1024]{2,0,1:T(8,128)(2,1)S(1)} %slice.228), channel_id=1, source_target_pairs={{0,1},{1,2},{2,3},{3,4},{4,5},{5,6},{6,7},{8,9},{9,10},{10,11},{11... | collective-permute-start | bytes 737288 | tf_op jit(solution)/shard_map/ppermute | solution.py:15

commit v5 on v4

--- a/solution.py
+++ b/solution.py
@@ -48,18 +48,12 @@
     groups = widen * ranks
     per_group = channels // groups
 
-    frames = voltages.reshape(local_inputs, spectra_dev, length).transpose(1, 0, 2)
-    frames = frames.astype(jnp.bfloat16)
-    previous = shifted(frames[spectra_dev - (lags - 1) :], "tm", 1)
-    taps_float = taps.astype(jnp.float32)
+    tail = voltages[:, (spectra_dev - (lags - 1)) * length :]
+    tail = tail.reshape(local_inputs, lags - 1, length).transpose(1, 0, 2).astype(jnp.bfloat16)
+    previous = shifted(tail, "tm", 1)
     table = dft_table(length, channels)
 
-    def channelize(extended, count):
-        extended = extended.astype(jnp.float32)
-        filtered = taps_float[0] * extended[lags - 1 : lags - 1 + count]
-        for lag in range(1, lags):
-            filtered = filtered + taps_float[lag] * extended[lags - 1 - lag : lags - 1 - lag + count]
-        filtered = filtered * FIR_SCALE
+    def channelize(filtered):
         return [
             jnp.einsum(
                 "sin,nk->kis",
@@ -71,8 +65,9 @@
             for part in range(2)
         ]
 
-    later = channelize(frames, spectra_dev - (lags - 1))
-    head = channelize(jnp.concatenate([previous, frames[: 2 * (lags - 1)]], axis=0), lags - 1)
+    later = channelize(polyphase(voltages, taps, lags - 1, spectra_dev - (lags - 1), None))
+    head_frames = voltages[:, : (lags - 1) * length]
+    head = channelize(polyphase(head_frames, taps, 0, lags - 1, previous))
     spectra = jnp.concatenate([head[0], later[0], head[1], later[1]], axis=-1)
     packed = spectra.reshape(groups, per_group * local_inputs, 2 * spectra_dev)
     got = lax.all_to_all(packed, ("wide", "tm"), 0, 0, tiled=True)
@@ -82,6 +77,60 @@
     back = lax.all_to_all(grams, "tm", 0, 0, tiled=True)
     rows = back.shape[3]
     return back.transpose(3, 1, 0, 2, 4).reshape(rows, 2, ranks * per_group, back.shape[4])
+
+
+def fir_kernel(first, count, v_ref, taps_ref, *rest):
+    if len(rest) == 4:
+        h_ref, o_ref, ext_ref, tb_ref = rest
+    else:
+        h_ref = None
+        o_ref, ext_ref, tb_ref = rest
+    lags, length = taps_ref.shape
+    local_inputs = v_ref.shape[0]
+    taps = taps_ref[...].astype(jnp.float32) * FIR_SCALE
+    for lag in range(lags):
+        tb_ref[lag] = jnp.broadcast_to(taps[lag : lag + 1, :], (local_inputs, length))
+    if h_ref is not None:
+        ext_ref[0 : lags - 1] = h_ref[...].astype(jnp.float32)
+
+    def fill(j, carry):
+        start = pl.multiple_of(j * length, length)
+        ext_ref[lags - 1 + j] = v_ref[:, pl.ds(start, length)].astype(jnp.float32)
+        return carry
+
+    lax.fori_loop(0, first + count, fill, 0)
+
+    def body(k, carry):
+        at = first + k + lags - 1
+        acc = tb_ref[0] * ext_ref[at]
+        for lag in range(1, lags):
+            acc = acc + tb_ref[lag] * ext_ref[at - lag]
+        o_ref[k] = acc
+        return carry
+
+    lax.fori_loop(0, count, body, 0)
+
+
+def polyphase(frames, taps, first, count, halo):
+    local_inputs = frames.shape[0]
+    lags, length = taps.shape
+    operands = [frames, taps] + ([halo] if halo is not None else [])
+    vmem = pl.BlockSpec(memory_space=pltpu.VMEM)
+    return pl.pallas_call(
+        lambda *refs: fir_kernel(first, count, *refs),
+        out_shape=jax.ShapeDtypeStruct((count, local_inputs, length), jnp.float32),
+        in_specs=[vmem] * len(operands),
+        out_specs=vmem,
+        scratch_shapes=[
+            pltpu.VMEM((first + count + lags - 1, local_inputs, length), jnp.float32),
+            pltpu.VMEM((lags, local_inputs, length), jnp.float32),
+        ],
+        cost_estimate=pl.CostEstimate(
+            flops=2 * lags * count * local_inputs * length,
+            transcendentals=0,
+            bytes_accessed=frames.size * 4 + count * local_inputs * length * 4,
+        ),
+    )(*operands)
 
 
 def gram_kernel(scale, x_ref, o_ref):

time: 90.8 us -> 101 us (1.11)
  Pallas kernels: 3.5 us -> 12.3 us
  other arithmetic: 8.67 us -> 3.41 us
  matrix products: 4.93 us -> 9.57 us
  local copies, waits for them, and re-layouts: 2.62 us -> 4.08 us
    pallas_call x0 -> x2, Pallas kernels: none -> 8.81 us  [polyphase(): pl.pallas_call(lambda *refs: fir_kernel(first, count, *refs), out_shape=j...]
    mul x2 -> x0, other arithmetic: 4.69 us -> none  [channelize(): filtered = filtered * FIR_SCALE]
    dot_general x4, matrix products: 4.93 us -> 9.57 us  [channelize(): jnp.einsum('sin,nk->kis', filtered, table[:, part, :], precision=lax.Prec...]
    convert_element_type x4 -> x0, other arithmetic: 2.58 us -> none  [the longest x2 2.37 us: shards(): frames = frames.astype(jnp.bfloat16)]
    another operation x0 -> x1, other arithmetic: none -> 2.01 us
    unnamed x10 -> x16, local copies, waits for them, and re-layouts: 0.03 us -> 1.63 us
  transfers between devices with their start and end apart: 1 -> 1, of which waited for: 0 -> 0; matrix products, arithmetic and copies ran while one was open for 9% -> 6% of each run, Pallas kernels for 0% -> 6%
where the time goes in v5:
time: 101 us; the launch traced here: 100 us
  blocking collectives  66.5 us (66%)
  Pallas kernels  12.3 us (12%)
  matrix products  9.57 us (9%)
  starting transfers between devices  4.18 us (4%)
  local copies, waits for them, and re-layouts  4.08 us (4%)
  other arithmetic  3.41 us (3%)
    all_to_all x1, blocking collectives, shards(): got = lax.all_to_all(packed, ('wide', 'tm'), 0, 0, tiled=True)  45.5 us
    all_to_all x1, blocking collectives, shards(): back = lax.all_to_all(grams, 'tm', 0, 0, tiled=True)  21.1 us
    dot_general x4, matrix products, channelize(): jnp.einsum('sin,nk->kis', filtered, table[:, part, :], precision=lax.Prec...  9.57 us
    pallas_call x2, Pallas kernels, polyphase(): pl.pallas_call(lambda *refs: fir_kernel(first, count, *refs), out_shape=j...  8.81 us
    ppermute x1, starting transfers between devices, shifted(): return lax.ppermute(array, axis, pairs)  4.18 us
    pallas_call x1, Pallas kernels, channel_grams(): pl.pallas_call(lambda x_ref, o_ref: gram_kernel(scale, x_ref, o_ref), out...  3.5 us
  transfers between devices with their start and end apart: 1, of which 0 were waited for; matrix products, arithmetic and copies ran while one was open for 6% of the time, Pallas kernels for 6%

profile of v5, /device:TPU:1, one launch (start us, length us, event | category | flops | bytes accessed | tf_op | source)
XLA Modules:
  0.0 100.2 jit_solution(15857201623099046018)
XLA Ops:
  0.0 2.0 %slice_convert_fusion = (bf16[8,15360]{1,0:T(8,128)(2,1)S(1)}, s32[8,15360]{1,0:T(8,128)}) fusion(s32[8,65536]{1,0:T(8,128)} %refs_0_.1), kind=kLoop, calls=%fused_computation.22 | loop fusion | flops 122880 | bytes 1720320 | tf_op jit(solution)/shard_map/convert
  2.0 0.0 copy-start.4
  2.0 0.0 copy-start.5
  2.0 0.0 copy-start.6
  2.0 0.0 copy-start.7
  2.0 4.2 %collective-permute-start = (bf16[15,8,1024]{2,1,0:T(8,128)(2,1)S(1)}, bf16[15,8,1024]{2,1,0:T(8,128)(2,1)S(1)}, u32[]{:S(2)}, u32[]{:S(2)}) collective-permute-start(bf16[15,8,1024]{2,1,0:T(8,128)(2,1)S(1)} %bitcast.49), channel_id=1, source_target_pairs={{0,1},{1,2},{2,3},{3,4},{4,5},{5,6},{6,7},{8,9},{9,10},{10,11},{11... | collective-permute-start | bytes 737288 | tf_op jit(solution)/shard_map/ppermute | solution.py:15
  6.2 5.9 %shard_map.65 = f32[49,8,1024]{2,1,0:T(8,128)} custom-call(s32[8,65536]{1,0:T(8,128)} %refs_0_.1, s32[16,1024]{1,0:T(8,128)} %refs_1_.3), custom_call_target="tpu_custom_call" | custom-call | flops 12845056 | bytes 3702784 | tf_op jit(solution)/shard_map/pallas_call | solution.py:119
  12.1 0.0 copy-done.4
  12.1 0.0 copy-done.5
  12.1 0.0 copy-done.6
  12.1 0.0 copy-done.7
  12.1 0.6 multiply_subtract_fusion
  12.8 0.0 copy-start
  12.8 0.5 maximum_multiply_fusion
  13.3 0.9 copy-done
  14.2 0.0 copy-start.1
  14.2 2.3 %fusion.12 = bf16[512,8,49]{0,2,1:T(8,128)(2,1)S(1)} fusion(f32[49,8,1024]{2,1,0:T(8,128)S(1)} %copy-done, f32[1024,2,512]{2,0,1:T(8,128)S(1)} %maximum_multiply_fusion), kind=kOutput, calls=%fused_computation.13 | convolution fusion | flops 1233326080 | bytes 4104192 | tf_op jit(solution)/shard_map/sin,nk->kis/dot_general | solution.py:58
  16.5 0.0 copy-done.1
  16.5 2.3 %fusion.15 = bf16[512,8,49]{0,2,1:T(8,128)(2,1)S(1)} fusion(f32[49,8,1024]{2,1,0:T(8,128)S(1)} %copy-done, f32[1024,2,512]{2,0,1:T(8,128)S(1)} %maximum_multiply_fusion), kind=kOutput, calls=%fused_computation.14 | convolution fusion | flops 1233326080 | bytes 4104192 | tf_op jit(solution)/shard_map/sin,nk->kis/dot_general | solution.py:58
  18.7 0.0 collective-permute-done.refs_2_
  18.8 0.0 copy-start.3
  18.8 0.7 copy-done.3
  19.5 2.9 %shard_map.64 = f32[15,8,1024]{2,1,0:T(8,128)} custom-call(s32[8,15360]{1,0:T(8,128)} %get-tuple-element.6.refs_0_, s32[16,1024]{1,0:T(8,128)} %refs_1_.3, bf16[15,8,1024]{2,1,0:T(8,128)(2,1)} %copy-done.3), custom_call_target="tpu_custom_call" | custom-call | flops 3932160 | bytes 983040 | tf_op jit(solution)/shard_map/pallas_call | solution.py:119
  22.4 0.0 copy-start.2
  22.4 2.6 %fusion.20 = bf16[512,8,15]{0,2,1:T(8,128)(2,1)S(1)} fusion(f32[1024,2,512]{2,0,1:T(8,128)} %copy-done.1, f32[15,8,1024]{2,1,0:T(8,128)} %shard_map.64), kind=kOutput, calls=%fused_computation.17 | convolution fusion | flops 377548800 | bytes 2711552 | tf_op jit(solution)/shard_map/sin,nk->kis/dot_general | solution.py:58
  25.0 0.0 copy-done.2
  25.0 2.5 %fusion.21 = bf16[512,8,15]{0,2,1:T(8,128)(2,1)S(1)} fusion(f32[1024,2,512]{2,0,1:T(8,128)} %copy-done.1, f32[15,8,1024]{2,1,0:T(8,128)S(1)} %copy-done.2), kind=kOutput, calls=%fused_computation.18 | convolution fusion | flops 377548800 | bytes 2711552 | tf_op jit(solution)/shard_map/sin,nk->kis/dot_general | solution.py:58
  27.5 0.3 pad_maximum_fusion
  27.7 0.8 copy.15
  28.5 45.5 %all_to_all.10 = bf16[256,16,128]{2,1,0:T(8,128)(2,1)} all-to-all(bf16[256,16,128]{2,1,0:T(8,128)(2,1)S(1)} %bitcast.45), channel_id=1, replica_groups=mesh['wide'=32,'tm'=8] {'wide','tm'}, dimensions={0} | all-to-all | bytes 2097152 | tf_op jit(solution)/shard_map/all_to_all | solution.py:73
  73.9 3.5 %shard_map.66 = f32[8,2,2,32,256]{4,3,2,1,0:T(8,128)} custom-call(bf16[32,8,16,128]{3,2,1,0:T(8,128)(2,1)} %bitcast.46), custom_call_target="tpu_custom_call" | custom-call | flops 536870912 | bytes 2097152 | tf_op jit(solution)/shard_map/pallas_call | solution.py:167
  77.4 21.1 %all_to_all.11 = f32[8,2,2,32,256]{4,3,2,1,0:T(8,128)S(1)} all-to-all(f32[8,2,2,32,256]{4,3,2,1,0:T(8,128)} %shard_map.66), channel_id=1, replica_groups=mesh['wide'=32,'tm'=8] {'tm'}, dimensions={0} | all-to-all | bytes 2097152 | tf_op jit(solution)/shard_map/all_to_all | solution.py:77
  98.5 0.1 copy.16
  98.6 1.6 %copy.17 = f32[32,2,16,256]{3,2,1,0:T(8,128)} copy(f32[32,2,16,256]{3,0,2,1:T(8,128)S(1)} %bitcast.48) | data formatting | bytes 2097152 | tf_op jit(solution)/shard_map/reshape | solution.py:79
Async XLA Ops:
  2.0 10.1 %copy-start.4 = (f32[32,512]{1,0:T(8,128)S(1)}, f32[32,512]{1,0:T(8,128)}, u32[]{:S(2)}) copy-start(f32[32,512]{1,0:T(8,128)} %constant.10.clone) | copy-start | bytes 196612
  2.0 10.1 %copy-start.5 = (f32[32,512]{1,0:T(8,128)S(1)}, f32[32,512]{1,0:T(8,128)}, u32[]{:S(2)}) copy-start(f32[32,512]{1,0:T(8,128)} %constant.11.clone) | copy-start | bytes 196612
  2.0 10.1 %copy-start.6 = (f32[32,512]{1,0:T(8,128)S(1)}, f32[32,512]{1,0:T(8,128)}, u32[]{:S(2)}) copy-start(f32[32,512]{1,0:T(8,128)} %constant.12.clone) | copy-start | bytes 196612
  2.0 10.1 %copy-start.7 = (f32[32,512]{1,0:T(8,128)S(1)}, f32[32,512]{1,0:T(8,128)}, u32[]{:S(2)}) copy-start(f32[32,512]{1,0:T(8,128)} %constant.13.clone) | copy-start | bytes 196612
  2.0 16.7 %collective-permute-start = (bf16[15,8,1024]{2,1,0:T(8,128)(2,1)S(1)}, bf16[15,8,1024]{2,1,0:T(8,128)(2,1)S(1)}, u32[]{:S(2)}, u32[]{:S(2)}) collective-permute-start(bf16[15,8,1024]{2,1,0:T(8,128)(2,1)S(1)} %bitcast.49), channel_id=1, source_target_pairs={{0,1},{1,2},{2,3},{3,4},{4,5},{5,6},{6,7},{8,9},{9,10},{10,11},{11... | collective-permute-start | bytes 737288 | tf_op jit(solution)/shard_map/ppermute | solution.py:15
  12.8 1.4 %copy-start = (f32[49,8,1024]{2,1,0:T(8,128)S(1)}, f32[49,8,1024]{2,1,0:T(8,128)}, u32[]{:S(2)}) copy-start(f32[49,8,1024]{2,1,0:T(8,128)} %shard_map.65) | copy-start | bytes 4816900
  14.2 2.3 %copy-start.1 = (f32[1024,2,512]{2,0,1:T(8,128)}, f32[1024,2,512]{2,0,1:T(8,128)S(1)}, u32[]{:S(2)}) copy-start(f32[1024,2,512]{2,0,1:T(8,128)S(1)} %maximum_multiply_fusion) | copy-start | bytes 12582916
  18.8 0.7 copy-start.3
  22.4 2.6 %copy-start.2 = (f32[15,8,1024]{2,1,0:T(8,128)S(1)}, f32[15,8,1024]{2,1,0:T(8,128)}, u32[]{:S(2)}) copy-start(f32[15,8,1024]{2,1,0:T(8,128)} %shard_map.64) | copy-start | bytes 1474564

commit v6 on v4

--- a/solution.py
+++ b/solution.py
@@ -49,8 +49,7 @@
     per_group = channels // groups
 
     frames = voltages.reshape(local_inputs, spectra_dev, length).transpose(1, 0, 2)
-    frames = frames.astype(jnp.bfloat16)
-    previous = shifted(frames[spectra_dev - (lags - 1) :], "tm", 1)
+    previous = shifted(frames[spectra_dev - (lags - 1) :].astype(jnp.bfloat16), "tm", 1)
     taps_float = taps.astype(jnp.float32)
     table = dft_table(length, channels)
 
@@ -72,7 +71,8 @@
         ]
 
     later = channelize(frames, spectra_dev - (lags - 1))
-    head = channelize(jnp.concatenate([previous, frames[: 2 * (lags - 1)]], axis=0), lags - 1)
+    head_frames = [previous.astype(jnp.float32), frames[: 2 * (lags - 1)].astype(jnp.float32)]
+    head = channelize(jnp.concatenate(head_frames, axis=0), lags - 1)
     spectra = jnp.concatenate([head[0], later[0], head[1], later[1]], axis=-1)
     packed = spectra.reshape(groups, per_group * local_inputs, 2 * spectra_dev)
     got = lax.all_to_all(packed, ("wide", "tm"), 0, 0, tiled=True)

time: 90.8 us -> 91.6 us (level)
  other arithmetic: 8.67 us -> 9.7 us
    transpose x0 -> x1, other arithmetic: none -> 2.94 us  [shards(): voltages.reshape(local_inputs, spectra_dev, length).transpose(1, 0, 2)]
    convert_element_type x3 -> x2, other arithmetic: 2.58 us -> 0.14 us  [the longest x1 0.1 us: shards(): frames[:2 * (lags - 1)].astype(jnp.float32)]
where the time goes in v6:
time: 91.6 us; the launch traced here: 91.4 us
  blocking collectives  66.5 us (73%)
  other arithmetic  9.7 us (11%)
  matrix products  4.91 us (5%)
  starting transfers between devices  4.05 us (4%)
  Pallas kernels  3.5 us (4%)
  local copies, waits for them, and re-layouts  2.52 us (3%)
    all_to_all x1, blocking collectives, shards(): got = lax.all_to_all(packed, ('wide', 'tm'), 0, 0, tiled=True)  45.5 us
    all_to_all x1, blocking collectives, shards(): back = lax.all_to_all(grams, 'tm', 0, 0, tiled=True)  21.1 us
    mul x2, other arithmetic, channelize(): filtered = filtered * FIR_SCALE  5.14 us
    dot_general x4, matrix products, channelize(): jnp.einsum('sin,nk->kis', filtered, table[:, part, :], precision=lax.Prec...  4.91 us
    ppermute x1, starting transfers between devices, shifted(): return lax.ppermute(array, axis, pairs)  4.05 us
    pallas_call x1, Pallas kernels, channel_grams(): pl.pallas_call(lambda x_ref, o_ref: gram_kernel(scale, x_ref, o_ref), out...  3.5 us
    transpose x1, other arithmetic, shards(): voltages.reshape(local_inputs, spectra_dev, length).transpose(1, 0, 2)  2.94 us
  transfers between devices with their start and end apart: 1, of which 0 were waited for; matrix products, arithmetic and copies ran while one was open for 9% of the time, Pallas kernels for 0%

profile of v6, /device:TPU:1, one launch (start us, length us, event | category | flops | bytes accessed | tf_op | source)
XLA Modules:
  0.0 91.4 jit_solution(6200628691203912503)
XLA Ops:
  0.0 0.0 copy-start.4
  0.0 0.0 copy-start
  0.0 0.0 copy-start.1
  0.0 0.0 copy-start.2
  0.0 0.0 copy-start.3
  0.0 2.9 %copy_bitcast_fusion = (s32[64,8,1024]{2,0,1:T(8,128)S(1)}, f32[64,8,1024]{2,0,1:T(8,128)S(1)}) fusion(s32[8,64,1024]{2,0,1:T(8,128)} %bitcast.71), kind=kLoop, calls=%fused_computation.29 | loop fusion | flops 524288 | bytes 6291456 | tf_op jit(solution)/shard_map/transpose | solution.py:51
  3.0 0.1 slice_convert_fusion.1
  3.0 4.0 %collective-permute-start = (bf16[15,8,1024]{2,0,1:T(8,128)(2,1)S(1)}, bf16[15,8,1024]{2,0,1:T(8,128)(2,1)S(1)}, u32[]{:S(2)}, u32[]{:S(2)}) collective-permute-start(bf16[15,8,1024]{2,0,1:T(8,128)(2,1)S(1)} %slice_convert_fusion.1), channel_id=1, source_target_pairs={{0,1},{1,2},{2,3},{3,4},{4,5},{5,6},{6,7},{8,9},{9,10},{10,11},{11... | collective-permute-start | bytes 737288 | tf_op jit(solution)/shard_map/ppermute | solution.py:15
  7.1 0.0 copy-done.4
  7.2 0.0 copy-done
  7.2 0.0 copy-done.1
  7.2 0.0 copy-done.2
  7.2 0.0 copy-done.3
  7.2 0.6 multiply_subtract_fusion
  7.8 0.5 maximum_multiply_fusion
  8.4 3.7 %fusion.5 = f32[49,8,1024]{2,0,1:T(8,128)S(1)} fusion(f32[64,8,1024]{2,0,1:T(8,128)S(1)} %get-tuple-element.6, f32[1024]{0:T(1024)S(1)} %bitcast.74, f32[1024]{0:T(1024)S(1)} %bitcast.76, f32[1024]{0:T(1024)S(1)} %bitcast.78, f32[1024]{0:T(1024)S(1)} %bitcast.80, f32[1024]{0:T(1024)S(1)} %bitcast.82, f32[1024]{0:T(1024)S(1)} %bitcast.84, ...), kind=kLoop, calls=%fused_computation.38 | loop fusion | flops 12845056 | bytes 27361280 | tf_op jit(solution)/shard_map/mul | solution.py:61
  12.0 1.7 %fusion.23 = bf16[512,8,49]{0,2,1:T(8,128)(2,1)S(1)} fusion(f32[49,8,1024]{2,0,1:T(8,128)S(1)} %fusion.5, f32[1024,2,512]{2,0,1:T(8,128)S(1)} %maximum_multiply_fusion), kind=kOutput, calls=%fused_computation.71 | convolution fusion | flops 1233326080 | bytes 4333568 | tf_op jit(solution)/shard_map/sin,nk->kis/dot_general | solution.py:63
  13.7 1.7 %fusion.22 = bf16[512,8,49]{0,2,1:T(8,128)(2,1)S(1)} fusion(f32[49,8,1024]{2,0,1:T(8,128)S(1)} %fusion.5, f32[1024,2,512]{2,0,1:T(8,128)S(1)} %maximum_multiply_fusion), kind=kOutput, calls=%fused_computation.70 | convolution fusion | flops 1233326080 | bytes 4333568 | tf_op jit(solution)/shard_map/sin,nk->kis/dot_general | solution.py:63
  15.4 0.1 slice_convert_fusion
  15.5 0.0 collective-permute-done
  15.6 1.5 %fusion.33 = f32[15,8,1024]{2,0,1:T(8,128)S(1)} fusion(f32[30,8,1024]{2,0,1:T(8,128)S(1)} %slice_convert_fusion, f32[15,8,1024]{2,0,1:T(8,128)S(1)} %convert_element_type.39, f32[1024]{0:T(1024)S(1)} %bitcast.75, f32[1024]{0:T(1024)S(1)} %bitcast.77, f32[1024]{0:T(1024)S(1)} %bitcast.79, f32[1024]{0:T(1024)S(1)} %bitcast.81, f32[1024]{0:T(1024)S(1)} %bitcast.83, ...), kind=kLoop, calls=%fused_computation.83 | loop fusion | flops 5652480 | bytes 2654208 | tf_op jit(solution)/shard_map/mul | solution.py:61
  17.1 0.8 fusion.27
  17.9 0.8 fusion.26
  18.6 0.3 pad_maximum_fusion
  18.9 0.8 copy.9
  19.7 45.5 %all_to_all.10 = bf16[256,16,128]{2,1,0:T(8,128)(2,1)} all-to-all(bf16[256,16,128]{2,1,0:T(8,128)(2,1)S(1)} %bitcast.67), channel_id=1, replica_groups=mesh['wide'=32,'tm'=8] {'wide','tm'}, dimensions={0} | all-to-all | bytes 2097152 | tf_op jit(solution)/shard_map/all_to_all | solution.py:78
  65.1 3.5 %shard_map.64 = f32[8,2,2,32,256]{4,3,2,1,0:T(8,128)} custom-call(bf16[32,8,16,128]{3,2,1,0:T(8,128)(2,1)} %bitcast.68), custom_call_target="tpu_custom_call" | custom-call | flops 536870912 | bytes 2097152 | tf_op jit(solution)/shard_map/pallas_call | solution.py:118
  68.6 21.1 %all_to_all.11 = f32[8,2,2,32,256]{4,3,2,1,0:T(8,128)S(1)} all-to-all(f32[8,2,2,32,256]{4,3,2,1,0:T(8,128)} %shard_map.64), channel_id=1, replica_groups=mesh['wide'=32,'tm'=8] {'tm'}, dimensions={0} | all-to-all | bytes 2097152 | tf_op jit(solution)/shard_map/all_to_all | solution.py:82
  89.7 0.1 copy.10
  89.8 1.6 %copy.11 = f32[32,2,16,256]{3,2,1,0:T(8,128)} copy(f32[32,2,16,256]{3,0,2,1:T(8,128)S(1)} %bitcast.70) | data formatting | bytes 2097152 | tf_op jit(solution)/shard_map/reshape | solution.py:84
  (3 shorter events, 0.1 us)
Async XLA Ops:
  0.0 7.1 %copy-start.4 = (s32[16,1024]{1,0:T(8,128)S(1)}, s32[16,1024]{1,0:T(8,128)}, u32[]{:S(2)}) copy-start(s32[16,1024]{1,0:T(8,128)} %param.7) | copy-start | bytes 196612
  0.0 7.2 %copy-start = (f32[32,512]{1,0:T(8,128)S(1)}, f32[32,512]{1,0:T(8,128)}, u32[]{:S(2)}) copy-start(f32[32,512]{1,0:T(8,128)} %constant.16.clone) | copy-start | bytes 196612
  0.0 7.2 %copy-start.1 = (f32[32,512]{1,0:T(8,128)S(1)}, f32[32,512]{1,0:T(8,128)}, u32[]{:S(2)}) copy-start(f32[32,512]{1,0:T(8,128)} %constant.15.clone) | copy-start | bytes 196612
  0.0 7.2 %copy-start.2 = (f32[32,512]{1,0:T(8,128)S(1)}, f32[32,512]{1,0:T(8,128)}, u32[]{:S(2)}) copy-start(f32[32,512]{1,0:T(8,128)} %constant.14.clone) | copy-start | bytes 196612
  0.0 7.2 %copy-start.3 = (f32[32,512]{1,0:T(8,128)S(1)}, f32[32,512]{1,0:T(8,128)}, u32[]{:S(2)}) copy-start(f32[32,512]{1,0:T(8,128)} %constant.5.clone) | copy-start | bytes 196612
  3.0 12.5 %collective-permute-start = (bf16[15,8,1024]{2,0,1:T(8,128)(2,1)S(1)}, bf16[15,8,1024]{2,0,1:T(8,128)(2,1)S(1)}, u32[]{:S(2)}, u32[]{:S(2)}) collective-permute-start(bf16[15,8,1024]{2,0,1:T(8,128)(2,1)S(1)} %slice_convert_fusion.1), channel_id=1, source_target_pairs={{0,1},{1,2},{2,3},{3,4},{4,5},{5,6},{6,7},{8,9},{9,10},{10,11},{11... | collective-permute-start | bytes 737288 | tf_op jit(solution)/shard_map/ppermute | solution.py:15

commit v7 on v6

--- a/solution.py
+++ b/solution.py
@@ -61,7 +61,7 @@
         filtered = filtered * FIR_SCALE
         return [
             jnp.einsum(
-                "sin,nk->kis",
+                "sin,nk->sik",
                 filtered,
                 table[:, part, :],
                 precision=lax.Precision.HIGH,
@@ -73,7 +73,8 @@
     later = channelize(frames, spectra_dev - (lags - 1))
     head_frames = [previous.astype(jnp.float32), frames[: 2 * (lags - 1)].astype(jnp.float32)]
     head = channelize(jnp.concatenate(head_frames, axis=0), lags - 1)
-    spectra = jnp.concatenate([head[0], later[0], head[1], later[1]], axis=-1)
+    pieces = [head[0], later[0], head[1], later[1]]
+    spectra = jnp.concatenate([piece.transpose(2, 1, 0) for piece in pieces], axis=-1)
     packed = spectra.reshape(groups, per_group * local_inputs, 2 * spectra_dev)
     got = lax.all_to_all(packed, ("wide", "tm"), 0, 0, tiled=True)
     got = got.reshape(widen, ranks, per_group * local_inputs, 2 * spectra_dev)

time: 91.6 us -> 92.1 us (level)
    transpose x1 -> x0, other arithmetic: 2.94 us -> none  [shards(): voltages.reshape(local_inputs, spectra_dev, length).transpose(1, 0, 2)]
    convert_element_type x0 -> x1, other arithmetic: none -> 1.76 us  [channelize(): extended = extended.astype(jnp.float32)]
    convert_element_type x1, other arithmetic: 0.1 us -> 1.27 us  [shards(): frames[:2 * (lags - 1)].astype(jnp.float32)]
    mul x2, other arithmetic: 5.14 us -> 4.1 us  [channelize(): filtered = filtered * FIR_SCALE]
    another operation x1, other arithmetic: 0.06 us -> 1.06 us
  transfers between devices with their start and end apart: 1 -> 1, of which waited for: 0 -> 0; matrix products, arithmetic and copies ran while one was open for 9% -> 12% of each run, Pallas kernels for 0% -> 0%
where the time goes in v7:
time: 92.1 us; the launch traced here: 91.8 us
  blocking collectives  66.5 us (72%)
  other arithmetic  9.47 us (10%)
  matrix products  4.85 us (5%)
  starting transfers between devices  4.18 us (5%)
  Pallas kernels  3.5 us (4%)
  local copies, waits for them, and re-layouts  3.05 us (3%)
    all_to_all x1, blocking collectives, shards(): got = lax.all_to_all(packed, ('wide', 'tm'), 0, 0, tiled=True)  45.5 us
    all_to_all x1, blocking collectives, shards(): back = lax.all_to_all(grams, 'tm', 0, 0, tiled=True)  21.1 us
    dot_general x4, matrix products, channelize(): jnp.einsum('sin,nk->sik', filtered, table[:, part, :], precision=lax.Prec...  4.85 us
    ppermute x1, starting transfers between devices, shifted(): return lax.ppermute(array, axis, pairs)  4.18 us
    mul x2, other arithmetic, channelize(): filtered = filtered * FIR_SCALE  4.1 us
    pallas_call x1, Pallas kernels, channel_grams(): pl.pallas_call(lambda x_ref, o_ref: gram_kernel(scale, x_ref, o_ref), out...  3.5 us
  transfers between devices with their start and end apart: 1, of which 0 were waited for; matrix products, arithmetic and copies ran while one was open for 12% of the time, Pallas kernels for 0%

profile of v7, /device:TPU:1, one launch (start us, length us, event | category | flops | bytes accessed | tf_op | source)
XLA Modules:
  0.0 91.8 jit_solution(12404401650901926104)
XLA Ops:
  0.0 1.1 %slice_convert_fusion.1 = bf16[15,8,1024]{2,1,0:T(8,128)(2,1)S(1)} fusion(s32[64,8,1024]{2,1,0:T(8,128)} %bitcast.65), kind=kLoop, calls=%fused_computation.121 | loop fusion | flops 122880 | bytes 737280 | tf_op jit(solution)/shard_map/convert
  1.1 0.0 copy-start.4
  1.1 0.0 copy-start
  1.1 0.0 copy-start.1
  1.1 0.0 copy-start.2
  1.1 0.0 copy-start.3
  1.1 4.2 %collective-permute-start = (bf16[15,8,1024]{2,1,0:T(8,128)(2,1)S(1)}, bf16[15,8,1024]{2,1,0:T(8,128)(2,1)S(1)}, u32[]{:S(2)}, u32[]{:S(2)}) collective-permute-start(bf16[15,8,1024]{2,1,0:T(8,128)(2,1)S(1)} %slice_convert_fusion.1), channel_id=1, source_target_pairs={{0,1},{1,2},{2,3},{3,4},{4,5},{5,6},{6,7},{8,9},{9,10},{10,11},{11... | collective-permute-start | bytes 737288 | tf_op jit(solution)/shard_map/ppermute | solution.py:15
  5.3 1.8 %convert_element_type.46 = f32[64,8,1024]{2,1,0:T(8,128)S(1)} convert(s32[64,8,1024]{2,1,0:T(8,128)} %bitcast.66) | non-fusion elementwise | flops 524288 | bytes 4194304 | tf_op jit(solution)/shard_map/convert_element_type | solution.py:57
  7.1 0.0 copy-done.4
  7.2 0.0 copy-done
  7.2 0.0 copy-done.1
  7.2 0.0 copy-done.2
  7.2 0.0 copy-done.3
  7.2 0.6 multiply_subtract_fusion
  7.8 0.5 maximum_multiply_fusion
  8.3 3.6 %fusion.5 = f32[49,8,1024]{2,1,0:T(8,128)S(1)} fusion(f32[64,8,1024]{2,1,0:T(8,128)S(1)} %convert_element_type.46, f32[1024]{0:T(1024)S(1)} %bitcast.74, f32[1024]{0:T(1024)S(1)} %bitcast.76, f32[1024]{0:T(1024)S(1)} %bitcast.78, f32[1024]{0:T(1024)S(1)} %bitcast.80, f32[1024]{0:T(1024)S(1)} %bitcast.82, f32[1024]{0:T(1024)S(1)} %bitcast.84, ...), kind=kLoop, calls=%fused_computation.37 | loop fusion | flops 12845056 | bytes 27361280 | tf_op jit(solution)/shard_map/mul | solution.py:61
  11.9 1.6 %fusion.22 = bf16[512,8,49]{0,1,2:T(8,128)(2,1)S(1)} fusion(f32[49,8,1024]{2,1,0:T(8,128)S(1)} %fusion.5, f32[1024,2,512]{2,0,1:T(8,128)S(1)} %maximum_multiply_fusion), kind=kOutput, calls=%fused_computation.69 | convolution fusion | flops 1233326080 | bytes 4104192 | tf_op jit(solution)/shard_map/sin,nk->sik/dot_general | solution.py:63
  13.5 1.6 %fusion.23 = bf16[512,8,49]{0,1,2:T(8,128)(2,1)S(1)} fusion(f32[49,8,1024]{2,1,0:T(8,128)S(1)} %fusion.5, f32[1024,2,512]{2,0,1:T(8,128)S(1)} %maximum_multiply_fusion), kind=kOutput, calls=%fused_computation.70 | convolution fusion | flops 1233326080 | bytes 4104192 | tf_op jit(solution)/shard_map/sin,nk->sik/dot_general | solution.py:63
  15.1 1.3 %slice_convert_fusion = f32[30,8,1024]{2,1,0:T(8,128)S(1)} fusion(s32[64,8,1024]{2,1,0:T(8,128)} %bitcast.67), kind=kLoop, calls=%fused_computation.76 | loop fusion | flops 245760 | bytes 1966080 | tf_op jit(solution)/shard_map/convert_element_type | solution.py:74
  16.4 0.0 collective-permute-done
  16.5 0.5 fusion.33
  17.0 0.8 fusion.26
  17.8 0.8 fusion.27
  18.6 0.1 pad_maximum_fusion
  18.8 1.3 %copy.7 = bf16[512,8,128]{2,1,0:T(8,128)(2,1)S(1)} copy(bf16[512,8,128]{0,1,2:T(8,128)(2,1)S(1)} %pad_maximum_fusion) | data formatting | bytes 2097152 | tf_op jit(solution)/shard_map/concatenate | solution.py:77
  20.1 45.5 %all_to_all.10 = bf16[256,16,128]{2,1,0:T(8,128)(2,1)} all-to-all(bf16[256,16,128]{2,1,0:T(8,128)(2,1)S(1)} %bitcast.68), channel_id=1, replica_groups=mesh['wide'=32,'tm'=8] {'wide','tm'}, dimensions={0} | all-to-all | bytes 2097152 | tf_op jit(solution)/shard_map/all_to_all | solution.py:79
  65.5 3.5 %shard_map.64 = f32[8,2,2,32,256]{4,3,2,1,0:T(8,128)} custom-call(bf16[32,8,16,128]{3,2,1,0:T(8,128)(2,1)} %bitcast.69), custom_call_target="tpu_custom_call" | custom-call | flops 536870912 | bytes 2097152 | tf_op jit(solution)/shard_map/pallas_call | solution.py:119
  69.0 21.1 %all_to_all.11 = f32[8,2,2,32,256]{4,3,2,1,0:T(8,128)S(1)} all-to-all(f32[8,2,2,32,256]{4,3,2,1,0:T(8,128)} %shard_map.64), channel_id=1, replica_groups=mesh['wide'=32,'tm'=8] {'tm'}, dimensions={0} | all-to-all | bytes 2097152 | tf_op jit(solution)/shard_map/all_to_all | solution.py:83
  90.1 0.1 copy.8
  90.2 1.6 %copy.9 = f32[32,2,16,256]{3,2,1,0:T(8,128)} copy(f32[32,2,16,256]{3,0,2,1:T(8,128)S(1)} %bitcast.71) | data formatting | bytes 2097152 | tf_op jit(solution)/shard_map/reshape | solution.py:85
  (3 shorter events, 0.1 us)
Async XLA Ops:
  1.1 6.0 %copy-start.4 = (s32[16,1024]{1,0:T(8,128)S(1)}, s32[16,1024]{1,0:T(8,128)}, u32[]{:S(2)}) copy-start(s32[16,1024]{1,0:T(8,128)} %param.7) | copy-start | bytes 196612
  1.1 6.1 %copy-start = (f32[32,512]{1,0:T(8,128)S(1)}, f32[32,512]{1,0:T(8,128)}, u32[]{:S(2)}) copy-start(f32[32,512]{1,0:T(8,128)} %constant.14.clone) | copy-start | bytes 196612
  1.1 6.1 %copy-start.1 = (f32[32,512]{1,0:T(8,128)S(1)}, f32[32,512]{1,0:T(8,128)}, u32[]{:S(2)}) copy-start(f32[32,512]{1,0:T(8,128)} %constant.15.clone) | copy-start | bytes 196612
  1.1 6.1 %copy-start.2 = (f32[32,512]{1,0:T(8,128)S(1)}, f32[32,512]{1,0:T(8,128)}, u32[]{:S(2)}) copy-start(f32[32,512]{1,0:T(8,128)} %constant.16.clone) | copy-start | bytes 196612
  1.1 6.1 %copy-start.3 = (f32[32,512]{1,0:T(8,128)S(1)}, f32[32,512]{1,0:T(8,128)}, u32[]{:S(2)}) copy-start(f32[32,512]{1,0:T(8,128)} %constant.5.clone) | copy-start | bytes 196612
  1.1 15.3 %collective-permute-start = (bf16[15,8,1024]{2,1,0:T(8,128)(2,1)S(1)}, bf16[15,8,1024]{2,1,0:T(8,128)(2,1)S(1)}, u32[]{:S(2)}, u32[]{:S(2)}) collective-permute-start(bf16[15,8,1024]{2,1,0:T(8,128)(2,1)S(1)} %slice_convert_fusion.1), channel_id=1, source_target_pairs={{0,1},{1,2},{2,3},{3,4},{4,5},{5,6},{6,7},{8,9},{9,10},{10,11},{11... | collective-permute-start | bytes 737288 | tf_op jit(solution)/shard_map/ppermute | solution.py:15

commit v8 on v4

--- a/solution.py
+++ b/solution.py
@@ -15,26 +15,24 @@
     return lax.ppermute(array, axis, pairs)
 
 
-def dft_factors(length, channels, split):
-    hi = np.arange(length // split)[:, None] * split * np.arange(channels)[None, :] % length
-    lo = np.arange(split)[:, None] * np.arange(channels)[None, :] % length
-    ang_hi = 2.0 * np.pi / length * hi
-    ang_lo = 2.0 * np.pi / length * lo
-    return (
-        np.cos(ang_hi).astype(np.float32),
-        (-np.sin(ang_hi)).astype(np.float32),
-        np.cos(ang_lo).astype(np.float32),
-        (-np.sin(ang_lo)).astype(np.float32),
-    )
+def radix4_tables(length, channels):
+    quarter = length // 4
+    n0 = np.arange(quarter)[:, None]
+    scale = length ** (-0.5)
 
+    def parts(q):
+        k = 4 * np.arange(channels // 4)[None, :] + q
+        angle = 2.0 * np.pi / length * (n0 * k % length)
+        return np.cos(angle) * scale, np.sin(angle) * scale
 
-def dft_table(length, channels):
-    split = 32
-    ch, sh, cl, sl = (jnp.asarray(t) for t in dft_factors(length, channels, split))
-    re = ch[:, None, :] * cl[None, :, :] - sh[:, None, :] * sl[None, :, :]
-    im = ch[:, None, :] * sl[None, :, :] + sh[:, None, :] * cl[None, :, :]
-    table = jnp.stack([re, im], axis=2).reshape(length, 2, channels)
-    return table * length ** (-0.5)
+    c0, s0 = parts(0)
+    c1, s1 = parts(1)
+    c2, s2 = parts(2)
+    c3, s3 = parts(3)
+    real_q0 = np.concatenate([c0, -s0], axis=1)
+    real_q2 = np.concatenate([c2, -s2], axis=1)
+    mixed = np.block([[c1, -s1, c3, -s3], [-s1, -c1, s3, c3]])
+    return tuple(t.astype(np.float32) for t in (real_q0, real_q2, mixed))
 
 
 def shards(voltages, taps):
@@ -52,7 +50,8 @@
     frames = frames.astype(jnp.bfloat16)
     previous = shifted(frames[spectra_dev - (lags - 1) :], "tm", 1)
     taps_float = taps.astype(jnp.float32)
-    table = dft_table(length, channels)
+    tables = [jnp.asarray(t) for t in radix4_tables(length, channels)]
+    quarter = length // 4
 
     def channelize(extended, count):
         extended = extended.astype(jnp.float32)
@@ -60,16 +59,23 @@
         for lag in range(1, lags):
             filtered = filtered + taps_float[lag] * extended[lags - 1 - lag : lags - 1 - lag + count]
         filtered = filtered * FIR_SCALE
-        return [
+        x0, x1, x2, x3 = (filtered[..., m * quarter : (m + 1) * quarter] for m in range(4))
+        inputs = [x0 + x1 + x2 + x3, x0 - x1 + x2 - x3, jnp.concatenate([x0 - x2, x1 - x3], axis=-1)]
+        outs = [
             jnp.einsum(
-                "sin,nk->kis",
-                filtered,
-                table[:, part, :],
+                "sin,nm->sim",
+                lhs,
+                table,
                 precision=lax.Precision.HIGH,
                 preferred_element_type=jnp.float32,
             ).astype(jnp.bfloat16)
-            for part in range(2)
+            for lhs, table in zip(inputs, tables)
         ]
+        per_q = channels // 4
+        q0, q2, q13 = outs
+        real = jnp.stack([q0[..., :per_q], q13[..., :per_q], q2[..., :per_q], q13[..., 2 * per_q : 3 * per_q]], axis=2)
+        imag = jnp.stack([q0[..., per_q:], q13[..., per_q : 2 * per_q], q2[..., per_q:], q13[..., 3 * per_q :]], axis=2)
+        return [part.transpose(3, 2, 1, 0).reshape(channels, local_inputs, count) for part in (real, imag)]
 
     later = channelize(frames, spectra_dev - (lags - 1))
     head = channelize(jnp.concatenate([previous, frames[: 2 * (lags - 1)]], axis=0), lags - 1)

time: 90.8 us -> 101 us (1.11)
  local copies, waits for them, and re-layouts: 2.62 us -> 12.7 us
  matrix products: 4.93 us -> 2.46 us
  other arithmetic: 8.67 us -> 10.3 us
    transpose x0 -> x4, local copies, waits for them, and re-layouts: none -> 7.74 us  [channelize(): part.transpose(3, 2, 1, 0).reshape(channels, local_inputs, count)]
    dot_general x4 -> x6, matrix products: 4.93 us -> 2.46 us  [channelize(): jnp.einsum('sin,nm->sim', lhs, table, precision=lax.Precision.HIGH, prefe...]
    concatenate x1, other arithmetic: 0.28 us -> 2.56 us  [shards(): spectra = jnp.concatenate([head[0], later[0], head[1], later[1]], axis=-1)]
    unnamed x10 -> x68, local copies, waits for them, and re-layouts: 0.03 us -> 1.58 us
    convert_element_type x1 -> x2, other arithmetic: 0.21 us -> 1.43 us  [channelize(): extended = extended.astype(jnp.float32)]
    convert_element_type x2 -> x1, other arithmetic: 2.37 us -> 1.69 us  [shards(): frames = frames.astype(jnp.bfloat16)]
  transfers between devices with their start and end apart: 1 -> 1, of which waited for: 0 -> 0; matrix products, arithmetic and copies ran while one was open for 9% -> 10% of each run, Pallas kernels for 0% -> 0%
where the time goes in v8:
time: 101 us; the launch traced here: 100 us
  blocking collectives  65.8 us (65%)
  local copies, waits for them, and re-layouts  12.7 us (13%)
  other arithmetic  10.3 us (10%)
  starting transfers between devices  4.85 us (5%)
  Pallas kernels  3.5 us (3%)
  matrix products  2.46 us (2%)
    all_to_all x1, blocking collectives, shards(): got = lax.all_to_all(packed, ('wide', 'tm'), 0, 0, tiled=True)  44.8 us
    all_to_all x1, blocking collectives, shards(): back = lax.all_to_all(grams, 'tm', 0, 0, tiled=True)  21.1 us
    transpose x4, local copies, waits for them, and re-layouts, channelize(): part.transpose(3, 2, 1, 0).reshape(channels, local_inputs, count)  7.74 us
    ppermute x1, starting transfers between devices, shifted(): return lax.ppermute(array, axis, pairs)  4.85 us
    mul x2, other arithmetic, channelize(): filtered = filtered * FIR_SCALE  4.28 us
    pallas_call x1, Pallas kernels, channel_grams(): pl.pallas_call(lambda x_ref, o_ref: gram_kernel(scale, x_ref, o_ref), out...  3.5 us
    concatenate x1, other arithmetic, shards(): spectra = jnp.concatenate([head[0], later[0], head[1], later[1]], axis=-1)  2.56 us
    dot_general x6, matrix products, channelize(): jnp.einsum('sin,nm->sim', lhs, table, precision=lax.Precision.HIGH, prefe...  2.46 us
  transfers between devices with their start and end apart: 1, of which 0 were waited for; matrix products, arithmetic and copies ran while one was open for 10% of the time, Pallas kernels for 0%

profile of v8, /device:TPU:1, one launch (start us, length us, event | category | flops | bytes accessed | tf_op | source)
XLA Modules:
  0.0 100.3 jit_solution(1804058686353404711)
XLA Ops:
  0.0 1.7 %convert_element_type.37 = bf16[8,65536]{1,0:T(8,128)(2,1)S(1)} convert(s32[8,65536]{1,0:T(8,128)} %param.5) | non-fusion elementwise | flops 524288 | bytes 3145728 | tf_op jit(solution)/shard_map/convert_element_type | solution.py:50
  1.7 0.7 slice.313
  2.4 4.9 %collective-permute-start = (bf16[15,8,1024]{2,1,0:T(8,128)(2,1)}, bf16[15,8,1024]{2,1,0:T(8,128)(2,1)}, u32[]{:S(2)}, u32[]{:S(2)}) collective-permute-start(bf16[15,8,1024]{2,1,0:T(8,128)(2,1)} %slice.313), channel_id=1, source_target_pairs={{0,1},{1,2},{2,3},{3,4},{4,5},{5,6},{6,7},{8,9},{9,10},{10,11},{11... | collective-permute-start | bytes 737288 | tf_op jit(solution)/shard_map/ppermute | solution.py:15
  7.3 0.2 convert_element_type.44
  7.5 0.0 copy-done.5
  7.6 0.0 copy-start.6
  7.6 0.0 copy-start.8
  7.6 0.0 copy-start.10
  7.6 0.0 copy-start.12
  7.6 0.0 copy-start.14
  7.6 0.0 copy-start.16
  7.6 0.0 copy-start.18
  7.7 0.0 copy-start.20
  7.7 0.0 copy-start.22
  7.7 0.0 copy-start.24
  7.7 0.0 copy-start.26
  7.7 0.0 copy-start.28
  7.7 0.0 copy-start.30
  7.7 0.0 copy-start.32
  7.7 3.7 %fusion.1 = f32[49,8,1024]{2,1,0:T(8,128)S(1)} fusion(f32[64,8,1024]{2,1,0:T(8,128)S(1)} %convert_element_type.44, f32[1024]{0:T(1024)S(1)} %bitcast.87, f32[1024]{0:T(1024)S(1)} %bitcast.89, f32[1024]{0:T(1024)S(1)} %bitcast.91, f32[1024]{0:T(1024)S(1)} %bitcast.93, f32[1024]{0:T(1024)S(1)} %bitcast.95, f32[1024]{0:T(1024)S(1)} %bitcast.97, ...), kind=kLoop, calls=%fused_computation.2 | loop fusion | flops 12845056 | bytes 27361280 | tf_op jit(solution)/shard_map/mul | solution.py:61
  11.5 0.0 copy-done.6
  11.6 0.0 copy-start
  11.6 0.1 slice_subtract_fusion.1
  11.7 0.0 copy-start.3
  11.7 1.1 %copy-done = f32[512,512,1]{1,0,2:T(8,128)S(1)} copy-done((f32[512,512,1]{1,0,2:T(8,128)S(1)}, f32[512,512,1]{1,0,2:T(8,128)}, u32[]{:S(2)}) %copy-start) | copy-done | bytes 1048600
  12.8 0.8 convolution_convert_fusion
  13.7 0.1 slice_bitcast_fusion.6
  13.8 0.4 convolution_convert_fusion.1
  14.2 0.4 convolution_convert_fusion.2
  14.6 0.8 slice.314
  15.4 0.1 maximum_bitcast_fusion
  15.5 1.7 %copy.9 = bf16[128,4,8,49]{3,2,1,0:T(8,128)(2,1)S(1)} copy(bf16[128,4,8,49]{0,2,3,1:T(8,128)(2,1)S(1)} %get-tuple-element.42) | data formatting | bytes 802816 | tf_op jit(solution)/shard_map/transpose | solution.py:78
  17.3 1.7 %copy.7 = bf16[128,4,8,49]{3,2,1,0:T(8,128)(2,1)S(1)} copy(bf16[128,4,8,49]{0,2,3,1:T(8,128)(2,1)S(1)} %get-tuple-element.41) | data formatting | bytes 802816 | tf_op jit(solution)/shard_map/transpose | solution.py:78
  19.2 0.0 collective-permute-done
  19.2 1.2 %maximum_convert_fusion = f32[45,8,1024]{2,1,0:T(8,128)S(1)} fusion(bf16[30,8,1024]{2,1,0:T(8,128)(2,1)} %slice.314, bf16[15,8,1024]{2,1,0:T(8,128)(2,1)} %collective-permute-done), kind=kLoop, calls=%fused_computation.42 | loop fusion | flops 737280 | bytes 2211840 | tf_op jit(solution)/shard_map/convert_element_type | solution.py:57
  20.4 0.0 copy-done.7
  20.4 0.0 copy-done.9
  20.4 0.0 copy-done.11
  20.4 0.0 copy-done.13
  20.4 0.0 copy-done.15
  20.4 0.0 copy-done.17
  20.4 0.0 copy-done.19
  20.4 0.0 copy-done.21
  20.4 0.0 copy-done.23
  20.5 0.0 copy-done.25
  20.5 0.0 copy-done.27
  20.5 0.0 copy-done.29
  20.5 0.0 copy-done.31
  20.5 0.0 copy-done.33
  20.5 0.0 copy-start.4
  20.5 0.0 copy-start.2
  20.5 0.5 fusion.20
  21.1 0.3 copy-done.4
  21.5 0.2 convolution_convert_fusion.4
  21.7 0.2 convolution_convert_fusion.5
  21.9 0.4 convolution_convert_fusion.3
  22.5 1.7 %copy.8 = bf16[128,4,8,15]{3,2,1,0:T(8,128)(2,1)S(1)} copy(bf16[128,4,8,15]{0,2,3,1:T(8,128)(2,1)S(1)} %get-tuple-element.44) | data formatting | bytes 245760 | tf_op jit(solution)/shard_map/transpose | solution.py:78
  24.2 2.6 %copy.6 = bf16[128,4,8,15]{3,2,1,0:T(8,128)(2,1)} copy(bf16[128,4,8,15]{0,2,3,1:T(8,128)(2,1)S(1)} %get-tuple-element.43) | data formatting | bytes 245760 | tf_op jit(solution)/shard_map/transpose | solution.py:78
  26.7 2.6 %pad_maximum_fusion = bf16[256,16,128]{2,1,0:T(8,128)(2,1)S(1)} fusion(bf16[256,16,49]{2,1,0:T(8,128)(2,1)S(1)} %bitcast.78, bf16[256,16,15]{2,1,0:T(8,128)(2,1)S(1)} %bitcast.80, bf16[256,16,49]{2,1,0:T(8,128)(2,1)S(1)} %bitcast.79, bf16[256,16,15]{2,1,0:T(8,128)(2,1)} %bitcast.81), kind=kLoop, calls=%fused_computation.38 | loop fusion | flops 4194304 | bytes 2097152 | tf_op jit(solution)/shard_map/concatenate | solution.py:82
  29.3 44.8 %all_to_all.10 = bf16[256,16,128]{2,1,0:T(8,128)(2,1)} all-to-all(bf16[256,16,128]{2,1,0:T(8,128)(2,1)S(1)} %pad_maximum_fusion), channel_id=1, replica_groups=mesh['wide'=32,'tm'=8] {'wide','tm'}, dimensions={0} | all-to-all | bytes 2097152 | tf_op jit(solution)/shard_map/all_to_all | solution.py:84
  74.1 3.5 %shard_map.55 = f32[8,2,2,32,256]{4,3,2,1,0:T(8,128)} custom-call(bf16[32,8,16,128]{3,2,1,0:T(8,128)(2,1)} %bitcast.82), custom_call_target="tpu_custom_call" | custom-call | flops 536870912 | bytes 2097152 | tf_op jit(solution)/shard_map/pallas_call | solution.py:124
  77.6 21.1 %all_to_all.11 = f32[8,2,2,32,256]{4,3,2,1,0:T(8,128)S(1)} all-to-all(f32[8,2,2,32,256]{4,3,2,1,0:T(8,128)} %shard_map.55), channel_id=1, replica_groups=mesh['wide'=32,'tm'=8] {'tm'}, dimensions={0} | all-to-all | bytes 2097152 | tf_op jit(solution)/shard_map/all_to_all | solution.py:88
  98.6 0.1 copy.10
  98.8 1.6 %copy.11 = f32[32,2,16,256]{3,2,1,0:T(8,128)} copy(f32[32,2,16,256]{3,0,2,1:T(8,128)S(1)} %bitcast.84) | data formatting | bytes 2097152 | tf_op jit(solution)/shard_map/reshape | solution.py:90
  (41 shorter events, 0.3 us)
Async XLA Ops:
  2.4 5.1 %copy-start.5 = (s32[16,1024]{1,0:T(8,128)S(1)}, s32[16,1024]{1,0:T(8,128)}, u32[]{:S(2)}) copy-start(s32[16,1024]{1,0:T(8,128)} %param.6) | copy-start | bytes 196612
  2.4 16.8 %collective-permute-start = (bf16[15,8,1024]{2,1,0:T(8,128)(2,1)}, bf16[15,8,1024]{2,1,0:T(8,128)(2,1)}, u32[]{:S(2)}, u32[]{:S(2)}) collective-permute-start(bf16[15,8,1024]{2,1,0:T(8,128)(2,1)} %slice.313), channel_id=1, source_target_pairs={{0,1},{1,2},{2,3},{3,4},{4,5},{5,6},{6,7},{8,9},{9,10},{10,11},{11... | collective-permute-start | bytes 737288 | tf_op jit(solution)/shard_map/ppermute | solution.py:15
  7.6 3.9 %copy-start.6 = (f32[1,1024]{1,0:T(1,128)}, f32[1,1024]{1,0:T(1,128)S(1)}, u32[]{:S(2)}) copy-start(f32[1,1024]{1,0:T(1,128)S(1)} %get-tuple-element.23) | copy-start | bytes 12292
  7.6 3.9 %copy-start.8 = (f32[1,1024]{1,0:T(1,128)}, f32[1,1024]{1,0:T(1,128)S(1)}, u32[]{:S(2)}) copy-start(f32[1,1024]{1,0:T(1,128)S(1)} %get-tuple-element.24) | copy-start | bytes 12292
  7.6 3.9 %copy-start.10 = (f32[1,1024]{1,0:T(1,128)}, f32[1,1024]{1,0:T(1,128)S(1)}, u32[]{:S(2)}) copy-start(f32[1,1024]{1,0:T(1,128)S(1)} %get-tuple-element.25) | copy-start | bytes 12292
  7.6 3.9 %copy-start.12 = (f32[1,1024]{1,0:T(1,128)}, f32[1,1024]{1,0:T(1,128)S(1)}, u32[]{:S(2)}) copy-start(f32[1,1024]{1,0:T(1,128)S(1)} %get-tuple-element.26) | copy-start | bytes 12292
  7.6 3.9 %copy-start.14 = (f32[1,1024]{1,0:T(1,128)}, f32[1,1024]{1,0:T(1,128)S(1)}, u32[]{:S(2)}) copy-start(f32[1,1024]{1,0:T(1,128)S(1)} %get-tuple-element.27) | copy-start | bytes 12292
  7.6 3.9 %copy-start.16 = (f32[1,1024]{1,0:T(1,128)}, f32[1,1024]{1,0:T(1,128)S(1)}, u32[]{:S(2)}) copy-start(f32[1,1024]{1,0:T(1,128)S(1)} %get-tuple-element.28) | copy-start | bytes 12292
  7.6 3.9 %copy-start.18 = (f32[1,1024]{1,0:T(1,128)}, f32[1,1024]{1,0:T(1,128)S(1)}, u32[]{:S(2)}) copy-start(f32[1,1024]{1,0:T(1,128)S(1)} %get-tuple-element.29) | copy-start | bytes 12292
  7.7 3.9 %copy-start.20 = (f32[1,1024]{1,0:T(1,128)}, f32[1,1024]{1,0:T(1,128)S(1)}, u32[]{:S(2)}) copy-start(f32[1,1024]{1,0:T(1,128)S(1)} %get-tuple-element.30) | copy-start | bytes 12292
  7.7 3.9 %copy-start.22 = (f32[1,1024]{1,0:T(1,128)}, f32[1,1024]{1,0:T(1,128)S(1)}, u32[]{:S(2)}) copy-start(f32[1,1024]{1,0:T(1,128)S(1)} %get-tuple-element.31) | copy-start | bytes 12292
  7.7 3.9 %copy-start.24 = (f32[1,1024]{1,0:T(1,128)}, f32[1,1024]{1,0:T(1,128)S(1)}, u32[]{:S(2)}) copy-start(f32[1,1024]{1,0:T(1,128)S(1)} %get-tuple-element.32) | copy-start | bytes 12292
  7.7 3.9 %copy-start.26 = (f32[1,1024]{1,0:T(1,128)}, f32[1,1024]{1,0:T(1,128)S(1)}, u32[]{:S(2)}) copy-start(f32[1,1024]{1,0:T(1,128)S(1)} %get-tuple-element.33) | copy-start | bytes 12292
  7.7 3.9 %copy-start.28 = (f32[1,1024]{1,0:T(1,128)}, f32[1,1024]{1,0:T(1,128)S(1)}, u32[]{:S(2)}) copy-start(f32[1,1024]{1,0:T(1,128)S(1)} %get-tuple-element.34) | copy-start | bytes 12292
  7.7 3.9 %copy-start.30 = (f32[1,1024]{1,0:T(1,128)}, f32[1,1024]{1,0:T(1,128)S(1)}, u32[]{:S(2)}) copy-start(f32[1,1024]{1,0:T(1,128)S(1)} %get-tuple-element.35) | copy-start | bytes 12292
  7.7 3.9 %copy-start.32 = (f32[1,1024]{1,0:T(1,128)}, f32[1,1024]{1,0:T(1,128)S(1)}, u32[]{:S(2)}) copy-start(f32[1,1024]{1,0:T(1,128)S(1)} %get-tuple-element.36) | copy-start | bytes 12292
  11.6 1.2 %copy-start = (f32[512,512,1]{1,0,2:T(8,128)S(1)}, f32[512,512,1]{1,0,2:T(8,128)}, u32[]{:S(2)}) copy-start(f32[512,512,1]{1,0,2:T(8,128)} %constant.14) | copy-start | bytes 3145732
  11.7 2.0 %copy-start.3 = (f32[256,256,1]{1,0,2:T(8,128)S(1)}, f32[256,256,1]{1,0,2:T(8,128)}, u32[]{:S(2)}) copy-start(f32[256,256,1]{1,0,2:T(8,128)} %constant.15) | copy-start | bytes 786436
  12.8 1.3 %copy-start.1 = (f32[256,256,1]{1,0,2:T(8,128)S(1)}, f32[256,256,1]{1,0,2:T(8,128)}, u32[]{:S(2)}) copy-start(f32[256,256,1]{1,0,2:T(8,128)} %constant.13) | copy-start | bytes 786436
  19.0 1.3 %copy-start.7 = (f32[1,1024]{1,0:T(1,128)S(1)}, f32[1,1024]{1,0:T(1,128)}, u32[]{:S(2)}) copy-start(f32[1,1024]{1,0:T(1,128)} %copy-done.6) | copy-start | bytes 12292
  19.0 1.3 %copy-start.9 = (f32[1,1024]{1,0:T(1,128)S(1)}, f32[1,1024]{1,0:T(1,128)}, u32[]{:S(2)}) copy-start(f32[1,1024]{1,0:T(1,128)} %copy-done.8) | copy-start | bytes 12292
  19.0 1.3 %copy-start.11 = (f32[1,1024]{1,0:T(1,128)S(1)}, f32[1,1024]{1,0:T(1,128)}, u32[]{:S(2)}) copy-start(f32[1,1024]{1,0:T(1,128)} %copy-done.10) | copy-start | bytes 12292
  19.1 1.3 %copy-start.13 = (f32[1,1024]{1,0:T(1,128)S(1)}, f32[1,1024]{1,0:T(1,128)}, u32[]{:S(2)}) copy-start(f32[1,1024]{1,0:T(1,128)} %copy-done.12) | copy-start | bytes 12292
  19.1 1.3 %copy-start.15 = (f32[1,1024]{1,0:T(1,128)S(1)}, f32[1,1024]{1,0:T(1,128)}, u32[]{:S(2)}) copy-start(f32[1,1024]{1,0:T(1,128)} %copy-done.14) | copy-start | bytes 12292
  19.1 1.3 %copy-start.17 = (f32[1,1024]{1,0:T(1,128)S(1)}, f32[1,1024]{1,0:T(1,128)}, u32[]{:S(2)}) copy-start(f32[1,1024]{1,0:T(1,128)} %copy-done.16) | copy-start | bytes 12292
  19.1 1.3 %copy-start.19 = (f32[1,1024]{1,0:T(1,128)S(1)}, f32[1,1024]{1,0:T(1,128)}, u32[]{:S(2)}) copy-start(f32[1,1024]{1,0:T(1,128)} %copy-done.18) | copy-start | bytes 12292
  19.1 1.3 %copy-start.21 = (f32[1,1024]{1,0:T(1,128)S(1)}, f32[1,1024]{1,0:T(1,128)}, u32[]{:S(2)}) copy-start(f32[1,1024]{1,0:T(1,128)} %copy-done.20) | copy-start | bytes 12292
  19.1 1.3 %copy-start.23 = (f32[1,1024]{1,0:T(1,128)S(1)}, f32[1,1024]{1,0:T(1,128)}, u32[]{:S(2)}) copy-start(f32[1,1024]{1,0:T(1,128)} %copy-done.22) | copy-start | bytes 12292
  19.1 1.3 %copy-start.25 = (f32[1,1024]{1,0:T(1,128)S(1)}, f32[1,1024]{1,0:T(1,128)}, u32[]{:S(2)}) copy-start(f32[1,1024]{1,0:T(1,128)} %copy-done.24) | copy-start | bytes 12292
  19.1 1.3 %copy-start.27 = (f32[1,1024]{1,0:T(1,128)S(1)}, f32[1,1024]{1,0:T(1,128)}, u32[]{:S(2)}) copy-start(f32[1,1024]{1,0:T(1,128)} %copy-done.26) | copy-start | bytes 12292
  19.1 1.3 %copy-start.29 = (f32[1,1024]{1,0:T(1,128)S(1)}, f32[1,1024]{1,0:T(1,128)}, u32[]{:S(2)}) copy-start(f32[1,1024]{1,0:T(1,128)} %copy-done.28) | copy-start | bytes 12292
  19.1 1.3 %copy-start.31 = (f32[1,1024]{1,0:T(1,128)S(1)}, f32[1,1024]{1,0:T(1,128)}, u32[]{:S(2)}) copy-start(f32[1,1024]{1,0:T(1,128)} %copy-done.30) | copy-start | bytes 12292
  19.2 1.3 %copy-start.33 = (f32[1,1024]{1,0:T(1,128)S(1)}, f32[1,1024]{1,0:T(1,128)}, u32[]{:S(2)}) copy-start(f32[1,1024]{1,0:T(1,128)} %copy-done.32) | copy-start | bytes 12292
  20.5 1.0 copy-start.4
  20.5 1.2 %copy-start.2 = (f32[256,256,1]{1,0,2:T(8,128)S(1)}, f32[256,256,1]{1,0,2:T(8,128)}, u32[]{:S(2)}) copy-start(f32[256,256,1]{1,0,2:T(8,128)} %constant.13) | copy-start | bytes 786436

commit v9 on v8

--- a/solution.py
+++ b/solution.py
@@ -29,10 +29,10 @@
     c1, s1 = parts(1)
     c2, s2 = parts(2)
     c3, s3 = parts(3)
-    real_q0 = np.concatenate([c0, -s0], axis=1)
-    real_q2 = np.concatenate([c2, -s2], axis=1)
-    mixed = np.block([[c1, -s1, c3, -s3], [-s1, -c1, s3, c3]])
-    return tuple(t.astype(np.float32) for t in (real_q0, real_q2, mixed))
+    zero = np.zeros_like(c0)
+    even = np.block([[c0, -s0, zero, zero], [zero, zero, c2, -s2]])
+    odd = np.block([[c1, -s1, c3, -s3], [-s1, -c1, s3, c3]])
+    return tuple(t.astype(np.float32) for t in (even, odd))
 
 
 def shards(voltages, taps):
@@ -60,26 +60,28 @@
             filtered = filtered + taps_float[lag] * extended[lags - 1 - lag : lags - 1 - lag + count]
         filtered = filtered * FIR_SCALE
         x0, x1, x2, x3 = (filtered[..., m * quarter : (m + 1) * quarter] for m in range(4))
-        inputs = [x0 + x1 + x2 + x3, x0 - x1 + x2 - x3, jnp.concatenate([x0 - x2, x1 - x3], axis=-1)]
-        outs = [
+        inputs = [
+            jnp.concatenate([x0 + x1 + x2 + x3, x0 - x1 + x2 - x3], axis=-1),
+            jnp.concatenate([x0 - x2, x1 - x3], axis=-1),
+        ]
+        even, odd = (
             jnp.einsum(
                 "sin,nm->sim",
                 lhs,
                 table,
                 precision=lax.Precision.HIGH,
                 preferred_element_type=jnp.float32,
-            ).astype(jnp.bfloat16)
+            )
+            .astype(jnp.bfloat16)
+            .reshape(count, local_inputs, 2, 2, channels // 4)
             for lhs, table in zip(inputs, tables)
-        ]
-        per_q = channels // 4
-        q0, q2, q13 = outs
-        real = jnp.stack([q0[..., :per_q], q13[..., :per_q], q2[..., :per_q], q13[..., 2 * per_q : 3 * per_q]], axis=2)
-        imag = jnp.stack([q0[..., per_q:], q13[..., per_q : 2 * per_q], q2[..., per_q:], q13[..., 3 * per_q :]], axis=2)
-        return [part.transpose(3, 2, 1, 0).reshape(channels, local_inputs, count) for part in (real, imag)]
+        )
+        return jnp.stack([even[:, :, 0], odd[:, :, 0], even[:, :, 1], odd[:, :, 1]], axis=2)
 
     later = channelize(frames, spectra_dev - (lags - 1))
     head = channelize(jnp.concatenate([previous, frames[: 2 * (lags - 1)]], axis=0), lags - 1)
-    spectra = jnp.concatenate([head[0], later[0], head[1], later[1]], axis=-1)
+    spectra = jnp.concatenate([head, later], axis=0).transpose(4, 2, 1, 3, 0)
+    spectra = spectra.reshape(channels, local_inputs, 2 * spectra_dev)
     packed = spectra.reshape(groups, per_group * local_inputs, 2 * spectra_dev)
     got = lax.all_to_all(packed, ("wide", "tm"), 0, 0, tiled=True)
     got = got.reshape(widen, ranks, per_group * local_inputs, 2 * spectra_dev)

time: 101 us -> 90.4 us (0.90)
  local copies, waits for them, and re-layouts: 12.7 us -> 6.8 us
  other arithmetic: 10.3 us -> 6.48 us
    transpose x4 -> x1, local copies, waits for them, and re-layouts: 7.74 us -> 2.22 us  [shards(): spectra = jnp.concatenate([head, later], axis=0).transpose(4, 2, 1, 3, 0)]
    concatenate x1 -> x0, other arithmetic: 2.56 us -> none  [shards(): spectra = jnp.concatenate([head[0], later[0], head[1], later[1]], axis=-1)]
    convert_element_type x2, other arithmetic: 1.43 us -> 0.34 us  [channelize(): extended = extended.astype(jnp.float32)]
    dot_general x6 -> x4, matrix products: 2.46 us -> 2.51 us  [channelize(): jnp.einsum('sin,nm->sim', lhs, table, precision=lax.Precision.HIGH, prefe...]
  transfers between devices with their start and end apart: 1 -> 1, of which waited for: 0 -> 0; matrix products, arithmetic and copies ran while one was open for 10% -> 7% of each run, Pallas kernels for 0% -> 0%
where the time goes in v9:
time: 90.4 us; the launch traced here: 90 us
  blocking collectives  66.5 us (74%)
  local copies, waits for them, and re-layouts  6.8 us (8%)
  other arithmetic  6.48 us (7%)
  starting transfers between devices  4.04 us (4%)
  Pallas kernels  3.5 us (4%)
  matrix products  2.51 us (3%)
    all_to_all x1, blocking collectives, shards(): got = lax.all_to_all(packed, ('wide', 'tm'), 0, 0, tiled=True)  45.5 us
    all_to_all x1, blocking collectives, shards(): back = lax.all_to_all(grams, 'tm', 0, 0, tiled=True)  21.1 us
    mul x2, other arithmetic, channelize(): filtered = filtered * FIR_SCALE  4.11 us
    ppermute x1, starting transfers between devices, shifted(): return lax.ppermute(array, axis, pairs)  4.04 us
    pallas_call x1, Pallas kernels, channel_grams(): pl.pallas_call(lambda x_ref, o_ref: gram_kernel(scale, x_ref, o_ref), out...  3.5 us
    dot_general x4, matrix products, channelize(): jnp.einsum('sin,nm->sim', lhs, table, precision=lax.Precision.HIGH, prefe...  2.51 us
    transpose x1, local copies, waits for them, and re-layouts, shards(): spectra = jnp.concatenate([head, later], axis=0).transpose(4, 2, 1, 3, 0)  2.22 us
  transfers between devices with their start and end apart: 1, of which 0 were waited for; matrix products, arithmetic and copies ran while one was open for 7% of the time, Pallas kernels for 0%

profile of v9, /device:TPU:1, one launch (start us, length us, event | category | flops | bytes accessed | tf_op | source)
XLA Modules:
  0.0 90.0 jit_solution(16445209773273773448)
XLA Ops:
  0.0 1.7 %convert_element_type.31 = bf16[8,65536]{1,0:T(8,128)(2,1)S(1)} convert(s32[8,65536]{1,0:T(8,128)} %param.4) | non-fusion elementwise | flops 524288 | bytes 3145728 | tf_op jit(solution)/shard_map/convert_element_type | solution.py:50
  1.7 4.0 %collective-permute-start = (bf16[15,8,1024]{2,1,0:T(8,128)(2,1)S(1)}, bf16[15,8,1024]{2,1,0:T(8,128)(2,1)S(1)}, u32[]{:S(2)}, u32[]{:S(2)}) collective-permute-start(bf16[15,8,1024]{2,1,0:T(8,128)(2,1)S(1)} %slice.281), channel_id=1, source_target_pairs={{0,1},{1,2},{2,3},{3,4},{4,5},{5,6},{6,7},{8,9},{9,10},{10,11},{11... | collective-permute-start | bytes 737288 | tf_op jit(solution)/shard_map/ppermute | solution.py:15
  5.8 0.0 copy-start.2
  5.8 0.2 convert_element_type.37
  6.1 0.6 copy-done.2
  6.7 3.6 %fusion.1 = f32[49,8,1024]{2,1,0:T(8,128)S(1)} fusion(f32[64,8,1024]{2,1,0:T(8,128)S(1)} %convert_element_type.37, f32[1024]{0:T(1024)S(1)} %bitcast.46, f32[1024]{0:T(1024)S(1)} %bitcast.48, f32[1024]{0:T(1024)S(1)} %bitcast.50, f32[1024]{0:T(1024)S(1)} %bitcast.52, f32[1024]{0:T(1024)S(1)} %bitcast.54, f32[1024]{0:T(1024)S(1)} %bitcast.56, ...), kind=kLoop, calls=%fused_computation.2 | loop fusion | flops 12845056 | bytes 27361280 | tf_op jit(solution)/shard_map/mul | solution.py:61
  10.3 0.0 copy-start.1
  10.3 0.2 add_add_fusion
  10.5 0.0 copy-start
  10.5 1.0 %copy-done.1 = f32[512,512,1]{1,0,2:T(8,128)S(1)} copy-done((f32[512,512,1]{1,0,2:T(8,128)S(1)}, f32[512,512,1]{1,0,2:T(8,128)}, u32[]{:S(2)}) %copy-start.1) | copy-done | bytes 1048600
  11.5 0.8 convolution_convert_fusion.1
  12.4 0.0 copy-done
  12.4 0.8 convolution_convert_fusion
  13.2 0.1 fusion.48
  13.4 0.0 collective-permute-done
  13.4 0.1 maximum_convert_fusion
  13.5 0.5 fusion.23
  14.1 0.4 convolution_convert_fusion.3
  14.5 0.4 convolution_convert_fusion.2
  15.0 0.1 maximum_bitcast_fusion
  15.1 2.2 %copy.16 = bf16[128,4,8,2,64]{4,3,2,1,0:T(2,128)(2,1)S(1)} copy(bf16[128,4,8,2,64]{0,2,3,1,4:T(8,128)(2,1)S(1)} %maximum_bitcast_fusion) | data formatting | bytes 2097152 | tf_op jit(solution)/shard_map/transpose | solution.py:83
  17.3 1.0 %reshape_reshape.3 = bf16[256,16,128]{2,1,0:T(8,128)(2,1)S(1)} reshape(bf16[128,4,8,2,64]{4,3,2,1,0:T(2,128)(2,1)S(1)} %copy.16) | data formatting | bytes 2097152 | tf_op jit(solution)/shard_map/reshape;reshape | solution.py:85
  18.3 45.5 %all_to_all.10 = bf16[256,16,128]{2,1,0:T(8,128)(2,1)} all-to-all(bf16[256,16,128]{2,1,0:T(8,128)(2,1)S(1)} %reshape_reshape.3), channel_id=1, replica_groups=mesh['wide'=32,'tm'=8] {'wide','tm'}, dimensions={0} | all-to-all | bytes 2097152 | tf_op jit(solution)/shard_map/all_to_all | solution.py:86
  63.8 3.5 %shard_map.46 = f32[8,2,2,32,256]{4,3,2,1,0:T(8,128)} custom-call(bf16[32,8,16,128]{3,2,1,0:T(8,128)(2,1)} %bitcast.37), custom_call_target="tpu_custom_call" | custom-call | flops 536870912 | bytes 2097152 | tf_op jit(solution)/shard_map/pallas_call | solution.py:126
  67.3 21.1 %all_to_all.11 = f32[8,2,2,32,256]{4,3,2,1,0:T(8,128)S(1)} all-to-all(f32[8,2,2,32,256]{4,3,2,1,0:T(8,128)} %shard_map.46), channel_id=1, replica_groups=mesh['wide'=32,'tm'=8] {'tm'}, dimensions={0} | all-to-all | bytes 2097152 | tf_op jit(solution)/shard_map/all_to_all | solution.py:90
  88.3 0.1 copy.17
  88.5 1.6 %copy.18 = f32[32,2,16,256]{3,2,1,0:T(8,128)} copy(f32[32,2,16,256]{3,0,2,1:T(8,128)S(1)} %bitcast.39) | data formatting | bytes 2097152 | tf_op jit(solution)/shard_map/reshape | solution.py:92
  (6 shorter events, 0.2 us)
Async XLA Ops:
  1.7 11.6 %collective-permute-start = (bf16[15,8,1024]{2,1,0:T(8,128)(2,1)S(1)}, bf16[15,8,1024]{2,1,0:T(8,128)(2,1)S(1)}, u32[]{:S(2)}, u32[]{:S(2)}) collective-permute-start(bf16[15,8,1024]{2,1,0:T(8,128)(2,1)S(1)} %slice.281), channel_id=1, source_target_pairs={{0,1},{1,2},{2,3},{3,4},{4,5},{5,6},{6,7},{8,9},{9,10},{10,11},{11... | collective-permute-start | bytes 737288 | tf_op jit(solution)/shard_map/ppermute | solution.py:15
  5.8 0.8 copy-start.2
  10.3 1.2 %copy-start.1 = (f32[512,512,1]{1,0,2:T(8,128)S(1)}, f32[512,512,1]{1,0,2:T(8,128)}, u32[]{:S(2)}) copy-start(f32[512,512,1]{1,0,2:T(8,128)} %constant.10) | copy-start | bytes 3145732
  10.5 1.9 %copy-start = (f32[512,512,1]{1,0,2:T(8,128)S(1)}, f32[512,512,1]{1,0,2:T(8,128)}, u32[]{:S(2)}) copy-start(f32[512,512,1]{1,0,2:T(8,128)} %constant.11) | copy-start | bytes 3145732

commit v10 on v9

--- a/solution.py
+++ b/solution.py
@@ -92,30 +92,35 @@
     return back.transpose(3, 1, 0, 2, 4).reshape(rows, 2, ranks * per_group, back.shape[4])
 
 
-def gram_kernel(scale, x_ref, o_ref):
-    widen, ranks, stacked, depth = x_ref.shape
-    groups = o_ref.shape[2]
+def gram_kernel(scale, x_ref, o_ref, acc_ref):
+    t = pl.program_id(0)
+    widen, _, stacked, depth = x_ref.shape
+    ranks, _, groups, rows, inputs = o_ref.shape
     local_inputs = stacked // groups
-    inputs = widen * local_inputs
     half = depth // 2
     lane = lax.broadcasted_iota(jnp.int32, (inputs, depth), 1)
     sign = jnp.where(lane < half, -1.0, 1.0).astype(jnp.float32)
-    rows = inputs // ranks
-    accs = [jnp.zeros((inputs, 2 * inputs), jnp.float32) for _ in range(groups)]
-    for t in range(ranks):
-        block = x_ref[:, t, :, :].astype(jnp.float32)
+
+    @pl.when(t == 0)
+    def _():
+        acc_ref[...] = jnp.zeros_like(acc_ref)
+
+    block = x_ref[:, 0, :, :].astype(jnp.float32)
+    for c in range(groups):
+        x = block[:, c * local_inputs : (c + 1) * local_inputs, :].reshape(inputs, depth)
+        rot = pltpu.roll(x, half, 1) * sign
+        y = jnp.concatenate([x, rot], axis=0).astype(jnp.bfloat16)
+        acc_ref[c] += lax.dot_general(
+            x.astype(jnp.bfloat16), y, (((1,), (1,)), ((), ())),
+            preferred_element_type=jnp.float32,
+        )
+
+    @pl.when(t == ranks - 1)
+    def _():
         for c in range(groups):
-            x = block[:, c * local_inputs : (c + 1) * local_inputs, :].reshape(inputs, depth)
-            rot = pltpu.roll(x, half, 1) * sign
-            y = jnp.concatenate([x, rot], axis=0).astype(jnp.bfloat16)
-            accs[c] = accs[c] + lax.dot_general(
-                x.astype(jnp.bfloat16), y, (((1,), (1,)), ((), ())),
-                preferred_element_type=jnp.float32,
-            )
-    for c in range(groups):
-        acc = accs[c] * scale
-        o_ref[:, 0, c, :, :] = acc[:, :inputs].reshape(ranks, rows, inputs)
-        o_ref[:, 1, c, :, :] = acc[:, inputs:].reshape(ranks, rows, inputs)
+            acc = acc_ref[c] * scale
+            o_ref[:, 0, c, :, :] = acc[:, :inputs].reshape(ranks, rows, inputs)
+            o_ref[:, 1, c, :, :] = acc[:, inputs:].reshape(ranks, rows, inputs)
 
 
 def channel_grams(got, scale, groups):
@@ -124,10 +129,13 @@
     rows = inputs // ranks
     flops = 2 * groups * ranks * inputs * 2 * inputs * depth
     return pl.pallas_call(
-        lambda x_ref, o_ref: gram_kernel(scale, x_ref, o_ref),
+        lambda x_ref, o_ref, acc_ref: gram_kernel(scale, x_ref, o_ref, acc_ref),
         out_shape=jax.ShapeDtypeStruct((ranks, 2, groups, rows, inputs), jnp.float32),
-        in_specs=[pl.BlockSpec(memory_space=pltpu.VMEM)],
-        out_specs=pl.BlockSpec(memory_space=pltpu.VMEM),
+        grid=(ranks,),
+        in_specs=[pl.BlockSpec((widen, 1, stacked, depth), lambda t: (0, t, 0, 0))],
+        out_specs=pl.BlockSpec((ranks, 2, groups, rows, inputs), lambda t: (0, 0, 0, 0, 0)),
+        scratch_shapes=[pltpu.VMEM((groups, inputs, 2 * inputs), jnp.float32)],
+        compiler_params=pltpu.CompilerParams(dimension_semantics=("arbitrary",)),
         cost_estimate=pl.CostEstimate(
             flops=flops, transcendentals=0, bytes_accessed=got.size * 2 + 2 * groups * inputs * inputs * 4
         ),

time: 90.4 us -> 93.6 us (1.035)
  Pallas kernels: 3.5 us -> 6.65 us
    pallas_call x1, Pallas kernels: 3.5 us -> 6.65 us  [channel_grams(): pl.pallas_call(lambda x_ref, o_ref, acc_ref: gram_kernel(scale, x_ref, o_...]
  transfers between devices with their start and end apart: 1 -> 1, of which waited for: 0 -> 0; matrix products, arithmetic and copies ran while one was open for 7% -> 6% of each run, Pallas kernels for 0% -> 0%
where the time goes in v10:
time: 93.6 us; the launch traced here: 93.2 us
  blocking collectives  66.5 us (71%)
  local copies, waits for them, and re-layouts  6.8 us (7%)
  Pallas kernels  6.65 us (7%)
  other arithmetic  6.48 us (7%)
  starting transfers between devices  4.04 us (4%)
  matrix products  2.51 us (3%)
    all_to_all x1, blocking collectives, shards(): got = lax.all_to_all(packed, ('wide', 'tm'), 0, 0, tiled=True)  45.5 us
    all_to_all x1, blocking collectives, shards(): back = lax.all_to_all(grams, 'tm', 0, 0, tiled=True)  21.1 us
    pallas_call x1, Pallas kernels, channel_grams(): pl.pallas_call(lambda x_ref, o_ref, acc_ref: gram_kernel(scale, x_ref, o_...  6.65 us
    mul x2, other arithmetic, channelize(): filtered = filtered * FIR_SCALE  4.11 us
    ppermute x1, starting transfers between devices, shifted(): return lax.ppermute(array, axis, pairs)  4.04 us
    dot_general x4, matrix products, channelize(): jnp.einsum('sin,nm->sim', lhs, table, precision=lax.Precision.HIGH, prefe...  2.51 us
    transpose x1, local copies, waits for them, and re-layouts, shards(): spectra = jnp.concatenate([head, later], axis=0).transpose(4, 2, 1, 3, 0)  2.22 us
  transfers between devices with their start and end apart: 1, of which 0 were waited for; matrix products, arithmetic and copies ran while one was open for 6% of the time, Pallas kernels for 0%

profile of v10, /device:TPU:1, one launch (start us, length us, event | category | flops | bytes accessed | tf_op | source)
XLA Modules:
  0.0 93.2 jit_solution(12286258565483271975)
XLA Ops:
  0.0 1.7 %convert_element_type.31 = bf16[8,65536]{1,0:T(8,128)(2,1)S(1)} convert(s32[8,65536]{1,0:T(8,128)} %param.4) | non-fusion elementwise | flops 524288 | bytes 3145728 | tf_op jit(solution)/shard_map/convert_element_type | solution.py:50
  1.7 4.0 %collective-permute-start = (bf16[15,8,1024]{2,1,0:T(8,128)(2,1)S(1)}, bf16[15,8,1024]{2,1,0:T(8,128)(2,1)S(1)}, u32[]{:S(2)}, u32[]{:S(2)}) collective-permute-start(bf16[15,8,1024]{2,1,0:T(8,128)(2,1)S(1)} %slice.281), channel_id=1, source_target_pairs={{0,1},{1,2},{2,3},{3,4},{4,5},{5,6},{6,7},{8,9},{9,10},{10,11},{11... | collective-permute-start | bytes 737288 | tf_op jit(solution)/shard_map/ppermute | solution.py:15
  5.8 0.0 copy-start.2
  5.8 0.2 convert_element_type.37
  6.1 0.6 copy-done.2
  6.7 3.6 %fusion.1 = f32[49,8,1024]{2,1,0:T(8,128)S(1)} fusion(f32[64,8,1024]{2,1,0:T(8,128)S(1)} %convert_element_type.37, f32[1024]{0:T(1024)S(1)} %bitcast.46, f32[1024]{0:T(1024)S(1)} %bitcast.48, f32[1024]{0:T(1024)S(1)} %bitcast.50, f32[1024]{0:T(1024)S(1)} %bitcast.52, f32[1024]{0:T(1024)S(1)} %bitcast.54, f32[1024]{0:T(1024)S(1)} %bitcast.56, ...), kind=kLoop, calls=%fused_computation.2 | loop fusion | flops 12845056 | bytes 27361280 | tf_op jit(solution)/shard_map/mul | solution.py:61
  10.3 0.0 copy-start.1
  10.3 0.2 add_add_fusion
  10.5 0.0 copy-start
  10.5 1.0 %copy-done.1 = f32[512,512,1]{1,0,2:T(8,128)S(1)} copy-done((f32[512,512,1]{1,0,2:T(8,128)S(1)}, f32[512,512,1]{1,0,2:T(8,128)}, u32[]{:S(2)}) %copy-start.1) | copy-done | bytes 1048600
  11.5 0.8 convolution_convert_fusion.1
  12.4 0.0 copy-done
  12.4 0.8 convolution_convert_fusion
  13.2 0.1 fusion.48
  13.4 0.0 collective-permute-done
  13.4 0.1 maximum_convert_fusion
  13.5 0.5 fusion.23
  14.1 0.4 convolution_convert_fusion.3
  14.5 0.4 convolution_convert_fusion.2
  15.0 0.1 maximum_bitcast_fusion
  15.1 2.2 %copy.16 = bf16[128,4,8,2,64]{4,3,2,1,0:T(2,128)(2,1)S(1)} copy(bf16[128,4,8,2,64]{0,2,3,1,4:T(8,128)(2,1)S(1)} %maximum_bitcast_fusion) | data formatting | bytes 2097152 | tf_op jit(solution)/shard_map/transpose | solution.py:83
  17.3 1.0 %reshape_reshape.3 = bf16[256,16,128]{2,1,0:T(8,128)(2,1)S(1)} reshape(bf16[128,4,8,2,64]{4,3,2,1,0:T(2,128)(2,1)S(1)} %copy.16) | data formatting | bytes 2097152 | tf_op jit(solution)/shard_map/reshape;reshape | solution.py:85
  18.3 45.5 %all_to_all.10 = bf16[256,16,128]{2,1,0:T(8,128)(2,1)} all-to-all(bf16[256,16,128]{2,1,0:T(8,128)(2,1)S(1)} %reshape_reshape.3), channel_id=1, replica_groups=mesh['wide'=32,'tm'=8] {'wide','tm'}, dimensions={0} | all-to-all | bytes 2097152 | tf_op jit(solution)/shard_map/all_to_all | solution.py:86
  63.8 6.6 %shard_map.46 = f32[8,2,2,32,256]{4,3,2,1,0:T(8,128)} custom-call(bf16[32,8,16,128]{3,2,1,0:T(8,128)(2,1)} %bitcast.37), custom_call_target="tpu_custom_call" | custom-call | flops 536870912 | bytes 2097152 | tf_op jit(solution)/shard_map/pallas_call | solution.py:131
  70.4 21.1 %all_to_all.11 = f32[8,2,2,32,256]{4,3,2,1,0:T(8,128)S(1)} all-to-all(f32[8,2,2,32,256]{4,3,2,1,0:T(8,128)} %shard_map.46), channel_id=1, replica_groups=mesh['wide'=32,'tm'=8] {'tm'}, dimensions={0} | all-to-all | bytes 2097152 | tf_op jit(solution)/shard_map/all_to_all | solution.py:90
  91.5 0.1 copy.17
  91.6 1.6 %copy.18 = f32[32,2,16,256]{3,2,1,0:T(8,128)} copy(f32[32,2,16,256]{3,0,2,1:T(8,128)S(1)} %bitcast.39) | data formatting | bytes 2097152 | tf_op jit(solution)/shard_map/reshape | solution.py:92
  (6 shorter events, 0.2 us)
Async XLA Ops:
  1.7 11.6 %collective-permute-start = (bf16[15,8,1024]{2,1,0:T(8,128)(2,1)S(1)}, bf16[15,8,1024]{2,1,0:T(8,128)(2,1)S(1)}, u32[]{:S(2)}, u32[]{:S(2)}) collective-permute-start(bf16[15,8,1024]{2,1,0:T(8,128)(2,1)S(1)} %slice.281), channel_id=1, source_target_pairs={{0,1},{1,2},{2,3},{3,4},{4,5},{5,6},{6,7},{8,9},{9,10},{10,11},{11... | collective-permute-start | bytes 737288 | tf_op jit(solution)/shard_map/ppermute | solution.py:15
  5.8 0.8 copy-start.2
  10.3 1.2 %copy-start.1 = (f32[512,512,1]{1,0,2:T(8,128)S(1)}, f32[512,512,1]{1,0,2:T(8,128)}, u32[]{:S(2)}) copy-start(f32[512,512,1]{1,0,2:T(8,128)} %constant.10) | copy-start | bytes 3145732
  10.5 1.9 %copy-start = (f32[512,512,1]{1,0,2:T(8,128)S(1)}, f32[512,512,1]{1,0,2:T(8,128)}, u32[]{:S(2)}) copy-start(f32[512,512,1]{1,0,2:T(8,128)} %constant.11) | copy-start | bytes 3145732

commit v11 on v9

--- a/solution.py
+++ b/solution.py
@@ -15,24 +15,30 @@
     return lax.ppermute(array, axis, pairs)
 
 
+def radix4_factors(length, channels, split):
+    quarter = length // 4
+    k = (4 * np.arange(channels // 4)[None, :] + np.arange(4)[:, None]).reshape(1, channels)
+    hi = np.arange(quarter // split)[:, None] * split * k % length
+    lo = np.arange(split)[:, None] * k % length
+    angles = [2.0 * np.pi / length * hi, 2.0 * np.pi / length * lo]
+    return [f(angle).astype(np.float32) for angle in angles for f in (np.cos, np.sin)]
+
+
 def radix4_tables(length, channels):
+    split = 16
+    ch, sh, cl, sl = (jnp.asarray(t) for t in radix4_factors(length, channels, split))
     quarter = length // 4
-    n0 = np.arange(quarter)[:, None]
-    scale = length ** (-0.5)
-
-    def parts(q):
-        k = 4 * np.arange(channels // 4)[None, :] + q
-        angle = 2.0 * np.pi / length * (n0 * k % length)
-        return np.cos(angle) * scale, np.sin(angle) * scale
-
-    c0, s0 = parts(0)
-    c1, s1 = parts(1)
-    c2, s2 = parts(2)
-    c3, s3 = parts(3)
-    zero = np.zeros_like(c0)
-    even = np.block([[c0, -s0, zero, zero], [zero, zero, c2, -s2]])
-    odd = np.block([[c1, -s1, c3, -s3], [-s1, -c1, s3, c3]])
-    return tuple(t.astype(np.float32) for t in (even, odd))
+    cos = (ch[:, None, :] * cl[None, :, :] - sh[:, None, :] * sl[None, :, :]).reshape(quarter, channels)
+    sin = (sh[:, None, :] * cl[None, :, :] + ch[:, None, :] * sl[None, :, :]).reshape(quarter, channels)
+    cos = cos * length ** (-0.5)
+    sin = sin * length ** (-0.5)
+    per_q = channels // 4
+    c0, c1, c2, c3 = (cos[:, q * per_q : (q + 1) * per_q] for q in range(4))
+    s0, s1, s2, s3 = (sin[:, q * per_q : (q + 1) * per_q] for q in range(4))
+    zero = jnp.zeros_like(c0)
+    even = jnp.block([[c0, -s0, zero, zero], [zero, zero, c2, -s2]])
+    odd = jnp.block([[c1, -s1, c3, -s3], [-s1, -c1, s3, c3]])
+    return even, odd
 
 
 def shards(voltages, taps):
@@ -50,7 +56,7 @@
     frames = frames.astype(jnp.bfloat16)
     previous = shifted(frames[spectra_dev - (lags - 1) :], "tm", 1)
     taps_float = taps.astype(jnp.float32)
-    tables = [jnp.asarray(t) for t in radix4_tables(length, channels)]
+    tables = radix4_tables(length, channels)
     quarter = length // 4
 
     def channelize(extended, count):

time: 90.4 us -> 90.3 us (level)
  local copies, waits for them, and re-layouts: 6.8 us -> 5.73 us
    unnamed x6 -> x10, local copies, waits for them, and re-layouts: 1.65 us -> 0.65 us
where the time goes in v11:
time: 90.3 us; the launch traced here: 89.9 us
  blocking collectives  67.1 us (74%)
  other arithmetic  6.66 us (7%)
  local copies, waits for them, and re-layouts  5.73 us (6%)
  starting transfers between devices  4.18 us (5%)
  Pallas kernels  3.5 us (4%)
  matrix products  2.45 us (3%)
    all_to_all x1, blocking collectives, shards(): got = lax.all_to_all(packed, ('wide', 'tm'), 0, 0, tiled=True)  46.1 us
    all_to_all x1, blocking collectives, shards(): back = lax.all_to_all(grams, 'tm', 0, 0, tiled=True)  21.1 us
    ppermute x1, starting transfers between devices, shifted(): return lax.ppermute(array, axis, pairs)  4.18 us
    mul x2, other arithmetic, channelize(): filtered = filtered * FIR_SCALE  4.04 us
    pallas_call x1, Pallas kernels, channel_grams(): pl.pallas_call(lambda x_ref, o_ref: gram_kernel(scale, x_ref, o_ref), out...  3.5 us
    dot_general x4, matrix products, channelize(): jnp.einsum('sin,nm->sim', lhs, table, precision=lax.Precision.HIGH, prefe...  2.45 us
    transpose x1, local copies, waits for them, and re-layouts, shards(): spectra = jnp.concatenate([head, later], axis=0).transpose(4, 2, 1, 3, 0)  2.21 us
  transfers between devices with their start and end apart: 1, of which 0 were waited for; matrix products, arithmetic and copies ran while one was open for 7% of the time, Pallas kernels for 0%

profile of v11, /device:TPU:1, one launch (start us, length us, event | category | flops | bytes accessed | tf_op | source)
XLA Modules:
  0.0 89.9 jit_solution(5127623989505110832)
XLA Ops:
  0.0 1.7 %convert_element_type.31 = bf16[8,65536]{1,0:T(8,128)(2,1)S(1)} convert(s32[8,65536]{1,0:T(8,128)} %param.6) | non-fusion elementwise | flops 524288 | bytes 3145728 | tf_op jit(solution)/shard_map/convert_element_type | solution.py:56
  1.7 0.0 copy-start
  1.7 4.2 %collective-permute-start = (bf16[15,8,1024]{2,1,0:T(8,128)(2,1)S(1)}, bf16[15,8,1024]{2,1,0:T(8,128)(2,1)S(1)}, u32[]{:S(2)}, u32[]{:S(2)}) collective-permute-start(bf16[15,8,1024]{2,1,0:T(8,128)(2,1)S(1)} %slice.313), channel_id=1, source_target_pairs={{0,1},{1,2},{2,3},{3,4},{4,5},{5,6},{6,7},{8,9},{9,10},{10,11},{11... | collective-permute-start | bytes 737288 | tf_op jit(solution)/shard_map/ppermute | solution.py:15
  5.9 0.2 convert_element_type.37
  6.2 0.0 copy-done
  6.2 3.5 %fusion.1 = f32[49,8,1024]{2,1,0:T(8,128)S(1)} fusion(f32[64,8,1024]{2,1,0:T(8,128)S(1)} %convert_element_type.37, f32[1024]{0:T(1024)S(1)} %bitcast.52, f32[1024]{0:T(1024)S(1)} %bitcast.54, f32[1024]{0:T(1024)S(1)} %bitcast.56, f32[1024]{0:T(1024)S(1)} %bitcast.58, f32[1024]{0:T(1024)S(1)} %bitcast.60, f32[1024]{0:T(1024)S(1)} %bitcast.62, ...), kind=kLoop, calls=%fused_computation.2 | loop fusion | flops 12845056 | bytes 27361280 | tf_op jit(solution)/shard_map/mul | solution.py:67
  9.7 0.0 copy-start.1
  9.8 0.0 copy-start.2
  9.8 0.0 copy-start.3
  9.8 0.0 copy-start.4
  9.8 0.1 add_add_fusion
  9.9 0.6 copy-done.1
  10.5 0.0 copy-done.2
  10.5 0.0 copy-done.3
  10.5 0.0 copy-done.4
  10.6 0.2 add_multiply_fusion
  10.7 0.1 slice_negate_fusion.2
  10.8 0.8 convolution_convert_fusion
  11.8 0.8 convolution_convert_fusion.1
  12.7 0.0 collective-permute-done
  12.7 0.1 maximum_convert_fusion
  12.8 0.5 fusion.23
  13.4 0.4 convolution_convert_fusion.2
  13.8 0.4 convolution_convert_fusion.3
  14.2 0.1 maximum_bitcast_fusion.2
  14.4 2.2 %copy.18 = bf16[128,4,8,2,64]{4,3,2,1,0:T(2,128)(2,1)S(1)} copy(bf16[128,4,8,2,64]{0,2,3,1,4:T(8,128)(2,1)S(1)} %maximum_bitcast_fusion.2) | data formatting | bytes 2097152 | tf_op jit(solution)/shard_map/transpose | solution.py:89
  16.6 1.0 %reshape_reshape.3 = bf16[256,16,128]{2,1,0:T(8,128)(2,1)S(1)} reshape(bf16[128,4,8,2,64]{4,3,2,1,0:T(2,128)(2,1)S(1)} %copy.18) | data formatting | bytes 2097152 | tf_op jit(solution)/shard_map/reshape;reshape | solution.py:91
  17.6 46.1 %all_to_all.10 = bf16[256,16,128]{2,1,0:T(8,128)(2,1)} all-to-all(bf16[256,16,128]{2,1,0:T(8,128)(2,1)S(1)} %reshape_reshape.3), channel_id=1, replica_groups=mesh['wide'=32,'tm'=8] {'wide','tm'}, dimensions={0} | all-to-all | bytes 2097152 | tf_op jit(solution)/shard_map/all_to_all | solution.py:92
  63.7 3.5 %shard_map.64 = f32[8,2,2,32,256]{4,3,2,1,0:T(8,128)} custom-call(bf16[32,8,16,128]{3,2,1,0:T(8,128)(2,1)} %bitcast.41), custom_call_target="tpu_custom_call" | custom-call | flops 536870912 | bytes 2097152 | tf_op jit(solution)/shard_map/pallas_call | solution.py:132
  67.2 21.1 %all_to_all.11 = f32[8,2,2,32,256]{4,3,2,1,0:T(8,128)S(1)} all-to-all(f32[8,2,2,32,256]{4,3,2,1,0:T(8,128)} %shard_map.64), channel_id=1, replica_groups=mesh['wide'=32,'tm'=8] {'tm'}, dimensions={0} | all-to-all | bytes 2097152 | tf_op jit(solution)/shard_map/all_to_all | solution.py:96
  88.2 0.1 copy.19
  88.3 1.6 %copy.20 = f32[32,2,16,256]{3,2,1,0:T(8,128)} copy(f32[32,2,16,256]{3,0,2,1:T(8,128)S(1)} %bitcast.43) | data formatting | bytes 2097152 | tf_op jit(solution)/shard_map/reshape | solution.py:98
  (10 shorter events, 0.2 us)
Async XLA Ops:
  1.7 4.4 %copy-start = (s32[16,1024]{1,0:T(8,128)S(1)}, s32[16,1024]{1,0:T(8,128)}, u32[]{:S(2)}) copy-start(s32[16,1024]{1,0:T(8,128)} %param.7) | copy-start | bytes 196612
  1.7 10.9 %collective-permute-start = (bf16[15,8,1024]{2,1,0:T(8,128)(2,1)S(1)}, bf16[15,8,1024]{2,1,0:T(8,128)(2,1)S(1)}, u32[]{:S(2)}, u32[]{:S(2)}) collective-permute-start(bf16[15,8,1024]{2,1,0:T(8,128)(2,1)S(1)} %slice.313), channel_id=1, source_target_pairs={{0,1},{1,2},{2,3},{3,4},{4,5},{5,6},{6,7},{8,9},{9,10},{10,11},{11... | collective-permute-start | bytes 737288 | tf_op jit(solution)/shard_map/ppermute | solution.py:15
  9.7 0.8 copy-start.1
  9.8 0.8 copy-start.2
  9.8 0.8 copy-start.3
  9.8 0.8 copy-start.4

commit v12 on v11

--- a/solution.py
+++ b/solution.py
@@ -35,10 +35,10 @@
     per_q = channels // 4
     c0, c1, c2, c3 = (cos[:, q * per_q : (q + 1) * per_q] for q in range(4))
     s0, s1, s2, s3 = (sin[:, q * per_q : (q + 1) * per_q] for q in range(4))
-    zero = jnp.zeros_like(c0)
-    even = jnp.block([[c0, -s0, zero, zero], [zero, zero, c2, -s2]])
+    real_q0 = jnp.concatenate([c0, -s0], axis=1)
+    real_q2 = jnp.concatenate([c2, -s2], axis=1)
     odd = jnp.block([[c1, -s1, c3, -s3], [-s1, -c1, s3, c3]])
-    return even, odd
+    return real_q0, real_q2, odd
 
 
 def shards(voltages, taps):
@@ -66,22 +66,18 @@
             filtered = filtered + taps_float[lag] * extended[lags - 1 - lag : lags - 1 - lag + count]
         filtered = filtered * FIR_SCALE
         x0, x1, x2, x3 = (filtered[..., m * quarter : (m + 1) * quarter] for m in range(4))
-        inputs = [
-            jnp.concatenate([x0 + x1 + x2 + x3, x0 - x1 + x2 - x3], axis=-1),
-            jnp.concatenate([x0 - x2, x1 - x3], axis=-1),
-        ]
-        even, odd = (
-            jnp.einsum(
+        def dft(lhs, table):
+            return jnp.einsum(
                 "sin,nm->sim",
                 lhs,
                 table,
                 precision=lax.Precision.HIGH,
                 preferred_element_type=jnp.float32,
-            )
-            .astype(jnp.bfloat16)
-            .reshape(count, local_inputs, 2, 2, channels // 4)
-            for lhs, table in zip(inputs, tables)
-        )
+            ).astype(jnp.bfloat16)
+
+        even = jnp.concatenate([dft(x0 + x1 + x2 + x3, tables[0]), dft(x0 - x1 + x2 - x3, tables[1])], axis=-1)
+        odd = dft(jnp.concatenate([x0 - x2, x1 - x3], axis=-1), tables[2])
+        even, odd = (part.reshape(count, local_inputs, 2, 2, channels // 4) for part in (even, odd))
         return jnp.stack([even[:, :, 0], odd[:, :, 0], even[:, :, 1], odd[:, :, 1]], axis=2)
 
     later = channelize(frames, spectra_dev - (lags - 1))

time: 90.3 us -> 90.4 us (level)
    dot_general x4 -> x6, matrix products: 2.45 us -> 2.44 us  [dft(): jnp.einsum('sin,nm->sim', lhs, table, precision=lax.Precision.HIGH, prefe...]
  transfers between devices with their start and end apart: 1 -> 1, of which waited for: 0 -> 0; matrix products, arithmetic and copies ran while one was open for 7% -> 6% of each run, Pallas kernels for 0% -> 0%
where the time goes in v12:
time: 90.4 us; the launch traced here: 90 us
  blocking collectives  67.2 us (74%)
  other arithmetic  6.66 us (7%)
  local copies, waits for them, and re-layouts  5.75 us (6%)
  starting transfers between devices  4.18 us (5%)
  Pallas kernels  3.5 us (4%)
  matrix products  2.44 us (3%)
    all_to_all x1, blocking collectives, shards(): got = lax.all_to_all(packed, ('wide', 'tm'), 0, 0, tiled=True)  46.1 us
    all_to_all x1, blocking collectives, shards(): back = lax.all_to_all(grams, 'tm', 0, 0, tiled=True)  21.1 us
    ppermute x1, starting transfers between devices, shifted(): return lax.ppermute(array, axis, pairs)  4.18 us
    mul x2, other arithmetic, channelize(): filtered = filtered * FIR_SCALE  4.04 us
    pallas_call x1, Pallas kernels, channel_grams(): pl.pallas_call(lambda x_ref, o_ref: gram_kernel(scale, x_ref, o_ref), out...  3.5 us
    dot_general x6, matrix products, dft(): jnp.einsum('sin,nm->sim', lhs, table, precision=lax.Precision.HIGH, prefe...  2.44 us
    transpose x1, local copies, waits for them, and re-layouts, shards(): spectra = jnp.concatenate([head, later], axis=0).transpose(4, 2, 1, 3, 0)  2.21 us
  transfers between devices with their start and end apart: 1, of which 0 were waited for; matrix products, arithmetic and copies ran while one was open for 6% of the time, Pallas kernels for 0%

profile of v12, /device:TPU:1, one launch (start us, length us, event | category | flops | bytes accessed | tf_op | source)
XLA Modules:
  0.0 90.0 jit_solution(14194487492745966000)
XLA Ops:
  0.0 1.7 %convert_element_type.37 = bf16[8,65536]{1,0:T(8,128)(2,1)S(1)} convert(s32[8,65536]{1,0:T(8,128)} %param.6) | non-fusion elementwise | flops 524288 | bytes 3145728 | tf_op jit(solution)/shard_map/convert_element_type | solution.py:56
  1.7 0.0 copy-start
  1.7 4.2 %collective-permute-start = (bf16[15,8,1024]{2,1,0:T(8,128)(2,1)S(1)}, bf16[15,8,1024]{2,1,0:T(8,128)(2,1)S(1)}, u32[]{:S(2)}, u32[]{:S(2)}) collective-permute-start(bf16[15,8,1024]{2,1,0:T(8,128)(2,1)S(1)} %slice.313), channel_id=1, source_target_pairs={{0,1},{1,2},{2,3},{3,4},{4,5},{5,6},{6,7},{8,9},{9,10},{10,11},{11... | collective-permute-start | bytes 737288 | tf_op jit(solution)/shard_map/ppermute | solution.py:15
  5.9 0.2 convert_element_type.44
  6.2 0.0 copy-done
  6.2 3.5 %fusion.1 = f32[49,8,1024]{2,1,0:T(8,128)S(1)} fusion(f32[64,8,1024]{2,1,0:T(8,128)S(1)} %convert_element_type.44, f32[1024]{0:T(1024)S(1)} %bitcast.56, f32[1024]{0:T(1024)S(1)} %bitcast.58, f32[1024]{0:T(1024)S(1)} %bitcast.60, f32[1024]{0:T(1024)S(1)} %bitcast.62, f32[1024]{0:T(1024)S(1)} %bitcast.64, f32[1024]{0:T(1024)S(1)} %bitcast.66, ...), kind=kLoop, calls=%fused_computation.2 | loop fusion | flops 12845056 | bytes 27361280 | tf_op jit(solution)/shard_map/mul | solution.py:67
  9.7 0.0 copy-start.1
  9.8 0.0 copy-start.2
  9.8 0.0 copy-start.3
  9.8 0.0 copy-start.4
  9.8 0.1 slice_subtract_fusion.1
  9.9 0.6 copy-done.1
  10.5 0.0 copy-done.2
  10.5 0.0 copy-done.3
  10.5 0.0 copy-done.4
  10.6 0.2 add_multiply_fusion
  10.7 0.1 slice_negate_fusion.2
  10.8 0.4 convolution_convert_fusion.2
  11.2 0.4 convolution_convert_fusion.1
  11.7 0.8 convolution_convert_fusion
  12.6 0.0 collective-permute-done
  12.6 0.1 maximum_convert_fusion
  12.7 0.5 fusion.20
  13.3 0.2 convolution_convert_fusion.5
  13.5 0.2 convolution_convert_fusion.4
  13.8 0.4 convolution_convert_fusion.3
  14.2 0.1 maximum_bitcast_fusion.1
  14.4 2.2 %copy.18 = bf16[128,4,8,2,64]{4,3,2,1,0:T(2,128)(2,1)S(1)} copy(bf16[128,4,8,2,64]{0,2,3,1,4:T(8,128)(2,1)S(1)} %maximum_bitcast_fusion.1) | data formatting | bytes 2097152 | tf_op jit(solution)/shard_map/transpose | solution.py:85
  16.6 1.0 %reshape_reshape.3 = bf16[256,16,128]{2,1,0:T(8,128)(2,1)S(1)} reshape(bf16[128,4,8,2,64]{4,3,2,1,0:T(2,128)(2,1)S(1)} %copy.18) | data formatting | bytes 2097152 | tf_op jit(solution)/shard_map/reshape;reshape | solution.py:87
  17.6 46.1 %all_to_all.10 = bf16[256,16,128]{2,1,0:T(8,128)(2,1)} all-to-all(bf16[256,16,128]{2,1,0:T(8,128)(2,1)S(1)} %reshape_reshape.3), channel_id=1, replica_groups=mesh['wide'=32,'tm'=8] {'wide','tm'}, dimensions={0} | all-to-all | bytes 2097152 | tf_op jit(solution)/shard_map/all_to_all | solution.py:88
  63.7 3.5 %shard_map.64 = f32[8,2,2,32,256]{4,3,2,1,0:T(8,128)} custom-call(bf16[32,8,16,128]{3,2,1,0:T(8,128)(2,1)} %bitcast.45), custom_call_target="tpu_custom_call" | custom-call | flops 536870912 | bytes 2097152 | tf_op jit(solution)/shard_map/pallas_call | solution.py:128
  67.2 21.1 %all_to_all.11 = f32[8,2,2,32,256]{4,3,2,1,0:T(8,128)S(1)} all-to-all(f32[8,2,2,32,256]{4,3,2,1,0:T(8,128)} %shard_map.64), channel_id=1, replica_groups=mesh['wide'=32,'tm'=8] {'tm'}, dimensions={0} | all-to-all | bytes 2097152 | tf_op jit(solution)/shard_map/all_to_all | solution.py:92
  88.3 0.1 copy.19
  88.4 1.6 %copy.20 = f32[32,2,16,256]{3,2,1,0:T(8,128)} copy(f32[32,2,16,256]{3,0,2,1:T(8,128)S(1)} %bitcast.47) | data formatting | bytes 2097152 | tf_op jit(solution)/shard_map/reshape | solution.py:94
  (11 shorter events, 0.3 us)
Async XLA Ops:
  1.7 4.4 %copy-start = (s32[16,1024]{1,0:T(8,128)S(1)}, s32[16,1024]{1,0:T(8,128)}, u32[]{:S(2)}) copy-start(s32[16,1024]{1,0:T(8,128)} %param.7) | copy-start | bytes 196612
  1.7 10.9 %collective-permute-start = (bf16[15,8,1024]{2,1,0:T(8,128)(2,1)S(1)}, bf16[15,8,1024]{2,1,0:T(8,128)(2,1)S(1)}, u32[]{:S(2)}, u32[]{:S(2)}) collective-permute-start(bf16[15,8,1024]{2,1,0:T(8,128)(2,1)S(1)} %slice.313), channel_id=1, source_target_pairs={{0,1},{1,2},{2,3},{3,4},{4,5},{5,6},{6,7},{8,9},{9,10},{10,11},{11... | collective-permute-start | bytes 737288 | tf_op jit(solution)/shard_map/ppermute | solution.py:15
  9.7 0.8 copy-start.1
  9.8 0.8 copy-start.2
  9.8 0.8 copy-start.3
  9.8 0.8 copy-start.4

commit v13 on v11

--- a/solution.py
+++ b/solution.py
@@ -54,17 +54,18 @@
 
     frames = voltages.reshape(local_inputs, spectra_dev, length).transpose(1, 0, 2)
     frames = frames.astype(jnp.bfloat16)
-    previous = shifted(frames[spectra_dev - (lags - 1) :], "tm", 1)
     taps_float = taps.astype(jnp.float32)
     tables = radix4_tables(length, channels)
     quarter = length // 4
 
-    def channelize(extended, count):
+    def polyphase(extended, count):
         extended = extended.astype(jnp.float32)
         filtered = taps_float[0] * extended[lags - 1 : lags - 1 + count]
         for lag in range(1, lags):
             filtered = filtered + taps_float[lag] * extended[lags - 1 - lag : lags - 1 - lag + count]
-        filtered = filtered * FIR_SCALE
+        return filtered * FIR_SCALE
+
+    def channelize(filtered, count):
         x0, x1, x2, x3 = (filtered[..., m * quarter : (m + 1) * quarter] for m in range(4))
         inputs = [
             jnp.concatenate([x0 + x1 + x2 + x3, x0 - x1 + x2 - x3], axis=-1),
@@ -84,8 +85,13 @@
         )
         return jnp.stack([even[:, :, 0], odd[:, :, 0], even[:, :, 1], odd[:, :, 1]], axis=2)
 
-    later = channelize(frames, spectra_dev - (lags - 1))
-    head = channelize(jnp.concatenate([previous, frames[: 2 * (lags - 1)]], axis=0), lags - 1)
+    count = spectra_dev - (lags - 1)
+    filtered = polyphase(frames, count)
+    tail, filtered = lax.optimization_barrier((frames[spectra_dev - (lags - 1) :], filtered))
+    previous = shifted(tail, "tm", 1)
+    later = channelize(filtered, count)
+    head_frames = jnp.concatenate([previous, frames[: 2 * (lags - 1)]], axis=0)
+    head = channelize(polyphase(head_frames, lags - 1), lags - 1)
     spectra = jnp.concatenate([head, later], axis=0).transpose(4, 2, 1, 3, 0)
     spectra = spectra.reshape(channels, local_inputs, 2 * spectra_dev)
     packed = spectra.reshape(groups, per_group * local_inputs, 2 * spectra_dev)

time: 90.3 us -> 94.7 us (1.049)
  waiting for transfers between devices: 0.01 us -> 2.33 us
  blocking collectives: 67.1 us -> 69.3 us
    ppermute x1, waiting for transfers between devices: 0.01 us -> 2.33 us  [shifted(): return lax.ppermute(array, axis, pairs)]
    all_to_all x1, blocking collectives: 46.1 us -> 48.2 us  [shards(): got = lax.all_to_all(packed, ('wide', 'tm'), 0, 0, tiled=True)]
  transfers between devices with their start and end apart: 1 -> 1, of which waited for: 0 -> 1; matrix products, arithmetic and copies ran while one was open for 7% -> 2% of each run, Pallas kernels for 0% -> 0%
where the time goes in v13:
time: 94.7 us; the launch traced here: 94.3 us
  blocking collectives  69.3 us (73%)
  other arithmetic  6.62 us (7%)
  local copies, waits for them, and re-layouts  5.69 us (6%)
  starting transfers between devices  4.18 us (4%)
  Pallas kernels  3.5 us (4%)
  matrix products  2.45 us (3%)
  waiting for transfers between devices  2.33 us (2%)
    all_to_all x1, blocking collectives, shards(): got = lax.all_to_all(packed, ('wide', 'tm'), 0, 0, tiled=True)  48.2 us
    all_to_all x1, blocking collectives, shards(): back = lax.all_to_all(grams, 'tm', 0, 0, tiled=True)  21.1 us
    ppermute x1, starting transfers between devices, shifted(): return lax.ppermute(array, axis, pairs)  4.18 us
    mul x2, other arithmetic, polyphase(): return filtered * FIR_SCALE  4 us
    pallas_call x1, Pallas kernels, channel_grams(): pl.pallas_call(lambda x_ref, o_ref: gram_kernel(scale, x_ref, o_ref), out...  3.5 us
    dot_general x4, matrix products, channelize(): jnp.einsum('sin,nm->sim', lhs, table, precision=lax.Precision.HIGH, prefe...  2.45 us
    ppermute x1, waiting for transfers between devices, shifted(): return lax.ppermute(array, axis, pairs)  2.33 us
    transpose x1, local copies, waits for them, and re-layouts, shards(): spectra = jnp.concatenate([head, later], axis=0).transpose(4, 2, 1, 3, 0)  2.21 us
  transfers between devices with their start and end apart: 1, of which 1 were waited for; matrix products, arithmetic and copies ran while one was open for 2% of the time, Pallas kernels for 0%

profile of v13, /device:TPU:1, one launch (start us, length us, event | category | flops | bytes accessed | tf_op | source)
XLA Modules:
  0.0 94.3 jit_solution(16153198283700441012)
XLA Ops:
  0.0 1.7 %convert_element_type.31 = bf16[8,65536]{1,0:T(8,128)(2,1)S(1)} convert(s32[8,65536]{1,0:T(8,128)} %param.6) | non-fusion elementwise | flops 524288 | bytes 3145728 | tf_op jit(solution)/shard_map/convert_element_type | solution.py:56
  1.7 0.0 copy-start
  1.7 0.2 convert_element_type.34
  2.0 0.6 copy-done
  2.6 3.5 %fusion.1 = f32[49,8,1024]{2,1,0:T(8,128)S(1)} fusion(f32[64,8,1024]{2,1,0:T(8,128)S(1)} %convert_element_type.34, f32[1024]{0:T(1024)S(1)} %bitcast.52, f32[1024]{0:T(1024)S(1)} %bitcast.54, f32[1024]{0:T(1024)S(1)} %bitcast.56, f32[1024]{0:T(1024)S(1)} %bitcast.58, f32[1024]{0:T(1024)S(1)} %bitcast.60, f32[1024]{0:T(1024)S(1)} %bitcast.62, ...), kind=kLoop, calls=%fused_computation.2 | loop fusion | flops 12845056 | bytes 27361280 | tf_op jit(solution)/shard_map/mul | solution.py:66
  6.1 0.0 copy-start.1
  6.1 0.0 copy-start.2
  6.1 0.0 copy-start.3
  6.1 0.0 copy-start.4
  6.1 4.2 %collective-permute-start = (bf16[15,8,1024]{2,1,0:T(8,128)(2,1)S(1)}, bf16[15,8,1024]{2,1,0:T(8,128)(2,1)S(1)}, u32[]{:S(2)}, u32[]{:S(2)}) collective-permute-start(bf16[15,8,1024]{2,1,0:T(8,128)(2,1)S(1)} %slice.313), channel_id=1, source_target_pairs={{0,1},{1,2},{2,3},{3,4},{4,5},{5,6},{6,7},{8,9},{9,10},{10,11},{11... | collective-permute-start | bytes 737288 | tf_op jit(solution)/shard_map/ppermute | solution.py:15
  10.3 0.1 add_add_fusion
  10.5 0.0 copy-done.1
  10.5 0.0 copy-done.2
  10.5 0.0 copy-done.3
  10.5 0.0 copy-done.4
  10.5 0.2 add_multiply_fusion
  10.7 0.1 slice_negate_fusion.2
  10.8 0.8 convolution_convert_fusion
  11.7 0.8 convolution_convert_fusion.1
  12.6 2.3 %collective-permute-done = bf16[15,8,1024]{2,1,0:T(8,128)(2,1)S(1)} collective-permute-done((bf16[15,8,1024]{2,1,0:T(8,128)(2,1)S(1)}, bf16[15,8,1024]{2,1,0:T(8,128)(2,1)S(1)}, u32[]{:S(2)}, u32[]{:S(2)}) %collective-permute-start) | collective-permute-done | bytes 245792 | tf_op jit(solution)/shard_map/ppermute | solution.py:15
  14.9 0.1 maximum_convert_fusion
  15.0 0.5 fusion.23
  15.6 0.4 convolution_convert_fusion.2
  16.0 0.4 convolution_convert_fusion.3
  16.5 0.1 maximum_bitcast_fusion.2
  16.6 2.2 %copy.18 = bf16[128,4,8,2,64]{4,3,2,1,0:T(2,128)(2,1)S(1)} copy(bf16[128,4,8,2,64]{0,2,3,1,4:T(8,128)(2,1)S(1)} %maximum_bitcast_fusion.2) | data formatting | bytes 2097152 | tf_op jit(solution)/shard_map/transpose | solution.py:95
  18.8 1.0 %reshape_reshape.3 = bf16[256,16,128]{2,1,0:T(8,128)(2,1)S(1)} reshape(bf16[128,4,8,2,64]{4,3,2,1,0:T(2,128)(2,1)S(1)} %copy.18) | data formatting | bytes 2097152 | tf_op jit(solution)/shard_map/reshape;reshape | solution.py:97
  19.8 48.2 %all_to_all.10 = bf16[256,16,128]{2,1,0:T(8,128)(2,1)} all-to-all(bf16[256,16,128]{2,1,0:T(8,128)(2,1)S(1)} %reshape_reshape.3), channel_id=1, replica_groups=mesh['wide'=32,'tm'=8] {'wide','tm'}, dimensions={0} | all-to-all | bytes 2097152 | tf_op jit(solution)/shard_map/all_to_all | solution.py:98
  68.1 3.5 %shard_map.64 = f32[8,2,2,32,256]{4,3,2,1,0:T(8,128)} custom-call(bf16[32,8,16,128]{3,2,1,0:T(8,128)(2,1)} %bitcast.41), custom_call_target="tpu_custom_call" | custom-call | flops 536870912 | bytes 2097152 | tf_op jit(solution)/shard_map/pallas_call | solution.py:138
  71.6 21.1 %all_to_all.11 = f32[8,2,2,32,256]{4,3,2,1,0:T(8,128)S(1)} all-to-all(f32[8,2,2,32,256]{4,3,2,1,0:T(8,128)} %shard_map.64), channel_id=1, replica_groups=mesh['wide'=32,'tm'=8] {'tm'}, dimensions={0} | all-to-all | bytes 2097152 | tf_op jit(solution)/shard_map/all_to_all | solution.py:102
  92.6 0.1 copy.19
  92.7 1.6 %copy.20 = f32[32,2,16,256]{3,2,1,0:T(8,128)} copy(f32[32,2,16,256]{3,0,2,1:T(8,128)S(1)} %bitcast.43) | data formatting | bytes 2097152 | tf_op jit(solution)/shard_map/reshape | solution.py:104
  (10 shorter events, 0.2 us)
Async XLA Ops:
  1.7 0.8 copy-start
  6.1 4.4 %copy-start.1 = (f32[16,512]{1,0:T(8,128)S(1)}, f32[16,512]{1,0:T(8,128)}, u32[]{:S(2)}) copy-start(f32[16,512]{1,0:T(8,128)} %constant.18.clone) | copy-start | bytes 98308
  6.1 4.4 %copy-start.2 = (f32[16,512]{1,0:T(8,128)S(1)}, f32[16,512]{1,0:T(8,128)}, u32[]{:S(2)}) copy-start(f32[16,512]{1,0:T(8,128)} %constant.17.clone) | copy-start | bytes 98308
  6.1 4.4 %copy-start.3 = (f32[16,512]{1,0:T(8,128)S(1)}, f32[16,512]{1,0:T(8,128)}, u32[]{:S(2)}) copy-start(f32[16,512]{1,0:T(8,128)} %constant.16.clone) | copy-start | bytes 98308
  6.1 4.4 %copy-start.4 = (f32[16,512]{1,0:T(8,128)S(1)}, f32[16,512]{1,0:T(8,128)}, u32[]{:S(2)}) copy-start(f32[16,512]{1,0:T(8,128)} %constant.6.clone) | copy-start | bytes 98308
  6.1 8.8 %collective-permute-start = (bf16[15,8,1024]{2,1,0:T(8,128)(2,1)S(1)}, bf16[15,8,1024]{2,1,0:T(8,128)(2,1)S(1)}, u32[]{:S(2)}, u32[]{:S(2)}) collective-permute-start(bf16[15,8,1024]{2,1,0:T(8,128)(2,1)S(1)} %slice.313), channel_id=1, source_target_pairs={{0,1},{1,2},{2,3},{3,4},{4,5},{5,6},{6,7},{8,9},{9,10},{10,11},{11... | collective-permute-start | bytes 737288 | tf_op jit(solution)/shard_map/ppermute | solution.py:15

commit v14 on v11

--- a/solution.py
+++ b/solution.py
@@ -17,16 +17,17 @@
 
 def radix4_factors(length, channels, split):
     quarter = length // 4
-    k = (4 * np.arange(channels // 4)[None, :] + np.arange(4)[:, None]).reshape(1, channels)
-    hi = np.arange(quarter // split)[:, None] * split * k % length
-    lo = np.arange(split)[:, None] * k % length
-    angles = [2.0 * np.pi / length * hi, 2.0 * np.pi / length * lo]
-    return [f(angle).astype(np.float32) for angle in angles for f in (np.cos, np.sin)]
+    column = lax.broadcasted_iota(jnp.int32, (1, channels), 1)
+    k = 4 * (column % (channels // 4)) + column // (channels // 4)
+    hi = (lax.broadcasted_iota(jnp.int32, (quarter // split, 1), 0) * split * k) % length
+    lo = (lax.broadcasted_iota(jnp.int32, (split, 1), 0) * k) % length
+    angles = [(2.0 * np.pi / length) * step.astype(jnp.float32) for step in (hi, lo)]
+    return [f(angle) for angle in angles for f in (jnp.cos, jnp.sin)]
 
 
 def radix4_tables(length, channels):
     split = 16
-    ch, sh, cl, sl = (jnp.asarray(t) for t in radix4_factors(length, channels, split))
+    ch, sh, cl, sl = radix4_factors(length, channels, split)
     quarter = length // 4
     cos = (ch[:, None, :] * cl[None, :, :] - sh[:, None, :] * sl[None, :, :]).reshape(quarter, channels)
     sin = (sh[:, None, :] * cl[None, :, :] + ch[:, None, :] * sl[None, :, :]).reshape(quarter, channels)

time: 90.3 us -> 90.2 us (level)
  no operation moved by 1% of the time
where the time goes in v14:
time: 90.2 us; the launch traced here: 89.9 us
  blocking collectives  67.4 us (75%)
  other arithmetic  7.06 us (8%)
  local copies, waits for them, and re-layouts  5.09 us (6%)
  starting transfers between devices  4.18 us (5%)
  Pallas kernels  3.5 us (4%)
  matrix products  2.44 us (3%)
    all_to_all x1, blocking collectives, shards(): got = lax.all_to_all(packed, ('wide', 'tm'), 0, 0, tiled=True)  46.4 us
    all_to_all x1, blocking collectives, shards(): back = lax.all_to_all(grams, 'tm', 0, 0, tiled=True)  21.1 us
    ppermute x1, starting transfers between devices, shifted(): return lax.ppermute(array, axis, pairs)  4.18 us
    mul x2, other arithmetic, channelize(): filtered = filtered * FIR_SCALE  4.11 us
    pallas_call x1, Pallas kernels, channel_grams(): pl.pallas_call(lambda x_ref, o_ref: gram_kernel(scale, x_ref, o_ref), out...  3.5 us
    dot_general x4, matrix products, channelize(): jnp.einsum('sin,nm->sim', lhs, table, precision=lax.Precision.HIGH, prefe...  2.44 us
    transpose x1, local copies, waits for them, and re-layouts, shards(): spectra = jnp.concatenate([head, later], axis=0).transpose(4, 2, 1, 3, 0)  2.22 us
  transfers between devices with their start and end apart: 1, of which 0 were waited for; matrix products, arithmetic and copies ran while one was open for 7% of the time, Pallas kernels for 0%

profile of v14, /device:TPU:1, one launch (start us, length us, event | category | flops | bytes accessed | tf_op | source)
XLA Modules:
  0.0 89.9 jit_solution(2716517654224577667)
XLA Ops:
  0.0 1.7 %convert_element_type.95 = bf16[8,65536]{1,0:T(8,128)(2,1)S(1)} convert(s32[8,65536]{1,0:T(8,128)} %param.2) | non-fusion elementwise | flops 524288 | bytes 3145728 | tf_op jit(solution)/shard_map/convert_element_type | solution.py:57
  1.7 0.0 copy-start
  1.7 4.2 %collective-permute-start = (bf16[15,8,1024]{2,1,0:T(8,128)(2,1)S(1)}, bf16[15,8,1024]{2,1,0:T(8,128)(2,1)S(1)}, u32[]{:S(2)}, u32[]{:S(2)}) collective-permute-start(bf16[15,8,1024]{2,1,0:T(8,128)(2,1)S(1)} %slice.321), channel_id=1, source_target_pairs={{0,1},{1,2},{2,3},{3,4},{4,5},{5,6},{6,7},{8,9},{9,10},{10,11},{11... | collective-permute-start | bytes 737288 | tf_op jit(solution)/shard_map/ppermute | solution.py:15
  5.9 0.2 convert_element_type.103
  6.2 0.0 copy-done
  6.3 3.6 %fusion.1 = f32[49,8,1024]{2,1,0:T(8,128)S(1)} fusion(f32[64,8,1024]{2,1,0:T(8,128)S(1)} %convert_element_type.103, f32[1024]{0:T(1024)S(1)} %bitcast.52, f32[1024]{0:T(1024)S(1)} %bitcast.54, f32[1024]{0:T(1024)S(1)} %bitcast.56, f32[1024]{0:T(1024)S(1)} %bitcast.58, f32[1024]{0:T(1024)S(1)} %bitcast.60, f32[1024]{0:T(1024)S(1)} %bitcast.62, ...), kind=kLoop, calls=%fused_computation.2 | loop fusion | flops 12845056 | bytes 27361280 | tf_op jit(solution)/shard_map/mul | solution.py:68
  9.8 0.2 add_add_fusion
  10.0 0.3 fusion.56
  10.3 0.2 add_multiply_fusion
  10.5 0.1 slice_negate_fusion.2
  10.6 0.8 convolution_convert_fusion
  11.5 0.8 convolution_convert_fusion.1
  12.4 0.0 collective-permute-done
  12.4 0.1 maximum_convert_fusion
  12.5 0.5 fusion.23
  13.1 0.4 convolution_convert_fusion.2
  13.5 0.4 convolution_convert_fusion.3
  13.9 0.1 maximum_bitcast_fusion.2
  14.1 2.2 %copy.14 = bf16[128,4,8,2,64]{4,3,2,1,0:T(2,128)(2,1)S(1)} copy(bf16[128,4,8,2,64]{0,2,3,1,4:T(8,128)(2,1)S(1)} %maximum_bitcast_fusion.2) | data formatting | bytes 2097152 | tf_op jit(solution)/shard_map/transpose | solution.py:90
  16.3 1.0 %reshape_reshape.3 = bf16[256,16,128]{2,1,0:T(8,128)(2,1)S(1)} reshape(bf16[128,4,8,2,64]{4,3,2,1,0:T(2,128)(2,1)S(1)} %copy.14) | data formatting | bytes 2097152 | tf_op jit(solution)/shard_map/reshape;reshape | solution.py:92
  17.3 46.4 %all_to_all.10 = bf16[256,16,128]{2,1,0:T(8,128)(2,1)} all-to-all(bf16[256,16,128]{2,1,0:T(8,128)(2,1)S(1)} %reshape_reshape.3), channel_id=1, replica_groups=mesh['wide'=32,'tm'=8] {'wide','tm'}, dimensions={0} | all-to-all | bytes 2097152 | tf_op jit(solution)/shard_map/all_to_all | solution.py:93
  63.7 3.5 %shard_map.28 = f32[8,2,2,32,256]{4,3,2,1,0:T(8,128)} custom-call(bf16[32,8,16,128]{3,2,1,0:T(8,128)(2,1)} %bitcast.41), custom_call_target="tpu_custom_call" | custom-call | flops 536870912 | bytes 2097152 | tf_op jit(solution)/shard_map/pallas_call | solution.py:133
  67.2 21.1 %all_to_all.11 = f32[8,2,2,32,256]{4,3,2,1,0:T(8,128)S(1)} all-to-all(f32[8,2,2,32,256]{4,3,2,1,0:T(8,128)} %shard_map.28), channel_id=1, replica_groups=mesh['wide'=32,'tm'=8] {'tm'}, dimensions={0} | all-to-all | bytes 2097152 | tf_op jit(solution)/shard_map/all_to_all | solution.py:97
  88.2 0.1 copy.15
  88.3 1.6 %copy.16 = f32[32,2,16,256]{3,2,1,0:T(8,128)} copy(f32[32,2,16,256]{3,0,2,1:T(8,128)S(1)} %bitcast.43) | data formatting | bytes 2097152 | tf_op jit(solution)/shard_map/reshape | solution.py:99
  (12 shorter events, 0.2 us)
Async XLA Ops:
  1.7 4.5 %copy-start = (s32[16,1024]{1,0:T(8,128)S(1)}, s32[16,1024]{1,0:T(8,128)}, u32[]{:S(2)}) copy-start(s32[16,1024]{1,0:T(8,128)} %param.3) | copy-start | bytes 196612
  1.7 10.6 %collective-permute-start = (bf16[15,8,1024]{2,1,0:T(8,128)(2,1)S(1)}, bf16[15,8,1024]{2,1,0:T(8,128)(2,1)S(1)}, u32[]{:S(2)}, u32[]{:S(2)}) collective-permute-start(bf16[15,8,1024]{2,1,0:T(8,128)(2,1)S(1)} %slice.321), channel_id=1, source_target_pairs={{0,1},{1,2},{2,3},{3,4},{4,5},{5,6},{6,7},{8,9},{9,10},{10,11},{11... | collective-permute-start | bytes 737288 | tf_op jit(solution)/shard_map/ppermute | solution.py:15
